TPU v7x, 512 devices: a whole 4x8x8 slice. The times are simulated.
512 devices in a mesh: dp: 4 (over x), shard: 128 (over z, y, core).
Axes of the slice: x: 4, y: 8, z: 8, core: 2. Of those that a mesh axis runs over, the one named last changes fastest.
Arguments:
- grad_parts: float32 [4, 1024, 16384], P('dp', None, 'shard'), may hold values from -0.3 to 0.3
- owner: int32 [1024], replicated, may hold values from 0 to 127, as said below
- master: float32 [4, 128, 4, 128, 128], P('dp', 'shard'), may hold values from -6 to 6
- first_moment: float32 [4, 128, 4, 128, 128], P('dp', 'shard'), may hold values from -0.12 to 0.12
- second_moment: float32 [4, 128, 4, 128, 128], P('dp', 'shard'), may hold values from 0.0001 to 0.001
- left_stat: float32 [4, 128, 4, 128, 128], P('dp', 'shard'), may hold values from -0.0062992126 to 10
- right_stat: float32 [4, 128, 4, 128, 128], P('dp', 'shard'), may hold values from -0.0062992126 to 10
- left_basis: float32 [4, 128, 4, 128, 128], P('dp', 'shard'), may hold values from -0.079549513 to 1.0795495
- right_basis: float32 [4, 128, 4, 128, 128], P('dp', 'shard'), may hold values from -0.079549513 to 1.0795495
Outputs:
- new_params: bfloat16 [1024, 16384], P(None, 'shard')
- master_out: float32 [4, 128, 4, 128, 128], P('dp', 'shard')
- first_out: float32 [4, 128, 4, 128, 128], P('dp', 'shard')
- second_out: float32 [4, 128, 4, 128, 128], P('dp', 'shard')
- left_stat_out: float32 [4, 128, 4, 128, 128], P('dp', 'shard')
- right_stat_out: float32 [4, 128, 4, 128, 128], P('dp', 'shard')
- left_basis_out: float32 [4, 128, 4, 128, 128], P('dp', 'shard')
- right_basis_out: float32 [4, 128, 4, 128, 128], P('dp', 'shard')
Inputs may be any that keep to these rules, and one draw needn't show every extreme that they name: In each group of 256 consecutive tiles no owner index holds more than 4 tiles, and some owner holds exactly 4.
All inputs are finite; a program needn't handle non-finite values.
Results may differ from a plain program's by a relative error of at most 0.001.
Values may be sent and summed in bfloat16 or wider, within the bound.
No kernel may reach another device: no remote copies, remote signals or barrier semaphores. Data moves between devices by JAX's collectives and lax.ppermute only.
A program may use at most 64 MiB of HBM per device.

v0:
```python
import jax
import jax.numpy as jnp
from jax import lax
from jax.sharding import PartitionSpec as P

NS_STEPS = 10


beta_one = 0.9
beta_two = 0.95
stat_decay = 0.95
learn_rate = 0.05
weight_decay = 0.01
adam_eps = 1e-08
highest = lax.Precision.HIGHEST


def product(form, left, right):
    return jnp.einsum(form, left, right, precision=highest)


def slot_index(owners, shards):
    matches = (owners[..., None] == jnp.arange(shards, dtype=jnp.int32)).astype(jnp.int32)
    running = jnp.cumsum(matches, axis=1)
    return jnp.sum(matches * running, axis=-1) - 1


def orthogonal(pending):
    iterate = pending * lax.rsqrt(jnp.sum(pending * pending, axis=(1, 2), keepdims=True) + 1e-06)
    for step in range(NS_STEPS):
        gram = product("nik,njk->nij", iterate, iterate)
        iterate = 1.5 * iterate - 0.5 * product("nij,njk->nik", gram, iterate)
    return iterate


def soap_update(gradient, master, first, second, lstat, rstat, lbasis, rbasis):
    first_new = beta_one * first + (1.0 - beta_one) * gradient
    grad_rot = product("nik,nkl->nil", product("nji,njk->nik", lbasis, gradient), rbasis)
    first_rot = product("nik,nkl->nil", product("nji,njk->nik", lbasis, first_new), rbasis)
    second_new = beta_two * second + (1.0 - beta_two) * grad_rot * grad_rot
    normed = first_rot / (jnp.sqrt(second_new) + adam_eps)
    update = product("nik,nlk->nil", product("nij,njk->nik", lbasis, normed), rbasis)
    master_new = master - learn_rate * (update + weight_decay * master)
    lstat_new = stat_decay * lstat + (1.0 - stat_decay) * product(
        "nik,njk->nij", gradient, gradient
    )
    rstat_new = stat_decay * rstat + (1.0 - stat_decay) * product(
        "nki,nkj->nij", gradient, gradient
    )
    lbasis_new = orthogonal(product("nij,njk->nik", lstat_new, lbasis))
    rbasis_new = orthogonal(product("nij,njk->nik", rstat_new, rbasis))
    return (master_new, first_new, second_new, lstat_new, rstat_new, lbasis_new, rbasis_new)


def body(
    grad_parts,
    owner,
    master,
    first_moment,
    second_moment,
    left_stat,
    right_stat,
    left_basis,
    right_basis,
):
    shards = lax.axis_size("shard")
    groups = lax.axis_size("dp")
    my_group = lax.axis_index("dp")
    capacity = master.shape[2]
    block_size = master.shape[4]
    piece_len = grad_parts.shape[2]
    tile_count = owner.shape[0]
    per_group = tile_count // groups
    owners = owner.reshape(groups, per_group)
    place_index = slot_index(owners, shards) * shards + owners
    own_place = lax.dynamic_index_in_dim(place_index, my_group, 0, keepdims=False)
    summed = lax.psum_scatter(grad_parts, "dp", scatter_dimension=1, tiled=True)
    outgoing = jnp.zeros((capacity * shards, piece_len), jnp.float32)
    outgoing = outgoing.at[own_place].set(summed[0])
    outgoing = outgoing.reshape(capacity, shards, piece_len)
    incoming = lax.all_to_all(outgoing, "shard", split_axis=1, concat_axis=1, tiled=True)

    def as_tiles(array):
        return array.reshape(capacity, block_size, block_size)

    results = soap_update(
        incoming,
        as_tiles(master),
        as_tiles(first_moment),
        as_tiles(second_moment),
        as_tiles(left_stat),
        as_tiles(right_stat),
        as_tiles(left_basis),
        as_tiles(right_basis),
    )
    shaped = [item.reshape(1, 1, capacity, block_size, block_size) for item in results]
    weights = results[0].astype(jnp.bfloat16)
    returned = lax.all_to_all(weights, "shard", split_axis=1, concat_axis=1, tiled=True)
    returned = returned.reshape(capacity * shards, piece_len)
    own_rows = returned[own_place]
    new_params = lax.all_gather(own_rows, "dp", axis=0, tiled=True)
    return (new_params, shaped[0], shaped[1], shaped[2], shaped[3], shaped[4], shaped[5], shaped[6])


def solution(mesh):
    placed = (
        P("dp", None, "shard"),
        P(),
        P("dp", "shard", None, None, None),
        P("dp", "shard", None, None, None),
        P("dp", "shard", None, None, None),
        P("dp", "shard", None, None, None),
        P("dp", "shard", None, None, None),
        P("dp", "shard", None, None, None),
        P("dp", "shard", None, None, None),
    )
    return jax.shard_map(
        body,
        mesh=mesh,
        in_specs=placed,
        out_specs=(
            P(None, "shard"),
            P("dp", "shard", None, None, None),
            P("dp", "shard", None, None, None),
            P("dp", "shard", None, None, None),
            P("dp", "shard", None, None, None),
            P("dp", "shard", None, None, None),
            P("dp", "shard", None, None, None),
            P("dp", "shard", None, None, None),
        ),
        check_vma=False,
    )
```

profile of v0, /device:TPU:1, one launch (start us, length us, event | category | flops | bytes accessed | tf_op | source)
XLA Modules:
  0.0 141.9 jit_solution(8679170944378737934)
XLA Ops:
  7.2 0.7 reduce-scatter.2.cloned.1.call-update
  7.9 0.7 copy-done.10
  8.8 0.9 fusion.26
  10.3 31.1 %reduce-scatter.2.cloned.1.call-done = f32[1,256,128]{2,1,0:T(8,128)} async-done(((f32[1,1024,128]{2,1,0:T(8,128)}), f32[1,256,128]{2,1,0:T(8,128)}) %reduce-scatter.2.cloned.1.call-update) | async-done | bytes 131088 | tf_op jit(solution)/shard_map/reduce_scatter | solution.py:77
  41.4 1.6 %scatter_custom_fusion = f32[512,128]{1,0:T(8,128)S(1)} fusion(s32[256]{0:T(256)S(1)} %bitcast.159, f32[1,256,128]{2,1,0:T(8,128)} %reduce-scatter.2.cloned.1.call-done, f32[]{:T(128)} %constant.18.clone.1), kind=kCustom, calls=%fused_computation.91 | custom fusion | bytes 393220 | tf_op jit(solution)/shard_map/scatter | solution.py:79
  43.0 0.9 copy.40
  43.9 16.3 %all-to-all-start = ((f32[4,128,128]{2,0,1:T(4,128)}), f32[4,128,128]{2,0,1:T(4,128)S(1)}, u32[]{:S(2)}, u32[]{:S(2)}) async-start(f32[4,128,128]{2,0,1:T(4,128)} %copy.40), calls=%async_computation.1 | async-start | bytes 524288 | tf_op jit(solution)/shard_map/all_to_all | solution.py:81
  60.2 15.0 %all-to-all-done = f32[4,128,128]{2,0,1:T(4,128)S(1)} async-done(((f32[4,128,128]{2,0,1:T(4,128)}), f32[4,128,128]{2,0,1:T(4,128)S(1)}, u32[]{:S(2)}, u32[]{:S(2)}) %all-to-all-start) | async-done | bytes 262176 | tf_op jit(solution)/shard_map/all_to_all | solution.py:81
  76.5 0.8 fusion.51
  77.7 0.7 fusion.76
  78.8 0.7 fusion.77
  82.0 0.7 fusion.80
  89.6 0.8 fusion.54
  91.9 0.8 fusion.68
  103.6 1.4 fusion.66
  105.0 0.8 copy.47
  105.8 5.5 %all-to-all-start.1 = ((bf16[4,128,128]{2,0,1:T(4,128)(2,1)}), bf16[4,128,128]{2,0,1:T(4,128)(2,1)S(1)}, u32[]{:S(2)}, u32[]{:S(2)}) async-start(bf16[4,128,128]{2,0,1:T(4,128)(2,1)} %copy.47), calls=%async_computation.2 | async-start | bytes 262144 | tf_op jit(solution)/shard_map/all_to_all | solution.py:98
  111.3 0.7 copy.53
  112.0 1.1 fusion.1
  113.1 1.1 fusion.12
  114.2 9.9 %all-to-all-done.1 = bf16[4,128,128]{2,0,1:T(4,128)(2,1)S(1)} async-done(((bf16[4,128,128]{2,0,1:T(4,128)(2,1)}), bf16[4,128,128]{2,0,1:T(4,128)(2,1)S(1)}, u32[]{:S(2)}, u32[]{:S(2)}) %all-to-all-start.1) | async-done | bytes 131104 | tf_op jit(solution)/shard_map/all_to_all | solution.py:98
  124.2 0.9 gather_fusion
  125.0 9.4 %all-gather = bf16[1024,128]{1,0:T(8,128)(2,1)S(1)} all-gather(bf16[256,128]{1,0:T(8,128)(2,1)S(1)} %gather_fusion), channel_id=2, replica_groups=mesh['dp'=4,'shard'=128] {'dp'}, dimensions={0}, use_global_device_ids=true | all-gather | bytes 327680 | tf_op jit(solution)/shard_map/all_gather | solution.py:101
  134.4 0.7 copy.69
  (79 shorter events, 24.6 us)
Async XLA Ops:
  7.2 68.6 %copy-start = (f32[1,1,4,128,128]{4,3,2,1,0:T(8,128)S(1)}, f32[1,1,4,128,128]{4,3,2,1,0:T(8,128)}, u32[]{:S(2)}) copy-start(f32[1,1,4,128,128]{4,3,2,1,0:T(8,128)} %param.17) | copy-start | bytes 786436
  7.2 34.2 %reduce-scatter.2.cloned.1.call-start = ((), (), s32[]{:S(2)}) async-start(), calls=%async_computation.3 | async-start | bytes 655360 | tf_op jit(solution)/shard_map/reduce_scatter | solution.py:77
  7.9 0.7 copy-start.10
  43.9 16.3 %copy-start.6 = (f32[1,1,4,128,128]{4,3,2,1,0:T(8,128)S(1)}, f32[1,1,4,128,128]{4,3,2,1,0:T(8,128)}, u32[]{:S(2)}) copy-start(f32[1,1,4,128,128]{4,3,2,1,0:T(8,128)} %param.12) | copy-start | bytes 786436
  43.9 31.3 %all-to-all-start = ((f32[4,128,128]{2,0,1:T(4,128)}), f32[4,128,128]{2,0,1:T(4,128)S(1)}, u32[]{:S(2)}, u32[]{:S(2)}) async-start(f32[4,128,128]{2,0,1:T(4,128)} %copy.40), calls=%async_computation.1 | async-start | bytes 524288 | tf_op jit(solution)/shard_map/all_to_all | solution.py:81
  60.2 15.2 %copy-start.7 = (f32[1,1,4,128,128]{4,3,2,1,0:T(8,128)S(1)}, f32[1,1,4,128,128]{4,3,2,1,0:T(8,128)}, u32[]{:S(2)}) copy-start(f32[1,1,4,128,128]{4,3,2,1,0:T(8,128)} %param.15) | copy-start | bytes 786436
  75.8 0.7 copy-start.3
  86.4 1.0 copy-start.1
  87.3 0.9 copy-start.5
  88.9 0.7 copy-start.2
  100.6 1.0 copy-start.8
  102.0 0.7 copy-start.4
  102.7 0.9 copy-start.9
  105.8 18.4 %all-to-all-start.1 = ((bf16[4,128,128]{2,0,1:T(4,128)(2,1)}), bf16[4,128,128]{2,0,1:T(4,128)(2,1)S(1)}, u32[]{:S(2)}, u32[]{:S(2)}) async-start(bf16[4,128,128]{2,0,1:T(4,128)(2,1)} %copy.47), calls=%async_computation.2 | async-start | bytes 262144 | tf_op jit(solution)/shard_map/all_to_all | solution.py:98
Sparse Core Ops, SparseCore 0:
  10.8 30.5 reduce-scatter.1
where the time goes:
time: 143 us; the launch traced here: 142 us
  waiting for transfers between devices  56.7 us (40%)
  matrix products  28.9 us (20%)
  starting transfers between devices  21.8 us (15%)
  between operations  14.6 us (10%)
  blocking collectives  9.36 us (7%)
  local copies, waits for them, and re-layouts  8.78 us (6%)
  other arithmetic  1.75 us (1%)
    reduce_scatter x1, waiting for transfers between devices, body(): summed = lax.psum_scatter(grad_parts, 'dp', scatter_dimension=1, tiled=True)  31.1 us
    dot_general x50, matrix products, product(): return jnp.einsum(form, left, right, precision=highest)  28.9 us
    all_to_all x1, starting transfers between devices, body(): lax.all_to_all(outgoing, 'shard', split_axis=1, concat_axis=1, tiled=True)  16.3 us
    all_to_all x1, waiting for transfers between devices, body(): lax.all_to_all(outgoing, 'shard', split_axis=1, concat_axis=1, tiled=True)  15 us
    all_to_all x1, waiting for transfers between devices, body(): lax.all_to_all(weights, 'shard', split_axis=1, concat_axis=1, tiled=True)  9.92 us
    all_gather x1, blocking collectives, body(): new_params = lax.all_gather(own_rows, 'dp', axis=0, tiled=True)  9.36 us
    all_to_all x1, starting transfers between devices, body(): lax.all_to_all(weights, 'shard', split_axis=1, concat_axis=1, tiled=True)  5.54 us
    unnamed x24, local copies, waits for them, and re-layouts  4.36 us
  transfers between devices with their start and end apart: 3, of which 3 were waited for; matrix products, arithmetic and copies ran while one was open for 3% of the time, Pallas kernels for 0%

commit v1 on v0

v1 whole, which is shorter than its diff:
```python
import jax
import jax.numpy as jnp
from jax import lax
from jax.sharding import PartitionSpec as P

NS_STEPS = 10


beta_one = 0.9
beta_two = 0.95
stat_decay = 0.95
learn_rate = 0.05
weight_decay = 0.01
adam_eps = 1e-08
highest = lax.Precision.HIGHEST


def product(form, left, right):
    return jnp.einsum(form, left, right, precision=highest)


def slot_index(owners, shards):
    matches = (owners[..., None] == jnp.arange(shards, dtype=jnp.int32)).astype(jnp.int32)
    running = jnp.cumsum(matches, axis=1)
    return jnp.sum(matches * running, axis=-1) - 1


def orthogonal(pending):
    iterate = pending * lax.rsqrt(jnp.sum(pending * pending, axis=(1, 2), keepdims=True) + 1e-06)
    for step in range(NS_STEPS):
        gram = product("nik,njk->nij", iterate, iterate)
        iterate = 1.5 * iterate - 0.5 * product("nij,njk->nik", gram, iterate)
    return iterate


def soap_weights(gradient, master, first, second, lbasis, rbasis):
    count = gradient.shape[0]
    first_new = beta_one * first + (1.0 - beta_one) * gradient
    both = jnp.concatenate([gradient, first_new], axis=0)
    lboth = jnp.concatenate([lbasis, lbasis], axis=0)
    rboth = jnp.concatenate([rbasis, rbasis], axis=0)
    rotated = product("nik,nkl->nil", product("nji,njk->nik", lboth, both), rboth)
    grad_rot, first_rot = rotated[:count], rotated[count:]
    second_new = beta_two * second + (1.0 - beta_two) * grad_rot * grad_rot
    normed = first_rot / (jnp.sqrt(second_new) + adam_eps)
    update = product("nik,nlk->nil", product("nij,njk->nik", lbasis, normed), rbasis)
    master_new = master - learn_rate * (update + weight_decay * master)
    return master_new, first_new, second_new


def soap_bases(gradient, lstat, rstat, lbasis, rbasis):
    count = gradient.shape[0]
    lstat_new = stat_decay * lstat + (1.0 - stat_decay) * product(
        "nik,njk->nij", gradient, gradient
    )
    rstat_new = stat_decay * rstat + (1.0 - stat_decay) * product(
        "nki,nkj->nij", gradient, gradient
    )
    pending = product(
        "nij,njk->nik",
        jnp.concatenate([lstat_new, rstat_new], axis=0),
        jnp.concatenate([lbasis, rbasis], axis=0),
    )
    bases = orthogonal(pending)
    return lstat_new, rstat_new, bases[:count], bases[count:]


def body(
    grad_parts,
    owner,
    master,
    first_moment,
    second_moment,
    left_stat,
    right_stat,
    left_basis,
    right_basis,
):
    shards = lax.axis_size("shard")
    groups = lax.axis_size("dp")
    my_group = lax.axis_index("dp")
    capacity = master.shape[2]
    block_size = master.shape[4]
    piece_len = grad_parts.shape[2]
    tile_count = owner.shape[0]
    per_group = tile_count // groups
    owners = owner.reshape(groups, per_group)
    place_index = slot_index(owners, shards) * shards + owners
    own_place = lax.dynamic_index_in_dim(place_index, my_group, 0, keepdims=False)
    parts = grad_parts.reshape(groups, per_group, piece_len)
    summed = jnp.sum(lax.all_to_all(parts, "dp", 0, 0, tiled=True), axis=0)
    outgoing = jnp.zeros((capacity * shards, piece_len), jnp.float32)
    outgoing = outgoing.at[own_place].set(summed)
    outgoing = outgoing.reshape(capacity, shards, piece_len)
    incoming = lax.all_to_all(outgoing, "shard", split_axis=1, concat_axis=1, tiled=True)

    def as_tiles(array):
        return array.reshape(capacity, block_size, block_size)

    gradient = incoming.reshape(capacity, block_size, block_size)
    master_new, first_new, second_new = soap_weights(
        gradient,
        as_tiles(master),
        as_tiles(first_moment),
        as_tiles(second_moment),
        as_tiles(left_basis),
        as_tiles(right_basis),
    )
    weights = master_new.astype(jnp.bfloat16)
    weights, gradient, left_stat, right_stat, left_basis, right_basis = lax.optimization_barrier(
        (weights, gradient, left_stat, right_stat, left_basis, right_basis)
    )
    returned = lax.all_to_all(weights, "shard", split_axis=1, concat_axis=1, tiled=True)
    returned = returned.reshape(capacity * shards, piece_len)
    own_rows = returned[own_place]
    spread = jnp.broadcast_to(own_rows[None], (groups,) + own_rows.shape)
    new_params = lax.all_to_all(spread, "dp", 0, 0, tiled=True).reshape(tile_count, piece_len)
    lstat_new, rstat_new, lbasis_new, rbasis_new = soap_bases(
        gradient,
        as_tiles(left_stat),
        as_tiles(right_stat),
        as_tiles(left_basis),
        as_tiles(right_basis),
    )
    results = (master_new, first_new, second_new, lstat_new, rstat_new, lbasis_new, rbasis_new)
    shaped = [item.reshape(1, 1, capacity, block_size, block_size) for item in results]
    return (new_params, *shaped)


def solution(mesh):
    state = P("dp", "shard", None, None, None)
    placed = (P("dp", None, "shard"), P()) + (state,) * 7
    return jax.shard_map(
        body,
        mesh=mesh,
        in_specs=placed,
        out_specs=(P(None, "shard"),) + (state,) * 7,
        check_vma=False,
    )
```

time: 143 us -> 107 us (0.75)
  waiting for transfers between devices: 56.7 us -> 36.8 us
  between operations: 14.6 us -> 0.97 us
  starting transfers between devices: 21.8 us -> 34.5 us
  blocking collectives: 9.36 us -> 0 us
  matrix products: 28.9 us -> 24.4 us
    reduce_scatter x1 -> x0, waiting for transfers between devices: 31.1 us -> none  [body(): summed = lax.psum_scatter(grad_parts, 'dp', scatter_dimension=1, tiled=True)]
    all_to_all x0 -> x2, waiting for transfers between devices: none -> 9.69 us  [the longest x1 5.17 us: body(): lax.all_to_all(spread, 'dp', 0, 0, tiled=True)]
    all_gather x1 -> x0, blocking collectives: 9.36 us -> none  [body(): new_params = lax.all_gather(own_rows, 'dp', axis=0, tiled=True)]
    all_to_all x0 -> x2, starting transfers between devices: none -> 8.26 us  [the longest x1 4.85 us: body(): summed = jnp.sum(lax.all_to_all(parts, 'dp', 0, 0, tiled=True), axis=0)]
    dot_general x50 -> x27, matrix products: 28.9 us -> 24.4 us  [product(): return jnp.einsum(form, left, right, precision=highest)]
    all_to_all x1, starting transfers between devices: 16.3 us -> 20.7 us  [body(): lax.all_to_all(outgoing, 'shard', split_axis=1, concat_axis=1, tiled=True)]
    all_to_all x1, waiting for transfers between devices: 9.92 us -> 12.2 us  [body(): lax.all_to_all(weights, 'shard', split_axis=1, concat_axis=1, tiled=True)]
  transfers between devices with their start and end apart: 3 -> 4, of which waited for: 3 -> 4; matrix products, arithmetic and copies ran while one was open for 3% -> 3% of each run, Pallas kernels for 0% -> 0%
where the time goes in v1:
time: 107 us
  waiting for transfers between devices  36.8 us (34%)
  starting transfers between devices  34.5 us (32%)
  matrix products  24.4 us (23%)
  local copies, waits for them, and re-layouts  7.68 us (7%)
  other arithmetic  2.47 us (2%)
    dot_general x27, matrix products, product(): return jnp.einsum(form, left, right, precision=highest)  24.4 us
    all_to_all x1, starting transfers between devices, body(): lax.all_to_all(outgoing, 'shard', split_axis=1, concat_axis=1, tiled=True)  20.7 us
    all_to_all x1, waiting for transfers between devices, body(): lax.all_to_all(outgoing, 'shard', split_axis=1, concat_axis=1, tiled=True)  14.9 us
    all_to_all x1, waiting for transfers between devices, body(): lax.all_to_all(weights, 'shard', split_axis=1, concat_axis=1, tiled=True)  12.2 us
    all_to_all x1, starting transfers between devices, body(): lax.all_to_all(weights, 'shard', split_axis=1, concat_axis=1, tiled=True)  5.54 us
    all_to_all x1, waiting for transfers between devices, body(): lax.all_to_all(spread, 'dp', 0, 0, tiled=True)  5.17 us
    all_to_all x1, starting transfers between devices, body(): summed = jnp.sum(lax.all_to_all(parts, 'dp', 0, 0, tiled=True), axis=0)  4.85 us
    all_to_all x1, waiting for transfers between devices, body(): summed = jnp.sum(lax.all_to_all(parts, 'dp', 0, 0, tiled=True), axis=0)  4.53 us
  transfers between devices with their start and end apart: 4, of which 4 were waited for; matrix products, arithmetic and copies ran while one was open for 3% of the time, Pallas kernels for 0%

profile of v1, /device:TPU:1, one launch (start us, length us, event | category | flops | bytes accessed | tf_op | source)
XLA Modules:
  0.0 106.7 jit_solution(5188002990233312155)
XLA Ops:
  0.6 4.9 %all-to-all-start = ((f32[4,256,128]{2,1,0:T(8,128)}), f32[4,256,128]{2,1,0:T(8,128)S(1)}, u32[]{:S(2)}, u32[]{:S(2)}) async-start(f32[4,256,128]{2,1,0:T(8,128)} %bitcast.106), calls=%async_computation | async-start | bytes 1048576 | tf_op jit(solution)/shard_map/all_to_all | solution.py:91
  6.3 0.9 fusion.14
  7.9 4.5 %all-to-all-done = f32[4,256,128]{2,1,0:T(8,128)S(1)} async-done(((f32[4,256,128]{2,1,0:T(8,128)}), f32[4,256,128]{2,1,0:T(8,128)S(1)}, u32[]{:S(2)}, u32[]{:S(2)}) %all-to-all-start) | async-done | bytes 524320 | tf_op jit(solution)/shard_map/all_to_all | solution.py:91
  12.5 1.2 %scatter_custom_fusion = f32[512,128]{1,0:T(8,128)S(1)} fusion(s32[256]{0:T(256)S(1)} %bitcast.109, f32[256,128]{1,0:T(8,128)S(1)} %reduce_sum.28, f32[]{:T(128)} %constant.17.clone.1), kind=kCustom, calls=%fused_computation.75 | custom fusion | bytes 262148 | tf_op jit(solution)/shard_map/scatter | solution.py:93
  13.7 0.9 copy.38
  14.6 20.7 %all-to-all-start.1 = ((f32[4,128,128]{2,0,1:T(4,128)}), f32[4,128,128]{2,0,1:T(4,128)S(1)}, u32[]{:S(2)}, u32[]{:S(2)}) async-start(f32[4,128,128]{2,0,1:T(4,128)} %copy.38), calls=%async_computation.1 | async-start | bytes 524288 | tf_op jit(solution)/shard_map/all_to_all | solution.py:95
  35.5 14.9 %all-to-all-done.1 = f32[4,128,128]{2,0,1:T(4,128)S(1)} async-done(((f32[4,128,128]{2,0,1:T(4,128)}), f32[4,128,128]{2,0,1:T(4,128)S(1)}, u32[]{:S(2)}, u32[]{:S(2)}) %all-to-all-start.1) | async-done | bytes 262176 | tf_op jit(solution)/shard_map/all_to_all | solution.py:95
  53.4 1.4 %fusion.63 = (bf16[4,128,128]{2,1,0:T(8,128)(2,1)S(1)}, f32[4,128,128]{2,1,0:T(8,128)}) fusion(f32[4,128,128]{1,2,0:T(8,128)S(1)} %fusion.39, f32[1,1,4,128,128]{4,3,2,1,0:T(8,128)S(1)} %copy-done, f32[1,1,4,128,128]{4,3,2,1,0:T(8,128)S(1)} %copy-done.9), kind=kOutput, calls=%fused_computation.94 | convolution fusion | flops 100990976 | bytes 1179648 | tf_op jit(solution)/shard_map/nik,nlk->nil/dot_general | solution.py:19
  57.2 1.3 %fusion.35 = f32[8,128,128]{2,1,0:T(8,128)S(1)} fusion(f32[8,128,128]{2,1,0:T(8,128)S(1)} %get-tuple-element.27, f32[8]{0:T(128)S(1)} %add_rsqrt_fusion), kind=kOutput, calls=%fused_computation.54 | convolution fusion | flops 201457664 | bytes 1048608 | tf_op jit(solution)/shard_map/nik,njk->nij/dot_general | solution.py:19
  59.2 1.2 %fusion.64 = f32[8,128,128]{2,1,0:T(8,128)S(1)} fusion(f32[8,128,128]{2,1,0:T(8,128)S(1)} %fusion.9), kind=kOutput, calls=%fused_computation.95 | convolution fusion | flops 201326592 | bytes 1048576 | tf_op jit(solution)/shard_map/nik,njk->nij/dot_general | solution.py:19
  61.1 1.2 %fusion.65 = f32[8,128,128]{2,1,0:T(8,128)S(1)} fusion(f32[8,128,128]{2,1,0:T(8,128)S(1)} %fusion.8), kind=kOutput, calls=%fused_computation.96 | convolution fusion | flops 201326592 | bytes 1048576 | tf_op jit(solution)/shard_map/nik,njk->nij/dot_general | solution.py:19
  63.0 1.2 %fusion.66 = f32[8,128,128]{2,1,0:T(8,128)S(1)} fusion(f32[8,128,128]{2,1,0:T(8,128)S(1)} %fusion.7), kind=kOutput, calls=%fused_computation.97 | convolution fusion | flops 201326592 | bytes 1048576 | tf_op jit(solution)/shard_map/nik,njk->nij/dot_general | solution.py:19
  64.9 1.2 %fusion.67 = f32[8,128,128]{2,1,0:T(8,128)S(1)} fusion(f32[8,128,128]{2,1,0:T(8,128)S(1)} %fusion.6), kind=kOutput, calls=%fused_computation.98 | convolution fusion | flops 201326592 | bytes 1048576 | tf_op jit(solution)/shard_map/nik,njk->nij/dot_general | solution.py:19
  66.8 1.4 %fusion.68 = f32[8,128,128]{2,1,0:T(8,128)S(1)} fusion(f32[8,128,128]{2,1,0:T(8,128)S(1)} %fusion.5), kind=kOutput, calls=%fused_computation.99 | convolution fusion | flops 201326592 | bytes 1048576 | tf_op jit(solution)/shard_map/nik,njk->nij/dot_general | solution.py:19
  68.9 1.2 %fusion.69 = f32[8,128,128]{2,1,0:T(8,128)S(1)} fusion(f32[8,128,128]{2,1,0:T(8,128)S(1)} %fusion.4), kind=kOutput, calls=%fused_computation.100 | convolution fusion | flops 201326592 | bytes 1048576 | tf_op jit(solution)/shard_map/nik,njk->nij/dot_general | solution.py:19
  70.8 1.2 %fusion.70 = f32[8,128,128]{2,1,0:T(8,128)S(1)} fusion(f32[8,128,128]{2,1,0:T(8,128)S(1)} %fusion.3), kind=kOutput, calls=%fused_computation.101 | convolution fusion | flops 201326592 | bytes 1048576 | tf_op jit(solution)/shard_map/nik,njk->nij/dot_general | solution.py:19
  72.7 1.2 %fusion.71 = f32[8,128,128]{2,1,0:T(8,128)S(1)} fusion(f32[8,128,128]{2,1,0:T(8,128)S(1)} %fusion.2), kind=kOutput, calls=%fused_computation.102 | convolution fusion | flops 201326592 | bytes 1048576 | tf_op jit(solution)/shard_map/nik,njk->nij/dot_general | solution.py:19
  74.6 1.2 %fusion.72 = f32[8,128,128]{2,1,0:T(8,128)S(1)} fusion(f32[8,128,128]{2,1,0:T(8,128)S(1)} %fusion.1), kind=kOutput, calls=%fused_computation.103 | convolution fusion | flops 201326592 | bytes 1048576 | tf_op jit(solution)/shard_map/nik,njk->nij/dot_general | solution.py:19
  76.6 5.5 %all-to-all-start.2 = ((bf16[4,128,128]{2,0,1:T(4,128)(2,1)}), bf16[4,128,128]{2,0,1:T(4,128)(2,1)S(1)}, u32[]{:S(2)}, u32[]{:S(2)}) async-start(bf16[4,128,128]{2,0,1:T(4,128)(2,1)} %copy.44), calls=%async_computation.2 | async-start | bytes 262144 | tf_op jit(solution)/shard_map/all_to_all | solution.py:113
  82.8 12.2 %all-to-all-done.2 = bf16[4,128,128]{2,0,1:T(4,128)(2,1)S(1)} async-done(((bf16[4,128,128]{2,0,1:T(4,128)(2,1)}), bf16[4,128,128]{2,0,1:T(4,128)(2,1)S(1)}, u32[]{:S(2)}, u32[]{:S(2)}) %all-to-all-start.2) | async-done | bytes 131104 | tf_op jit(solution)/shard_map/all_to_all | solution.py:113
  95.0 0.9 gather_fusion
  96.6 3.4 %all-to-all-start.3 = ((bf16[4,256,128]{2,1,0:T(8,128)(2,1)}), bf16[4,256,128]{2,1,0:T(8,128)(2,1)S(1)}, u32[]{:S(2)}, u32[]{:S(2)}) async-start(bf16[4,256,128]{2,1,0:T(8,128)(2,1)} %broadcast_in_dim.5), calls=%async_computation.3 | async-start | bytes 524288 | tf_op jit(solution)/shard_map/all_to_all | solution.py:117
  100.0 0.9 slice_bitcast_fusion
  100.9 5.2 %all-to-all-done.3 = bf16[4,256,128]{2,1,0:T(8,128)(2,1)S(1)} async-done(((bf16[4,256,128]{2,1,0:T(8,128)(2,1)}), bf16[4,256,128]{2,1,0:T(8,128)(2,1)S(1)}, u32[]{:S(2)}, u32[]{:S(2)}) %all-to-all-start.3) | async-done | bytes 262176 | tf_op jit(solution)/shard_map/all_to_all | solution.py:117
  (56 shorter events, 16.1 us)
Async XLA Ops:
  0.6 11.8 %all-to-all-start = ((f32[4,256,128]{2,1,0:T(8,128)}), f32[4,256,128]{2,1,0:T(8,128)S(1)}, u32[]{:S(2)}, u32[]{:S(2)}) async-start(f32[4,256,128]{2,1,0:T(8,128)} %bitcast.106), calls=%async_computation | async-start | bytes 1048576 | tf_op jit(solution)/shard_map/all_to_all | solution.py:91
  5.5 0.7 copy-start.10
  14.6 20.7 %copy-start.4 = (f32[1,1,4,128,128]{4,3,2,1,0:T(8,128)S(1)}, f32[1,1,4,128,128]{4,3,2,1,0:T(8,128)}, u32[]{:S(2)}) copy-start(f32[1,1,4,128,128]{4,3,2,1,0:T(8,128)} %param.16) | copy-start | bytes 786436
  14.6 35.8 %all-to-all-start.1 = ((f32[4,128,128]{2,0,1:T(4,128)}), f32[4,128,128]{2,0,1:T(4,128)S(1)}, u32[]{:S(2)}, u32[]{:S(2)}) async-start(f32[4,128,128]{2,0,1:T(4,128)} %copy.38), calls=%async_computation.1 | async-start | bytes 524288 | tf_op jit(solution)/shard_map/all_to_all | solution.py:95
  35.3 15.1 %copy-start.8 = (f32[1,1,4,128,128]{4,3,2,1,0:T(8,128)S(1)}, f32[1,1,4,128,128]{4,3,2,1,0:T(8,128)}, u32[]{:S(2)}) copy-start(f32[1,1,4,128,128]{4,3,2,1,0:T(8,128)} %param.12) | copy-start | bytes 786436
  50.4 0.7 copy-start.1
  50.4 1.0 copy-start
  51.5 0.9 copy-start.7
  52.4 0.9 copy-start.9
  53.4 1.4 %copy-start.5 = (f32[1,1,4,128,128]{4,3,2,1,0:T(8,128)S(1)}, f32[1,1,4,128,128]{4,3,2,1,0:T(8,128)}, u32[]{:S(2)}) copy-start(f32[1,1,4,128,128]{4,3,2,1,0:T(8,128)} %param.14) | copy-start | bytes 786436
  54.8 1.0 copy-start.6
  55.7 0.7 copy-start.2
  56.3 0.8 copy-start.3
  76.6 18.4 %all-to-all-start.2 = ((bf16[4,128,128]{2,0,1:T(4,128)(2,1)}), bf16[4,128,128]{2,0,1:T(4,128)(2,1)S(1)}, u32[]{:S(2)}, u32[]{:S(2)}) async-start(bf16[4,128,128]{2,0,1:T(4,128)(2,1)} %copy.44), calls=%async_computation.2 | async-start | bytes 262144 | tf_op jit(solution)/shard_map/all_to_all | solution.py:113
  96.6 9.5 %all-to-all-start.3 = ((bf16[4,256,128]{2,1,0:T(8,128)(2,1)}), bf16[4,256,128]{2,1,0:T(8,128)(2,1)S(1)}, u32[]{:S(2)}, u32[]{:S(2)}) async-start(bf16[4,256,128]{2,1,0:T(8,128)(2,1)} %broadcast_in_dim.5), calls=%async_computation.3 | async-start | bytes 524288 | tf_op jit(solution)/shard_map/all_to_all | solution.py:117

commit v2 on v1

--- a/solution.py
+++ b/solution.py
@@ -13,10 +13,11 @@
 weight_decay = 0.01
 adam_eps = 1e-08
 highest = lax.Precision.HIGHEST
+high = lax.Precision.HIGH
 
 
-def product(form, left, right):
-    return jnp.einsum(form, left, right, precision=highest)
+def product(form, left, right, precision=highest):
+    return jnp.einsum(form, left, right, precision=precision)
 
 
 def slot_index(owners, shards):
@@ -28,8 +29,8 @@
 def orthogonal(pending):
     iterate = pending * lax.rsqrt(jnp.sum(pending * pending, axis=(1, 2), keepdims=True) + 1e-06)
     for step in range(NS_STEPS):
-        gram = product("nik,njk->nij", iterate, iterate)
-        iterate = 1.5 * iterate - 0.5 * product("nij,njk->nik", gram, iterate)
+        gram = product("nik,njk->nij", iterate, iterate, high)
+        iterate = 1.5 * iterate - 0.5 * product("nij,njk->nik", gram, iterate, high)
     return iterate
 
 

time: 107 us -> 99.3 us (0.928)
  matrix products: 24.4 us -> 16.1 us
    dot_general x27, matrix products: 24.4 us -> 16.1 us  [product(): return jnp.einsum(form, left, right, precision=precision)]
where the time goes in v2:
time: 99.3 us; the launch traced here: 98.8 us
  waiting for transfers between devices  37 us (37%)
  starting transfers between devices  34.5 us (35%)
  matrix products  16.1 us (16%)
  local copies, waits for them, and re-layouts  7.68 us (8%)
  other arithmetic  2.47 us (2%)
    all_to_all x1, starting transfers between devices, body(): lax.all_to_all(outgoing, 'shard', split_axis=1, concat_axis=1, tiled=True)  20.7 us
    dot_general x27, matrix products, product(): return jnp.einsum(form, left, right, precision=precision)  16.1 us
    all_to_all x1, waiting for transfers between devices, body(): lax.all_to_all(outgoing, 'shard', split_axis=1, concat_axis=1, tiled=True)  14.9 us
    all_to_all x1, waiting for transfers between devices, body(): lax.all_to_all(weights, 'shard', split_axis=1, concat_axis=1, tiled=True)  12.4 us
    all_to_all x1, starting transfers between devices, body(): lax.all_to_all(weights, 'shard', split_axis=1, concat_axis=1, tiled=True)  5.54 us
    all_to_all x1, waiting for transfers between devices, body(): lax.all_to_all(spread, 'dp', 0, 0, tiled=True)  5.17 us
    all_to_all x1, starting transfers between devices, body(): summed = jnp.sum(lax.all_to_all(parts, 'dp', 0, 0, tiled=True), axis=0)  4.85 us
    all_to_all x1, waiting for transfers between devices, body(): summed = jnp.sum(lax.all_to_all(parts, 'dp', 0, 0, tiled=True), axis=0)  4.53 us
  transfers between devices with their start and end apart: 4, of which 4 were waited for; matrix products, arithmetic and copies ran while one was open for 3% of the time, Pallas kernels for 0%

profile of v2, /device:TPU:1, one launch (start us, length us, event | category | flops | bytes accessed | tf_op | source)
XLA Modules:
  0.0 98.8 jit_solution(17223329904262207598)
XLA Ops:
  0.6 4.9 %all-to-all-start = ((f32[4,256,128]{2,1,0:T(8,128)}), f32[4,256,128]{2,1,0:T(8,128)S(1)}, u32[]{:S(2)}, u32[]{:S(2)}) async-start(f32[4,256,128]{2,1,0:T(8,128)} %bitcast.106), calls=%async_computation | async-start | bytes 1048576 | tf_op jit(solution)/shard_map/all_to_all | solution.py:92
  5.5 0.7 copy-done.10
  6.3 0.9 fusion.14
  7.9 4.5 %all-to-all-done = f32[4,256,128]{2,1,0:T(8,128)S(1)} async-done(((f32[4,256,128]{2,1,0:T(8,128)}), f32[4,256,128]{2,1,0:T(8,128)S(1)}, u32[]{:S(2)}, u32[]{:S(2)}) %all-to-all-start) | async-done | bytes 524320 | tf_op jit(solution)/shard_map/all_to_all | solution.py:92
  12.5 1.2 %scatter_custom_fusion = f32[512,128]{1,0:T(8,128)S(1)} fusion(s32[256]{0:T(256)S(1)} %bitcast.109, f32[256,128]{1,0:T(8,128)S(1)} %reduce_sum.28, f32[]{:T(128)} %constant.17.clone.1), kind=kCustom, calls=%fused_computation.75 | custom fusion | bytes 262148 | tf_op jit(solution)/shard_map/scatter | solution.py:94
  13.7 0.9 copy.38
  14.6 20.7 %all-to-all-start.1 = ((f32[4,128,128]{2,0,1:T(4,128)}), f32[4,128,128]{2,0,1:T(4,128)S(1)}, u32[]{:S(2)}, u32[]{:S(2)}) async-start(f32[4,128,128]{2,0,1:T(4,128)} %copy.38), calls=%async_computation.1 | async-start | bytes 524288 | tf_op jit(solution)/shard_map/all_to_all | solution.py:96
  35.5 14.9 %all-to-all-done.1 = f32[4,128,128]{2,0,1:T(4,128)S(1)} async-done(((f32[4,128,128]{2,0,1:T(4,128)}), f32[4,128,128]{2,0,1:T(4,128)S(1)}, u32[]{:S(2)}, u32[]{:S(2)}) %all-to-all-start.1) | async-done | bytes 262176 | tf_op jit(solution)/shard_map/all_to_all | solution.py:96
  53.4 1.4 %fusion.63 = (bf16[4,128,128]{2,1,0:T(8,128)(2,1)S(1)}, f32[4,128,128]{2,1,0:T(8,128)}) fusion(f32[4,128,128]{1,2,0:T(8,128)S(1)} %fusion.39, f32[1,1,4,128,128]{4,3,2,1,0:T(8,128)S(1)} %copy-done, f32[1,1,4,128,128]{4,3,2,1,0:T(8,128)S(1)} %copy-done.9), kind=kOutput, calls=%fused_computation.94 | convolution fusion | flops 100990976 | bytes 1179648 | tf_op jit(solution)/shard_map/nik,nlk->nil/dot_general | solution.py:20
  56.4 0.7 multiply_reduce_fusion
  57.2 0.8 fusion.35
  58.4 0.7 fusion.64
  62.7 0.7 fusion.68
  63.8 0.7 fusion.69
  67.0 0.9 fusion.72
  67.9 0.8 copy.44
  68.6 5.5 %all-to-all-start.2 = ((bf16[4,128,128]{2,0,1:T(4,128)(2,1)}), bf16[4,128,128]{2,0,1:T(4,128)(2,1)S(1)}, u32[]{:S(2)}, u32[]{:S(2)}) async-start(bf16[4,128,128]{2,0,1:T(4,128)(2,1)} %copy.44), calls=%async_computation.2 | async-start | bytes 262144 | tf_op jit(solution)/shard_map/all_to_all | solution.py:114
  74.6 12.4 %all-to-all-done.2 = bf16[4,128,128]{2,0,1:T(4,128)(2,1)S(1)} async-done(((bf16[4,128,128]{2,0,1:T(4,128)(2,1)}), bf16[4,128,128]{2,0,1:T(4,128)(2,1)S(1)}, u32[]{:S(2)}, u32[]{:S(2)}) %all-to-all-start.2) | async-done | bytes 131104 | tf_op jit(solution)/shard_map/all_to_all | solution.py:114
  87.0 0.9 gather_fusion
  87.9 0.7 broadcast_in_dim.5
  88.6 3.4 %all-to-all-start.3 = ((bf16[4,256,128]{2,1,0:T(8,128)(2,1)}), bf16[4,256,128]{2,1,0:T(8,128)(2,1)S(1)}, u32[]{:S(2)}, u32[]{:S(2)}) async-start(bf16[4,256,128]{2,1,0:T(8,128)(2,1)} %broadcast_in_dim.5), calls=%async_computation.3 | async-start | bytes 524288 | tf_op jit(solution)/shard_map/all_to_all | solution.py:118
  92.0 0.9 slice_bitcast_fusion
  92.9 5.2 %all-to-all-done.3 = bf16[4,256,128]{2,1,0:T(8,128)(2,1)S(1)} async-done(((bf16[4,256,128]{2,1,0:T(8,128)(2,1)}), bf16[4,256,128]{2,1,0:T(8,128)(2,1)S(1)}, u32[]{:S(2)}, u32[]{:S(2)}) %all-to-all-start.3) | async-done | bytes 262176 | tf_op jit(solution)/shard_map/all_to_all | solution.py:118
  98.1 0.7 copy.62
  (56 shorter events, 12.9 us)
Async XLA Ops:
  0.6 11.8 %all-to-all-start = ((f32[4,256,128]{2,1,0:T(8,128)}), f32[4,256,128]{2,1,0:T(8,128)S(1)}, u32[]{:S(2)}, u32[]{:S(2)}) async-start(f32[4,256,128]{2,1,0:T(8,128)} %bitcast.106), calls=%async_computation | async-start | bytes 1048576 | tf_op jit(solution)/shard_map/all_to_all | solution.py:92
  5.5 0.7 copy-start.10
  14.6 20.7 %copy-start.4 = (f32[1,1,4,128,128]{4,3,2,1,0:T(8,128)S(1)}, f32[1,1,4,128,128]{4,3,2,1,0:T(8,128)}, u32[]{:S(2)}) copy-start(f32[1,1,4,128,128]{4,3,2,1,0:T(8,128)} %param.16) | copy-start | bytes 786436
  14.6 35.8 %all-to-all-start.1 = ((f32[4,128,128]{2,0,1:T(4,128)}), f32[4,128,128]{2,0,1:T(4,128)S(1)}, u32[]{:S(2)}, u32[]{:S(2)}) async-start(f32[4,128,128]{2,0,1:T(4,128)} %copy.38), calls=%async_computation.1 | async-start | bytes 524288 | tf_op jit(solution)/shard_map/all_to_all | solution.py:96
  35.3 15.1 %copy-start.8 = (f32[1,1,4,128,128]{4,3,2,1,0:T(8,128)S(1)}, f32[1,1,4,128,128]{4,3,2,1,0:T(8,128)}, u32[]{:S(2)}) copy-start(f32[1,1,4,128,128]{4,3,2,1,0:T(8,128)} %param.12) | copy-start | bytes 786436
  50.4 0.7 copy-start.1
  50.4 1.0 %copy-start = (f32[1,1,4,128,128]{4,3,2,1,0:T(8,128)S(1)}, f32[1,1,4,128,128]{4,3,2,1,0:T(8,128)}, u32[]{:S(2)}) copy-start(f32[1,1,4,128,128]{4,3,2,1,0:T(8,128)} %param.17) | copy-start | bytes 786436
  51.5 0.9 copy-start.7
  52.4 0.9 copy-start.9
  53.4 1.4 %copy-start.5 = (f32[1,1,4,128,128]{4,3,2,1,0:T(8,128)S(1)}, f32[1,1,4,128,128]{4,3,2,1,0:T(8,128)}, u32[]{:S(2)}) copy-start(f32[1,1,4,128,128]{4,3,2,1,0:T(8,128)} %param.14) | copy-start | bytes 786436
  54.8 1.0 copy-start.6
  55.7 0.7 copy-start.2
  56.3 0.8 copy-start.3
  68.6 18.4 %all-to-all-start.2 = ((bf16[4,128,128]{2,0,1:T(4,128)(2,1)}), bf16[4,128,128]{2,0,1:T(4,128)(2,1)S(1)}, u32[]{:S(2)}, u32[]{:S(2)}) async-start(bf16[4,128,128]{2,0,1:T(4,128)(2,1)} %copy.44), calls=%async_computation.2 | async-start | bytes 262144 | tf_op jit(solution)/shard_map/all_to_all | solution.py:114
  88.6 9.5 %all-to-all-start.3 = ((bf16[4,256,128]{2,1,0:T(8,128)(2,1)}), bf16[4,256,128]{2,1,0:T(8,128)(2,1)S(1)}, u32[]{:S(2)}, u32[]{:S(2)}) async-start(bf16[4,256,128]{2,1,0:T(8,128)(2,1)} %broadcast_in_dim.5), calls=%async_computation.3 | async-start | bytes 524288 | tf_op jit(solution)/shard_map/all_to_all | solution.py:118

commit v3 on v2

--- a/solution.py
+++ b/solution.py
@@ -28,10 +28,11 @@
 
 def orthogonal(pending):
     iterate = pending * lax.rsqrt(jnp.sum(pending * pending, axis=(1, 2), keepdims=True) + 1e-06)
-    for step in range(NS_STEPS):
+    def newton_schulz(step, iterate):
         gram = product("nik,njk->nij", iterate, iterate, high)
-        iterate = 1.5 * iterate - 0.5 * product("nij,njk->nik", gram, iterate, high)
-    return iterate
+        return 1.5 * iterate - 0.5 * product("nij,njk->nik", gram, iterate, high)
+
+    return lax.fori_loop(0, NS_STEPS, newton_schulz, iterate)
 
 
 def soap_weights(gradient, master, first, second, lbasis, rbasis):

time: 99.3 us -> 88.6 us (0.89)
  waiting for transfers between devices: 37 us -> 26.2 us
    all_to_all x1, waiting for transfers between devices: 12.4 us -> 1.42 us  [body(): lax.all_to_all(weights, 'shard', split_axis=1, concat_axis=1, tiled=True)]
  transfers between devices with their start and end apart: 4 -> 4, of which waited for: 4 -> 4; matrix products, arithmetic and copies ran while one was open for 3% -> 16% of each run, Pallas kernels for 0% -> 0%
where the time goes in v3:
time: 88.6 us; the launch traced here: 88.1 us
  starting transfers between devices  34.3 us (39%)
  waiting for transfers between devices  26.2 us (30%)
  matrix products  15.7 us (18%)
  local copies, waits for them, and re-layouts  8.05 us (9%)
  other arithmetic  2.57 us (3%)
    all_to_all x1, starting transfers between devices, body(): lax.all_to_all(outgoing, 'shard', split_axis=1, concat_axis=1, tiled=True)  20.5 us
    dot_general x27, matrix products, product(): return jnp.einsum(form, left, right, precision=precision)  15.7 us
    all_to_all x1, waiting for transfers between devices, body(): lax.all_to_all(outgoing, 'shard', split_axis=1, concat_axis=1, tiled=True)  15.1 us
    all_to_all x1, starting transfers between devices, body(): lax.all_to_all(weights, 'shard', split_axis=1, concat_axis=1, tiled=True)  5.54 us
    all_to_all x1, waiting for transfers between devices, body(): lax.all_to_all(spread, 'dp', 0, 0, tiled=True)  5.17 us
    all_to_all x1, starting transfers between devices, body(): summed = jnp.sum(lax.all_to_all(parts, 'dp', 0, 0, tiled=True), axis=0)  4.85 us
    all_to_all x1, waiting for transfers between devices, body(): summed = jnp.sum(lax.all_to_all(parts, 'dp', 0, 0, tiled=True), axis=0)  4.53 us
    all_to_all x1, starting transfers between devices, body(): lax.all_to_all(spread, 'dp', 0, 0, tiled=True)  3.41 us
  transfers between devices with their start and end apart: 4, of which 4 were waited for; matrix products, arithmetic and copies ran while one was open for 16% of the time, Pallas kernels for 0%

profile of v3, /device:TPU:1, one launch (start us, length us, event | category | flops | bytes accessed | tf_op | source)
XLA Modules:
  0.0 88.1 jit_solution(14665165257991071108)
XLA Ops:
  0.6 4.9 %all-to-all-start = ((f32[4,256,128]{2,1,0:T(8,128)}), f32[4,256,128]{2,1,0:T(8,128)S(1)}, u32[]{:S(2)}, u32[]{:S(2)}) async-start(f32[4,256,128]{2,1,0:T(8,128)} %bitcast.81), calls=%async_computation | async-start | bytes 1048576 | tf_op jit(solution)/shard_map/all_to_all | solution.py:93
  5.5 0.7 copy-done.10
  6.3 0.9 fusion.5
  7.9 4.5 %all-to-all-done = f32[4,256,128]{2,1,0:T(8,128)S(1)} async-done(((f32[4,256,128]{2,1,0:T(8,128)}), f32[4,256,128]{2,1,0:T(8,128)S(1)}, u32[]{:S(2)}, u32[]{:S(2)}) %all-to-all-start) | async-done | bytes 524320 | tf_op jit(solution)/shard_map/all_to_all | solution.py:93
  12.5 1.2 %scatter_custom_fusion = f32[512,128]{1,0:T(8,128)S(1)} fusion(s32[256]{0:T(256)S(1)} %bitcast.84, f32[256,128]{1,0:T(8,128)S(1)} %reduce_sum.28, f32[]{:T(128)} %constant.23.clone.1), kind=kCustom, calls=%fused_computation.53 | custom fusion | bytes 262148 | tf_op jit(solution)/shard_map/scatter | solution.py:95
  13.7 0.9 copy.38
  14.6 20.5 %all-to-all-start.1 = ((f32[4,128,128]{2,0,1:T(4,128)}), f32[4,128,128]{2,0,1:T(4,128)S(1)}, u32[]{:S(2)}, u32[]{:S(2)}) async-start(f32[4,128,128]{2,0,1:T(4,128)} %copy.38), calls=%async_computation.1 | async-start | bytes 524288 | tf_op jit(solution)/shard_map/all_to_all | solution.py:97
  35.3 15.1 %all-to-all-done.1 = f32[4,128,128]{2,0,1:T(4,128)S(1)} async-done(((f32[4,128,128]{2,0,1:T(4,128)}), f32[4,128,128]{2,0,1:T(4,128)S(1)}, u32[]{:S(2)}, u32[]{:S(2)}) %all-to-all-start.1) | async-done | bytes 262176 | tf_op jit(solution)/shard_map/all_to_all | solution.py:97
  53.4 1.4 %fusion.49 = (bf16[4,128,128]{2,1,0:T(8,128)(2,1)S(1)}, f32[4,128,128]{2,1,0:T(8,128)}) fusion(f32[4,128,128]{1,2,0:T(8,128)S(1)} %fusion.27, f32[1,1,4,128,128]{4,3,2,1,0:T(8,128)S(1)} %copy-done, f32[1,1,4,128,128]{4,3,2,1,0:T(8,128)S(1)} %copy-done.9), kind=kOutput, calls=%fused_computation.72 | convolution fusion | flops 100990976 | bytes 1179648 | tf_op jit(solution)/shard_map/nik,nlk->nil/dot_general | solution.py:20
  56.4 0.7 multiply_reduce_fusion
  57.2 0.8 copy.44
  57.9 5.5 %all-to-all-start.2 = ((bf16[4,128,128]{2,0,1:T(4,128)(2,1)}), bf16[4,128,128]{2,0,1:T(4,128)(2,1)S(1)}, u32[]{:S(2)}, u32[]{:S(2)}) async-start(bf16[4,128,128]{2,0,1:T(4,128)(2,1)} %copy.44), calls=%async_computation.2 | async-start | bytes 262144 | tf_op jit(solution)/shard_map/all_to_all | solution.py:115
  63.6 11.3 %while.10 = (s32[]{:T(128)}, f32[8,128,128]{2,1,0:T(8,128)S(1)}, s32[]{:T(128)}) while((s32[]{:T(128)}, f32[8,128,128]{2,1,0:T(8,128)S(1)}, s32[]{:T(128)}) %tuple.29), condition=%wide.region_7.8_spmd, body=%wide.region_6.7_spmd.sunk | while | flops 201719808 | bytes 3670061 | solution.py:35
  65.9 0.7 fusion.67
  67.0 0.7 fusion.67
  70.4 0.7 fusion.67
  71.6 0.7 fusion.67
  74.9 1.4 %all-to-all-done.2 = bf16[4,128,128]{2,0,1:T(4,128)(2,1)S(1)} async-done(((bf16[4,128,128]{2,0,1:T(4,128)(2,1)}), bf16[4,128,128]{2,0,1:T(4,128)(2,1)S(1)}, u32[]{:S(2)}, u32[]{:S(2)}) %all-to-all-start.2) | async-done | bytes 131104 | tf_op jit(solution)/shard_map/all_to_all | solution.py:115
  76.4 0.9 gather_fusion
  77.2 0.7 broadcast_in_dim.5
  78.0 3.4 %all-to-all-start.3 = ((bf16[4,256,128]{2,1,0:T(8,128)(2,1)}), bf16[4,256,128]{2,1,0:T(8,128)(2,1)S(1)}, u32[]{:S(2)}, u32[]{:S(2)}) async-start(bf16[4,256,128]{2,1,0:T(8,128)(2,1)} %broadcast_in_dim.5), calls=%async_computation.3 | async-start | bytes 524288 | tf_op jit(solution)/shard_map/all_to_all | solution.py:119
  81.4 0.9 %slice_bitcast_fusion = (f32[1,1,4,128,128]{4,3,2,1,0:T(8,128)}, f32[1,1,4,128,128]{4,3,2,1,0:T(8,128)}, f32[1,1,4,128,128]{4,3,2,1,0:T(8,128)}) fusion(f32[8,128,128]{2,1,0:T(8,128)S(1)} %get-tuple-element.32, f32[8,128,128]{2,1,0:T(8,128)S(1)} %fusion.13, f32[1,1,4,128,128]{4,3,2,1,0:T(8,128)S(1)} %copy-done.7), kind=kLoop, calls=%fused_computation.43 | loop fusion | flops 262144 | bytes 1835008 | tf_op jit(solution)/shard_map/reshape | solution.py:128
  82.3 5.2 %all-to-all-done.3 = bf16[4,256,128]{2,1,0:T(8,128)(2,1)S(1)} async-done(((bf16[4,256,128]{2,1,0:T(8,128)(2,1)}), bf16[4,256,128]{2,1,0:T(8,128)(2,1)S(1)}, u32[]{:S(2)}, u32[]{:S(2)}) %all-to-all-start.3) | async-done | bytes 262176 | tf_op jit(solution)/shard_map/all_to_all | solution.py:119
  87.4 0.7 copy.72
  (68 shorter events, 14.0 us)
Async XLA Ops:
  0.6 11.8 %all-to-all-start = ((f32[4,256,128]{2,1,0:T(8,128)}), f32[4,256,128]{2,1,0:T(8,128)S(1)}, u32[]{:S(2)}, u32[]{:S(2)}) async-start(f32[4,256,128]{2,1,0:T(8,128)} %bitcast.81), calls=%async_computation | async-start | bytes 1048576 | tf_op jit(solution)/shard_map/all_to_all | solution.py:93
  5.5 0.7 copy-start.10
  14.6 20.6 %copy-start.4 = (f32[1,1,4,128,128]{4,3,2,1,0:T(8,128)S(1)}, f32[1,1,4,128,128]{4,3,2,1,0:T(8,128)}, u32[]{:S(2)}) copy-start(f32[1,1,4,128,128]{4,3,2,1,0:T(8,128)} %param.18) | copy-start | bytes 786436
  14.6 35.8 %all-to-all-start.1 = ((f32[4,128,128]{2,0,1:T(4,128)}), f32[4,128,128]{2,0,1:T(4,128)S(1)}, u32[]{:S(2)}, u32[]{:S(2)}) async-start(f32[4,128,128]{2,0,1:T(4,128)} %copy.38), calls=%async_computation.1 | async-start | bytes 524288 | tf_op jit(solution)/shard_map/all_to_all | solution.py:97
  35.1 15.3 %copy-start.8 = (f32[1,1,4,128,128]{4,3,2,1,0:T(8,128)S(1)}, f32[1,1,4,128,128]{4,3,2,1,0:T(8,128)}, u32[]{:S(2)}) copy-start(f32[1,1,4,128,128]{4,3,2,1,0:T(8,128)} %param.14) | copy-start | bytes 786436
  50.4 0.7 copy-start.1
  50.4 1.0 %copy-start = (f32[1,1,4,128,128]{4,3,2,1,0:T(8,128)S(1)}, f32[1,1,4,128,128]{4,3,2,1,0:T(8,128)}, u32[]{:S(2)}) copy-start(f32[1,1,4,128,128]{4,3,2,1,0:T(8,128)} %param.19) | copy-start | bytes 786436
  51.5 0.9 %copy-start.7 = (f32[1,1,4,128,128]{4,3,2,1,0:T(8,128)S(1)}, f32[1,1,4,128,128]{4,3,2,1,0:T(8,128)}, u32[]{:S(2)}) copy-start(f32[1,1,4,128,128]{4,3,2,1,0:T(8,128)} %param.15) | copy-start | bytes 786436
  52.4 0.9 %copy-start.9 = (f32[1,1,4,128,128]{4,3,2,1,0:T(8,128)S(1)}, f32[1,1,4,128,128]{4,3,2,1,0:T(8,128)}, u32[]{:S(2)}) copy-start(f32[1,1,4,128,128]{4,3,2,1,0:T(8,128)} %param.13) | copy-start | bytes 786436
  53.4 1.4 %copy-start.5 = (f32[1,1,4,128,128]{4,3,2,1,0:T(8,128)S(1)}, f32[1,1,4,128,128]{4,3,2,1,0:T(8,128)}, u32[]{:S(2)}) copy-start(f32[1,1,4,128,128]{4,3,2,1,0:T(8,128)} %param.16) | copy-start | bytes 786436
  54.8 1.0 %copy-start.6 = (f32[1,1,4,128,128]{4,3,2,1,0:T(8,128)S(1)}, f32[1,1,4,128,128]{4,3,2,1,0:T(8,128)}, u32[]{:S(2)}) copy-start(f32[1,1,4,128,128]{4,3,2,1,0:T(8,128)} %param.17) | copy-start | bytes 786436
  55.7 0.7 copy-start.2
  56.3 0.8 copy-start.3
  57.9 18.4 %all-to-all-start.2 = ((bf16[4,128,128]{2,0,1:T(4,128)(2,1)}), bf16[4,128,128]{2,0,1:T(4,128)(2,1)S(1)}, u32[]{:S(2)}, u32[]{:S(2)}) async-start(bf16[4,128,128]{2,0,1:T(4,128)(2,1)} %copy.44), calls=%async_computation.2 | async-start | bytes 262144 | tf_op jit(solution)/shard_map/all_to_all | solution.py:115
  78.0 9.5 %all-to-all-start.3 = ((bf16[4,256,128]{2,1,0:T(8,128)(2,1)}), bf16[4,256,128]{2,1,0:T(8,128)(2,1)S(1)}, u32[]{:S(2)}, u32[]{:S(2)}) async-start(bf16[4,256,128]{2,1,0:T(8,128)(2,1)} %broadcast_in_dim.5), calls=%async_computation.3 | async-start | bytes 524288 | tf_op jit(solution)/shard_map/all_to_all | solution.py:119

commit v4 on v3

--- a/solution.py
+++ b/solution.py
@@ -16,7 +16,7 @@
 high = lax.Precision.HIGH
 
 
-def product(form, left, right, precision=highest):
+def product(form, left, right, precision=high):
     return jnp.einsum(form, left, right, precision=precision)
 
 
@@ -109,9 +109,6 @@
         as_tiles(right_basis),
     )
     weights = master_new.astype(jnp.bfloat16)
-    weights, gradient, left_stat, right_stat, left_basis, right_basis = lax.optimization_barrier(
-        (weights, gradient, left_stat, right_stat, left_basis, right_basis)
-    )
     returned = lax.all_to_all(weights, "shard", split_axis=1, concat_axis=1, tiled=True)
     returned = returned.reshape(capacity * shards, piece_len)
     own_rows = returned[own_place]

time: 88.6 us -> 87.7 us (0.990)
  matrix products: 15.7 us -> 14.6 us
  local copies, waits for them, and re-layouts: 8.05 us -> 9.11 us
  waiting for transfers between devices: 26.2 us -> 25.2 us
    dot_general x27, matrix products: 15.7 us -> 14.6 us  [product(): return jnp.einsum(form, left, right, precision=precision)]
    unnamed x24 -> x25, local copies, waits for them, and re-layouts: 3.03 us -> 4.1 us
    all_to_all x1, waiting for transfers between devices: 15.1 us -> 14.1 us  [body(): lax.all_to_all(outgoing, 'shard', split_axis=1, concat_axis=1, tiled=True)]
where the time goes in v4:
time: 87.7 us; the launch traced here: 87.1 us
  starting transfers between devices  34.3 us (39%)
  waiting for transfers between devices  25.2 us (29%)
  matrix products  14.6 us (17%)
  local copies, waits for them, and re-layouts  9.11 us (10%)
  other arithmetic  2.57 us (3%)
    all_to_all x1, starting transfers between devices, body(): lax.all_to_all(outgoing, 'shard', split_axis=1, concat_axis=1, tiled=True)  20.5 us
    dot_general x27, matrix products, product(): return jnp.einsum(form, left, right, precision=precision)  14.6 us
    all_to_all x1, waiting for transfers between devices, body(): lax.all_to_all(outgoing, 'shard', split_axis=1, concat_axis=1, tiled=True)  14.1 us
    all_to_all x1, starting transfers between devices, body(): lax.all_to_all(weights, 'shard', split_axis=1, concat_axis=1, tiled=True)  5.54 us
    all_to_all x1, waiting for transfers between devices, body(): lax.all_to_all(spread, 'dp', 0, 0, tiled=True)  5.17 us
    all_to_all x1, starting transfers between devices, body(): summed = jnp.sum(lax.all_to_all(parts, 'dp', 0, 0, tiled=True), axis=0)  4.85 us
    all_to_all x1, waiting for transfers between devices, body(): summed = jnp.sum(lax.all_to_all(parts, 'dp', 0, 0, tiled=True), axis=0)  4.53 us
    unnamed x25, local copies, waits for them, and re-layouts  4.1 us
  transfers between devices with their start and end apart: 4, of which 4 were waited for; matrix products, arithmetic and copies ran while one was open for 16% of the time, Pallas kernels for 0%

profile of v4, /device:TPU:1, one launch (start us, length us, event | category | flops | bytes accessed | tf_op | source)
XLA Modules:
  0.0 87.1 jit_solution(8067588684055870028)
XLA Ops:
  0.6 4.9 %all-to-all-start = ((f32[4,256,128]{2,1,0:T(8,128)}), f32[4,256,128]{2,1,0:T(8,128)S(1)}, u32[]{:S(2)}, u32[]{:S(2)}) async-start(f32[4,256,128]{2,1,0:T(8,128)} %bitcast.80), calls=%async_computation | async-start | bytes 1048576 | tf_op jit(solution)/shard_map/all_to_all | solution.py:93
  5.5 0.7 copy-done.10
  6.3 0.9 fusion.8
  7.9 4.5 %all-to-all-done = f32[4,256,128]{2,1,0:T(8,128)S(1)} async-done(((f32[4,256,128]{2,1,0:T(8,128)}), f32[4,256,128]{2,1,0:T(8,128)S(1)}, u32[]{:S(2)}, u32[]{:S(2)}) %all-to-all-start) | async-done | bytes 524320 | tf_op jit(solution)/shard_map/all_to_all | solution.py:93
  12.5 1.2 %scatter_custom_fusion = f32[512,128]{1,0:T(8,128)S(1)} fusion(s32[256]{0:T(256)S(1)} %bitcast.83, f32[256,128]{1,0:T(8,128)S(1)} %reduce_sum.28, f32[]{:T(128)} %constant.23.clone.1), kind=kCustom, calls=%fused_computation.48 | custom fusion | bytes 262148 | tf_op jit(solution)/shard_map/scatter | solution.py:95
  13.7 0.9 %copy.42 = f32[4,128,128]{2,0,1:T(4,128)} copy(f32[4,128,128]{2,1,0:T(8,128)S(1)} %bitcast.79) | data formatting | bytes 524288 | tf_op jit(solution)/shard_map/reshape | solution.py:96
  14.6 20.5 %all-to-all-start.1 = ((f32[4,128,128]{2,0,1:T(4,128)}), f32[4,128,128]{2,0,1:T(4,128)S(1)}, u32[]{:S(2)}, u32[]{:S(2)}) async-start(f32[4,128,128]{2,0,1:T(4,128)} %copy.42), calls=%async_computation.1 | async-start | bytes 524288 | tf_op jit(solution)/shard_map/all_to_all | solution.py:97
  35.3 0.8 copy-done.3
  36.2 14.1 %all-to-all-done.1 = f32[4,128,128]{2,0,1:T(4,128)S(1)} async-done(((f32[4,128,128]{2,0,1:T(4,128)}), f32[4,128,128]{2,0,1:T(4,128)S(1)}, u32[]{:S(2)}, u32[]{:S(2)}) %all-to-all-start.1) | async-done | bytes 262176 | tf_op jit(solution)/shard_map/all_to_all | solution.py:97
  51.5 0.8 multiply_reduce_fusion
  55.1 1.1 %fusion.42 = (bf16[4,128,128]{2,1,0:T(8,128)(2,1)S(1)}, f32[4,128,128]{2,1,0:T(8,128)}) fusion(f32[4,128,128]{1,2,0:T(8,128)S(1)} %fusion.20, f32[1,1,4,128,128]{4,3,2,1,0:T(8,128)S(1)} %copy-done.3, f32[1,1,4,128,128]{4,3,2,1,0:T(8,128)S(1)} %copy-done.9), kind=kOutput, calls=%fused_computation.68 | convolution fusion | flops 50659328 | bytes 1179648 | tf_op jit(solution)/shard_map/nik,nlk->nil/dot_general | solution.py:20
  56.2 0.8 copy.51
  57.0 5.5 %all-to-all-start.2 = ((bf16[4,128,128]{2,0,1:T(4,128)(2,1)}), bf16[4,128,128]{2,0,1:T(4,128)(2,1)S(1)}, u32[]{:S(2)}, u32[]{:S(2)}) async-start(bf16[4,128,128]{2,0,1:T(4,128)(2,1)} %copy.51), calls=%async_computation.2 | async-start | bytes 262144 | tf_op jit(solution)/shard_map/all_to_all | solution.py:112
  62.6 11.3 %while.10 = (s32[]{:T(128)}, f32[8,128,128]{2,1,0:T(8,128)S(1)}, s32[]{:T(128)}) while((s32[]{:T(128)}, f32[8,128,128]{2,1,0:T(8,128)S(1)}, s32[]{:T(128)}) %tuple.27), condition=%wide.region_7.8_spmd, body=%wide.region_6.7_spmd.sunk | while | flops 201719808 | bytes 3670061 | solution.py:35
  62.7 0.7 fusion.60
  67.2 0.7 fusion.60
  71.7 0.7 fusion.60
  73.9 1.4 %all-to-all-done.2 = bf16[4,128,128]{2,0,1:T(4,128)(2,1)S(1)} async-done(((bf16[4,128,128]{2,0,1:T(4,128)(2,1)}), bf16[4,128,128]{2,0,1:T(4,128)(2,1)S(1)}, u32[]{:S(2)}, u32[]{:S(2)}) %all-to-all-start.2) | async-done | bytes 131104 | tf_op jit(solution)/shard_map/all_to_all | solution.py:112
  75.4 0.9 gather_fusion
  76.2 0.7 broadcast_in_dim.5
  77.0 3.4 %all-to-all-start.3 = ((bf16[4,256,128]{2,1,0:T(8,128)(2,1)}), bf16[4,256,128]{2,1,0:T(8,128)(2,1)S(1)}, u32[]{:S(2)}, u32[]{:S(2)}) async-start(bf16[4,256,128]{2,1,0:T(8,128)(2,1)} %broadcast_in_dim.5), calls=%async_computation.3 | async-start | bytes 524288 | tf_op jit(solution)/shard_map/all_to_all | solution.py:116
  80.4 0.9 %slice_bitcast_fusion = (f32[1,1,4,128,128]{4,3,2,1,0:T(8,128)}, f32[1,1,4,128,128]{4,3,2,1,0:T(8,128)}, f32[1,1,4,128,128]{4,3,2,1,0:T(8,128)}) fusion(f32[8,128,128]{2,1,0:T(8,128)S(1)} %get-tuple-element.20, f32[8,128,128]{2,1,0:T(8,128)S(1)} %fusion.5, f32[1,1,4,128,128]{4,3,2,1,0:T(8,128)S(1)} %copy-done.6), kind=kLoop, calls=%fused_computation.40 | loop fusion | flops 262144 | bytes 1835008 | tf_op jit(solution)/shard_map/reshape | solution.py:125
  81.3 5.2 %all-to-all-done.3 = bf16[4,256,128]{2,1,0:T(8,128)(2,1)S(1)} async-done(((bf16[4,256,128]{2,1,0:T(8,128)(2,1)}), bf16[4,256,128]{2,1,0:T(8,128)(2,1)S(1)}, u32[]{:S(2)}, u32[]{:S(2)}) %all-to-all-start.3) | async-done | bytes 262176 | tf_op jit(solution)/shard_map/all_to_all | solution.py:116
  86.4 0.7 copy.85
  (69 shorter events, 14.1 us)
Async XLA Ops:
  0.6 11.8 %all-to-all-start = ((f32[4,256,128]{2,1,0:T(8,128)}), f32[4,256,128]{2,1,0:T(8,128)S(1)}, u32[]{:S(2)}, u32[]{:S(2)}) async-start(f32[4,256,128]{2,1,0:T(8,128)} %bitcast.80), calls=%async_computation | async-start | bytes 1048576 | tf_op jit(solution)/shard_map/all_to_all | solution.py:93
  5.5 0.7 copy-start.10
  14.6 20.6 %copy-start.7 = (f32[1,1,4,128,128]{4,3,2,1,0:T(8,128)S(1)}, f32[1,1,4,128,128]{4,3,2,1,0:T(8,128)}, u32[]{:S(2)}) copy-start(f32[1,1,4,128,128]{4,3,2,1,0:T(8,128)} %param.18) | copy-start | bytes 786436
  14.6 35.8 %all-to-all-start.1 = ((f32[4,128,128]{2,0,1:T(4,128)}), f32[4,128,128]{2,0,1:T(4,128)S(1)}, u32[]{:S(2)}, u32[]{:S(2)}) async-start(f32[4,128,128]{2,0,1:T(4,128)} %copy.42), calls=%async_computation.1 | async-start | bytes 524288 | tf_op jit(solution)/shard_map/all_to_all | solution.py:97
  35.1 1.0 %copy-start.3 = (f32[1,1,4,128,128]{4,3,2,1,0:T(8,128)S(1)}, f32[1,1,4,128,128]{4,3,2,1,0:T(8,128)}, u32[]{:S(2)}) copy-start(f32[1,1,4,128,128]{4,3,2,1,0:T(8,128)} %param.19) | copy-start | bytes 786436
  36.1 14.3 %copy-start.4 = (f32[1,1,4,128,128]{4,3,2,1,0:T(8,128)S(1)}, f32[1,1,4,128,128]{4,3,2,1,0:T(8,128)}, u32[]{:S(2)}) copy-start(f32[1,1,4,128,128]{4,3,2,1,0:T(8,128)} %param.17) | copy-start | bytes 786436
  36.2 14.5 %copy-start.5 = (f32[1,1,4,128,128]{4,3,2,1,0:T(8,128)S(1)}, f32[1,1,4,128,128]{4,3,2,1,0:T(8,128)}, u32[]{:S(2)}) copy-start(f32[1,1,4,128,128]{4,3,2,1,0:T(8,128)} %param.16) | copy-start | bytes 786436
  50.8 0.7 copy-start
  51.2 1.1 %copy-start.1 = (f32[4,128,128]{2,1,0:T(8,128)}, f32[4,128,128]{2,1,0:T(8,128)S(1)}, u32[]{:S(2)}) copy-start(f32[4,128,128]{2,1,0:T(8,128)S(1)} %fusion.2) | copy-start | bytes 786436
  51.5 0.9 %copy-start.8 = (f32[1,1,4,128,128]{4,3,2,1,0:T(8,128)S(1)}, f32[1,1,4,128,128]{4,3,2,1,0:T(8,128)}, u32[]{:S(2)}) copy-start(f32[1,1,4,128,128]{4,3,2,1,0:T(8,128)} %param.14) | copy-start | bytes 786436
  52.5 0.7 copy-start.2
  53.2 0.9 %copy-start.6 = (f32[1,1,4,128,128]{4,3,2,1,0:T(8,128)S(1)}, f32[1,1,4,128,128]{4,3,2,1,0:T(8,128)}, u32[]{:S(2)}) copy-start(f32[1,1,4,128,128]{4,3,2,1,0:T(8,128)} %param.15) | copy-start | bytes 786436
  54.1 0.9 %copy-start.9 = (f32[1,1,4,128,128]{4,3,2,1,0:T(8,128)S(1)}, f32[1,1,4,128,128]{4,3,2,1,0:T(8,128)}, u32[]{:S(2)}) copy-start(f32[1,1,4,128,128]{4,3,2,1,0:T(8,128)} %param.13) | copy-start | bytes 786436
  57.0 18.4 %all-to-all-start.2 = ((bf16[4,128,128]{2,0,1:T(4,128)(2,1)}), bf16[4,128,128]{2,0,1:T(4,128)(2,1)S(1)}, u32[]{:S(2)}, u32[]{:S(2)}) async-start(bf16[4,128,128]{2,0,1:T(4,128)(2,1)} %copy.51), calls=%async_computation.2 | async-start | bytes 262144 | tf_op jit(solution)/shard_map/all_to_all | solution.py:112
  77.0 9.5 %all-to-all-start.3 = ((bf16[4,256,128]{2,1,0:T(8,128)(2,1)}), bf16[4,256,128]{2,1,0:T(8,128)(2,1)S(1)}, u32[]{:S(2)}, u32[]{:S(2)}) async-start(bf16[4,256,128]{2,1,0:T(8,128)(2,1)} %broadcast_in_dim.5), calls=%async_computation.3 | async-start | bytes 524288 | tf_op jit(solution)/shard_map/all_to_all | solution.py:116

commit v5 on v4

--- a/solution.py
+++ b/solution.py
@@ -87,13 +87,14 @@
     tile_count = owner.shape[0]
     per_group = tile_count // groups
     owners = owner.reshape(groups, per_group)
-    place_index = slot_index(owners, shards) * shards + owners
+    place_index = owners * capacity + slot_index(owners, shards)
     own_place = lax.dynamic_index_in_dim(place_index, my_group, 0, keepdims=False)
     parts = grad_parts.reshape(groups, per_group, piece_len)
     summed = jnp.sum(lax.all_to_all(parts, "dp", 0, 0, tiled=True), axis=0)
-    outgoing = jnp.zeros((capacity * shards, piece_len), jnp.float32)
-    outgoing = outgoing.at[own_place].set(summed)
-    outgoing = outgoing.reshape(capacity, shards, piece_len)
+    places = jnp.arange(capacity * shards, dtype=jnp.int32)
+    placing = (places[:, None] == own_place[None, :]).astype(jnp.float32)
+    outgoing = jnp.dot(placing, summed, precision=highest)
+    outgoing = outgoing.reshape(shards, capacity, piece_len).transpose(1, 0, 2)
     incoming = lax.all_to_all(outgoing, "shard", split_axis=1, concat_axis=1, tiled=True)
 
     def as_tiles(array):
@@ -109,10 +110,13 @@
         as_tiles(right_basis),
     )
     weights = master_new.astype(jnp.bfloat16)
-    returned = lax.all_to_all(weights, "shard", split_axis=1, concat_axis=1, tiled=True)
-    returned = returned.reshape(capacity * shards, piece_len)
-    own_rows = returned[own_place]
-    spread = jnp.broadcast_to(own_rows[None], (groups,) + own_rows.shape)
+    weights = weights.transpose(1, 0, 2)
+    returned = lax.all_to_all(weights, "shard", split_axis=0, concat_axis=0, tiled=True)
+    returned = returned.reshape(shards * capacity, piece_len)
+    picking = (own_place[:, None] == places[None, :]).astype(jnp.bfloat16)
+    picking = jnp.broadcast_to(picking[None], (groups,) + picking.shape)
+    spread = jnp.einsum("gtp,pc->gtc", picking, returned, preferred_element_type=jnp.float32)
+    spread = spread.astype(jnp.bfloat16)
     new_params = lax.all_to_all(spread, "dp", 0, 0, tiled=True).reshape(tile_count, piece_len)
     lstat_new, rstat_new, lbasis_new, rbasis_new = soap_bases(
         gradient,

time: 87.7 us -> 85.7 us (0.977)
  local copies, waits for them, and re-layouts: 9.11 us -> 5.61 us
  matrix products: 14.6 us -> 15.5 us
    transpose x0 -> x2, local copies, waits for them, and re-layouts: none -> 1.64 us  [the longest x1 0.87 us: body(): outgoing = outgoing.reshape(shards, capacity, piece_len).transpose(1, 0, 2)]
    dot_general x0 -> x2, matrix products: none -> 1.56 us  [the longest x1 1.14 us: body(): jnp.einsum('gtp,pc->gtc', picking, returned, preferred_element_type=jnp.f...]
    scatter x1 -> x0, local copies, waits for them, and re-layouts: 1.22 us -> none  [body(): outgoing = outgoing.at[own_place].set(summed)]
    unnamed x25 -> x27, local copies, waits for them, and re-layouts: 4.1 us -> 3.42 us
where the time goes in v5:
time: 85.7 us; the launch traced here: 85.2 us
  starting transfers between devices  34.3 us (40%)
  waiting for transfers between devices  25.8 us (30%)
  matrix products  15.5 us (18%)
  local copies, waits for them, and re-layouts  5.61 us (7%)
  other arithmetic  2.7 us (3%)
  between operations  0.91 us (1%)
    all_to_all x1, starting transfers between devices, body(): lax.all_to_all(outgoing, 'shard', split_axis=1, concat_axis=1, tiled=True)  20.5 us
    all_to_all x1, waiting for transfers between devices, body(): lax.all_to_all(outgoing, 'shard', split_axis=1, concat_axis=1, tiled=True)  14 us
    dot_general x27, matrix products, product(): return jnp.einsum(form, left, right, precision=precision)  13.9 us
    all_to_all x1, starting transfers between devices, body(): lax.all_to_all(weights, 'shard', split_axis=0, concat_axis=0, tiled=True)  5.54 us
    all_to_all x1, waiting for transfers between devices, body(): summed = jnp.sum(lax.all_to_all(parts, 'dp', 0, 0, tiled=True), axis=0)  5.19 us
    all_to_all x1, waiting for transfers between devices, body(): lax.all_to_all(spread, 'dp', 0, 0, tiled=True)  5.17 us
    all_to_all x1, starting transfers between devices, body(): summed = jnp.sum(lax.all_to_all(parts, 'dp', 0, 0, tiled=True), axis=0)  4.85 us
    unnamed x27, local copies, waits for them, and re-layouts  3.42 us
  transfers between devices with their start and end apart: 4, of which 4 were waited for; matrix products, arithmetic and copies ran while one was open for 16% of the time, Pallas kernels for 0%

profile of v5, /device:TPU:1, one launch (start us, length us, event | category | flops | bytes accessed | tf_op | source)
XLA Modules:
  0.0 85.2 jit_solution(2418995713662463192)
XLA Ops:
  0.6 4.9 %all-to-all-start = ((f32[4,256,128]{2,1,0:T(8,128)}), f32[4,256,128]{2,1,0:T(8,128)S(1)}, u32[]{:S(2)}, u32[]{:S(2)}) async-start(f32[4,256,128]{2,1,0:T(8,128)} %bitcast.82), calls=%async_computation | async-start | bytes 1048576 | tf_op jit(solution)/shard_map/all_to_all | solution.py:93
  5.7 0.9 %fusion.8 = s32[4,128,2,128]{1,2,3,0:T(2,128)S(1)} fusion(s32[4,2,128]{1,2,0:T(8,128)S(1)} %copy.22), kind=kOutput, calls=%fused_computation.18 | output fusion | flops 16908288 | bytes 528384 | tf_op jit(solution)/shard_map/reduce-window
  7.2 5.2 %all-to-all-done = f32[4,256,128]{2,1,0:T(8,128)S(1)} async-done(((f32[4,256,128]{2,1,0:T(8,128)}), f32[4,256,128]{2,1,0:T(8,128)S(1)}, u32[]{:S(2)}, u32[]{:S(2)}) %all-to-all-start) | async-done | bytes 524320 | tf_op jit(solution)/shard_map/all_to_all | solution.py:93
  12.9 0.9 %copy.25 = f32[4,128,128]{2,0,1:T(4,128)} copy(f32[4,128,128]{2,1,0:T(8,128)S(1)} %convolution_bitcast_fusion) | data formatting | bytes 524288 | tf_op jit(solution)/shard_map/transpose | solution.py:97
  13.8 20.5 %all-to-all-start.1 = ((f32[4,128,128]{2,0,1:T(4,128)}), f32[4,128,128]{2,0,1:T(4,128)S(1)}, u32[]{:S(2)}, u32[]{:S(2)}) async-start(f32[4,128,128]{2,0,1:T(4,128)} %copy.25), calls=%async_computation.1 | async-start | bytes 524288 | tf_op jit(solution)/shard_map/all_to_all | solution.py:98
  34.5 0.8 copy-done.8
  35.6 14.0 %all-to-all-done.1 = f32[4,128,128]{2,0,1:T(4,128)S(1)} async-done(((f32[4,128,128]{2,0,1:T(4,128)}), f32[4,128,128]{2,0,1:T(4,128)S(1)}, u32[]{:S(2)}, u32[]{:S(2)}) %all-to-all-start.1) | async-done | bytes 262176 | tf_op jit(solution)/shard_map/all_to_all | solution.py:98
  50.7 0.8 multiply_reduce_fusion
  54.8 0.8 copy.34
  55.5 5.5 %all-to-all-start.2 = ((bf16[128,4,128]{2,1,0:T(4,128)(2,1)}), bf16[128,4,128]{2,1,0:T(4,128)(2,1)S(1)}, u32[]{:S(2)}, u32[]{:S(2)}) async-start(bf16[128,4,128]{2,1,0:T(4,128)(2,1)} %copy.34), calls=%async_computation.2 | async-start | bytes 262144 | tf_op jit(solution)/shard_map/all_to_all | solution.py:114
  61.2 11.3 %while.10 = (s32[]{:T(128)}, f32[8,128,128]{2,1,0:T(8,128)S(1)}, s32[]{:T(128)}) while((s32[]{:T(128)}, f32[8,128,128]{2,1,0:T(8,128)S(1)}, s32[]{:T(128)}) %tuple.26), condition=%wide.region_6.7_spmd, body=%wide.region_5.6_spmd.sunk | while | flops 201719808 | bytes 3670061 | solution.py:35
  61.2 0.7 fusion.63
  63.5 0.7 fusion.63
  64.6 0.7 fusion.63
  65.8 0.7 fusion.63
  66.9 0.7 fusion.63
  69.1 0.7 fusion.63
  70.3 0.7 fusion.63
  72.5 1.4 %all-to-all-done.2 = bf16[128,4,128]{2,1,0:T(4,128)(2,1)S(1)} async-done(((bf16[128,4,128]{2,1,0:T(4,128)(2,1)}), bf16[128,4,128]{2,1,0:T(4,128)(2,1)S(1)}, u32[]{:S(2)}, u32[]{:S(2)}) %all-to-all-start.2) | async-done | bytes 131104 | tf_op jit(solution)/shard_map/all_to_all | solution.py:114
  73.9 1.1 %convolution_convert_fusion = bf16[4,256,128]{2,1,0:T(8,128)(2,1)} fusion(bf16[512,128,1]{1,0,2:T(8,128)(2,1)S(1)} %bitcast.83, bf16[256,512]{1,0:T(8,128)(2,1)S(1)} %fusion.20), kind=kOutput, calls=%fused_computation.2 | convolution fusion | flops 134348800 | bytes 655360 | tf_op jit(solution)/shard_map/gtp,pc->gtc/dot_general | solution.py:118
  75.1 3.4 %all-to-all-start.3 = ((bf16[4,256,128]{2,1,0:T(8,128)(2,1)}), bf16[4,256,128]{2,1,0:T(8,128)(2,1)S(1)}, u32[]{:S(2)}, u32[]{:S(2)}) async-start(bf16[4,256,128]{2,1,0:T(8,128)(2,1)} %convolution_convert_fusion), calls=%async_computation.3 | async-start | bytes 524288 | tf_op jit(solution)/shard_map/all_to_all | solution.py:120
  78.5 0.9 %slice_bitcast_fusion = (f32[1,1,4,128,128]{4,3,2,1,0:T(8,128)}, f32[1,1,4,128,128]{4,3,2,1,0:T(8,128)}, f32[1,1,4,128,128]{4,3,2,1,0:T(8,128)}) fusion(f32[8,128,128]{2,1,0:T(8,128)S(1)} %get-tuple-element.20, f32[8,128,128]{2,1,0:T(8,128)S(1)} %fusion.5, f32[1,1,4,128,128]{4,3,2,1,0:T(8,128)S(1)} %copy-done.7), kind=kLoop, calls=%fused_computation.44 | loop fusion | flops 262144 | bytes 1835008 | tf_op jit(solution)/shard_map/reshape | solution.py:129
  79.4 5.2 %all-to-all-done.3 = bf16[4,256,128]{2,1,0:T(8,128)(2,1)S(1)} async-done(((bf16[4,256,128]{2,1,0:T(8,128)(2,1)}), bf16[4,256,128]{2,1,0:T(8,128)(2,1)S(1)}, u32[]{:S(2)}, u32[]{:S(2)}) %all-to-all-start.3) | async-done | bytes 262176 | tf_op jit(solution)/shard_map/all_to_all | solution.py:120
  84.5 0.7 copy.67
  (71 shorter events, 12.4 us)
Async XLA Ops:
  0.6 4.9 %copy-start.11 = (s32[1024]{0:T(1024)S(1)}, s32[1024]{0:T(1024)}, u32[]{:S(2)}) copy-start(s32[1024]{0:T(1024)} %param.12) | copy-start | bytes 12292
  0.6 11.8 %all-to-all-start = ((f32[4,256,128]{2,1,0:T(8,128)}), f32[4,256,128]{2,1,0:T(8,128)S(1)}, u32[]{:S(2)}, u32[]{:S(2)}) async-start(f32[4,256,128]{2,1,0:T(8,128)} %bitcast.82), calls=%async_computation | async-start | bytes 1048576 | tf_op jit(solution)/shard_map/all_to_all | solution.py:93
  13.8 20.6 %copy-start.3 = (f32[1,1,4,128,128]{4,3,2,1,0:T(8,128)S(1)}, f32[1,1,4,128,128]{4,3,2,1,0:T(8,128)}, u32[]{:S(2)}) copy-start(f32[1,1,4,128,128]{4,3,2,1,0:T(8,128)} %param.19) | copy-start | bytes 786436
  13.8 35.8 %all-to-all-start.1 = ((f32[4,128,128]{2,0,1:T(4,128)}), f32[4,128,128]{2,0,1:T(4,128)S(1)}, u32[]{:S(2)}, u32[]{:S(2)}) async-start(f32[4,128,128]{2,0,1:T(4,128)} %copy.25), calls=%async_computation.1 | async-start | bytes 524288 | tf_op jit(solution)/shard_map/all_to_all | solution.py:98
  34.3 1.0 %copy-start.8 = (f32[1,1,4,128,128]{4,3,2,1,0:T(8,128)S(1)}, f32[1,1,4,128,128]{4,3,2,1,0:T(8,128)}, u32[]{:S(2)}) copy-start(f32[1,1,4,128,128]{4,3,2,1,0:T(8,128)} %param.18) | copy-start | bytes 786436
  35.4 14.2 %copy-start.5 = (f32[1,1,4,128,128]{4,3,2,1,0:T(8,128)S(1)}, f32[1,1,4,128,128]{4,3,2,1,0:T(8,128)}, u32[]{:S(2)}) copy-start(f32[1,1,4,128,128]{4,3,2,1,0:T(8,128)} %param.17) | copy-start | bytes 786436
  35.5 14.4 %copy-start.6 = (f32[1,1,4,128,128]{4,3,2,1,0:T(8,128)S(1)}, f32[1,1,4,128,128]{4,3,2,1,0:T(8,128)}, u32[]{:S(2)}) copy-start(f32[1,1,4,128,128]{4,3,2,1,0:T(8,128)} %param.16) | copy-start | bytes 786436
  50.0 0.7 copy-start
  50.4 1.1 %copy-start.1 = (f32[4,128,128]{2,1,0:T(8,128)}, f32[4,128,128]{2,1,0:T(8,128)S(1)}, u32[]{:S(2)}) copy-start(f32[4,128,128]{2,1,0:T(8,128)S(1)} %fusion.2) | copy-start | bytes 786436
  50.7 0.9 %copy-start.9 = (f32[1,1,4,128,128]{4,3,2,1,0:T(8,128)S(1)}, f32[1,1,4,128,128]{4,3,2,1,0:T(8,128)}, u32[]{:S(2)}) copy-start(f32[1,1,4,128,128]{4,3,2,1,0:T(8,128)} %param.14) | copy-start | bytes 786436
  51.7 0.7 copy-start.2
  52.4 0.9 %copy-start.7 = (f32[1,1,4,128,128]{4,3,2,1,0:T(8,128)S(1)}, f32[1,1,4,128,128]{4,3,2,1,0:T(8,128)}, u32[]{:S(2)}) copy-start(f32[1,1,4,128,128]{4,3,2,1,0:T(8,128)} %param.15) | copy-start | bytes 786436
  53.4 0.9 %copy-start.10 = (f32[1,1,4,128,128]{4,3,2,1,0:T(8,128)S(1)}, f32[1,1,4,128,128]{4,3,2,1,0:T(8,128)}, u32[]{:S(2)}) copy-start(f32[1,1,4,128,128]{4,3,2,1,0:T(8,128)} %param.13) | copy-start | bytes 786436
  54.7 0.8 copy-start.4
  55.5 18.4 %all-to-all-start.2 = ((bf16[128,4,128]{2,1,0:T(4,128)(2,1)}), bf16[128,4,128]{2,1,0:T(4,128)(2,1)S(1)}, u32[]{:S(2)}, u32[]{:S(2)}) async-start(bf16[128,4,128]{2,1,0:T(4,128)(2,1)} %copy.34), calls=%async_computation.2 | async-start | bytes 262144 | tf_op jit(solution)/shard_map/all_to_all | solution.py:114
  75.1 9.5 %all-to-all-start.3 = ((bf16[4,256,128]{2,1,0:T(8,128)(2,1)}), bf16[4,256,128]{2,1,0:T(8,128)(2,1)S(1)}, u32[]{:S(2)}, u32[]{:S(2)}) async-start(bf16[4,256,128]{2,1,0:T(8,128)(2,1)} %convolution_convert_fusion), calls=%async_computation.3 | async-start | bytes 524288 | tf_op jit(solution)/shard_map/all_to_all | solution.py:120

commit v6 on v5

--- a/solution.py
+++ b/solution.py
@@ -35,23 +35,26 @@
     return lax.fori_loop(0, NS_STEPS, newton_schulz, iterate)
 
 
-def soap_weights(gradient, master, first, second, lbasis, rbasis):
-    count = gradient.shape[0]
+def rotate(lbasis, tiles, rbasis):
+    return product("nik,nkl->nil", product("nji,njk->nik", lbasis, tiles), rbasis)
+
+
+def soap_weights(gradient, first, second, lbasis, rbasis, first_held, master_held):
     first_new = beta_one * first + (1.0 - beta_one) * gradient
-    both = jnp.concatenate([gradient, first_new], axis=0)
-    lboth = jnp.concatenate([lbasis, lbasis], axis=0)
-    rboth = jnp.concatenate([rbasis, rbasis], axis=0)
-    rotated = product("nik,nkl->nil", product("nji,njk->nik", lboth, both), rboth)
-    grad_rot, first_rot = rotated[:count], rotated[count:]
+    grad_rot = rotate(lbasis, gradient, rbasis)
+    first_rot = beta_one * first_held + (1.0 - beta_one) * grad_rot
     second_new = beta_two * second + (1.0 - beta_two) * grad_rot * grad_rot
     normed = first_rot / (jnp.sqrt(second_new) + adam_eps)
     update = product("nik,nlk->nil", product("nij,njk->nik", lbasis, normed), rbasis)
-    master_new = master - learn_rate * (update + weight_decay * master)
+    master_new = master_held - learn_rate * update
     return master_new, first_new, second_new
 
 
-def soap_bases(gradient, lstat, rstat, lbasis, rbasis):
+def soap_bases(gradient, lstat, rstat, lbasis, rbasis, weights):
     count = gradient.shape[0]
+    weights, gradient, lstat, rstat, lbasis, rbasis = lax.optimization_barrier(
+        (weights, gradient, lstat, rstat, lbasis, rbasis)
+    )
     lstat_new = stat_decay * lstat + (1.0 - stat_decay) * product(
         "nik,njk->nij", gradient, gradient
     )
@@ -64,7 +67,7 @@
         jnp.concatenate([lbasis, rbasis], axis=0),
     )
     bases = orthogonal(pending)
-    return lstat_new, rstat_new, bases[:count], bases[count:]
+    return weights, lstat_new, rstat_new, bases[:count], bases[count:]
 
 
 def body(
@@ -101,30 +104,34 @@
         return array.reshape(capacity, block_size, block_size)
 
     gradient = incoming.reshape(capacity, block_size, block_size)
+    first_held = rotate(as_tiles(left_basis), as_tiles(first_moment), as_tiles(right_basis))
+    master_held = as_tiles(master) * (1.0 - learn_rate * weight_decay)
     master_new, first_new, second_new = soap_weights(
         gradient,
-        as_tiles(master),
         as_tiles(first_moment),
         as_tiles(second_moment),
         as_tiles(left_basis),
         as_tiles(right_basis),
+        first_held,
+        master_held,
     )
-    weights = master_new.astype(jnp.bfloat16)
-    weights = weights.transpose(1, 0, 2)
+    weights = master_new.astype(jnp.bfloat16).transpose(1, 0, 2)
+    weights, lstat_new, rstat_new, lbasis_new, rbasis_new = soap_bases(
+        gradient,
+        as_tiles(left_stat),
+        as_tiles(right_stat),
+        as_tiles(left_basis),
+        as_tiles(right_basis),
+        weights,
+    )
     returned = lax.all_to_all(weights, "shard", split_axis=0, concat_axis=0, tiled=True)
     returned = returned.reshape(shards * capacity, piece_len)
+    returned, lbasis_new, rbasis_new = lax.optimization_barrier((returned, lbasis_new, rbasis_new))
     picking = (own_place[:, None] == places[None, :]).astype(jnp.bfloat16)
     picking = jnp.broadcast_to(picking[None], (groups,) + picking.shape)
     spread = jnp.einsum("gtp,pc->gtc", picking, returned, preferred_element_type=jnp.float32)
     spread = spread.astype(jnp.bfloat16)
     new_params = lax.all_to_all(spread, "dp", 0, 0, tiled=True).reshape(tile_count, piece_len)
-    lstat_new, rstat_new, lbasis_new, rbasis_new = soap_bases(
-        gradient,
-        as_tiles(left_stat),
-        as_tiles(right_stat),
-        as_tiles(left_basis),
-        as_tiles(right_basis),
-    )
     results = (master_new, first_new, second_new, lstat_new, rstat_new, lbasis_new, rbasis_new)
     shaped = [item.reshape(1, 1, capacity, block_size, block_size) for item in results]
     return (new_params, *shaped)

time: 85.7 us -> 87 us (1.015)
  local copies, waits for them, and re-layouts: 5.61 us -> 8 us
  waiting for transfers between devices: 25.8 us -> 24.9 us
    unnamed x27 -> x23, local copies, waits for them, and re-layouts: 3.42 us -> 4.98 us
    dot_general x27 -> x29, matrix products: 13.9 us -> 13.8 us  [product(): return jnp.einsum(form, left, right, precision=precision)]
  transfers between devices with their start and end apart: 4 -> 4, of which waited for: 4 -> 4; matrix products, arithmetic and copies ran while one was open for 16% -> 17% of each run, Pallas kernels for 0% -> 0%
where the time goes in v6:
time: 87 us; the launch traced here: 86.5 us
  starting transfers between devices  34.3 us (39%)
  waiting for transfers between devices  24.9 us (29%)
  matrix products  15.4 us (18%)
  local copies, waits for them, and re-layouts  8 us (9%)
  other arithmetic  2.63 us (3%)
  between operations  0.9 us (1%)
    all_to_all x1, starting transfers between devices, body(): lax.all_to_all(outgoing, 'shard', split_axis=1, concat_axis=1, tiled=True)  20.5 us
    all_to_all x1, waiting for transfers between devices, body(): lax.all_to_all(outgoing, 'shard', split_axis=1, concat_axis=1, tiled=True)  13.9 us
    dot_general x29, matrix products, product(): return jnp.einsum(form, left, right, precision=precision)  13.8 us
    all_to_all x1, starting transfers between devices, body(): lax.all_to_all(weights, 'shard', split_axis=0, concat_axis=0, tiled=True)  5.54 us
    all_to_all x1, waiting for transfers between devices, body(): summed = jnp.sum(lax.all_to_all(parts, 'dp', 0, 0, tiled=True), axis=0)  5.19 us
    all_to_all x1, waiting for transfers between devices, body(): lax.all_to_all(spread, 'dp', 0, 0, tiled=True)  5.16 us
    unnamed x23, local copies, waits for them, and re-layouts  4.98 us
    all_to_all x1, starting transfers between devices, body(): summed = jnp.sum(lax.all_to_all(parts, 'dp', 0, 0, tiled=True), axis=0)  4.85 us
  transfers between devices with their start and end apart: 4, of which 4 were waited for; matrix products, arithmetic and copies ran while one was open for 17% of the time, Pallas kernels for 0%

profile of v6, /device:TPU:1, one launch (start us, length us, event | category | flops | bytes accessed | tf_op | source)
XLA Modules:
  0.0 86.5 jit_solution(10561828256006963709)
XLA Ops:
  0.6 4.9 %all-to-all-start = ((f32[4,256,128]{2,1,0:T(8,128)}), f32[4,256,128]{2,1,0:T(8,128)S(1)}, u32[]{:S(2)}, u32[]{:S(2)}) async-start(f32[4,256,128]{2,1,0:T(8,128)} %bitcast.86), calls=%async_computation | async-start | bytes 1048576 | tf_op jit(solution)/shard_map/all_to_all | solution.py:96
  5.7 0.9 fusion.6
  7.2 5.2 %all-to-all-done = f32[4,256,128]{2,1,0:T(8,128)S(1)} async-done(((f32[4,256,128]{2,1,0:T(8,128)}), f32[4,256,128]{2,1,0:T(8,128)S(1)}, u32[]{:S(2)}, u32[]{:S(2)}) %all-to-all-start) | async-done | bytes 524320 | tf_op jit(solution)/shard_map/all_to_all | solution.py:96
  12.9 0.9 %copy.25 = f32[4,128,128]{2,0,1:T(4,128)} copy(f32[4,128,128]{2,1,0:T(8,128)S(1)} %convolution_bitcast_fusion) | data formatting | bytes 524288 | tf_op jit(solution)/shard_map/transpose | solution.py:100
  13.8 20.5 %all-to-all-start.1 = ((f32[4,128,128]{2,0,1:T(4,128)}), f32[4,128,128]{2,0,1:T(4,128)S(1)}, u32[]{:S(2)}, u32[]{:S(2)}) async-start(f32[4,128,128]{2,0,1:T(4,128)} %copy.25), calls=%async_computation.1 | async-start | bytes 524288 | tf_op jit(solution)/shard_map/all_to_all | solution.py:101
  34.5 0.8 copy-done
  35.7 13.9 %all-to-all-done.1 = f32[4,128,128]{2,0,1:T(4,128)S(1)} async-done(((f32[4,128,128]{2,0,1:T(4,128)}), f32[4,128,128]{2,0,1:T(4,128)S(1)}, u32[]{:S(2)}, u32[]{:S(2)}) %all-to-all-start.1) | async-done | bytes 262176 | tf_op jit(solution)/shard_map/all_to_all | solution.py:101
  50.3 0.7 copy-done.9
  51.6 0.7 copy-done.8
  52.7 1.0 %copy-done.6 = f32[1,1,4,128,128]{4,3,2,1,0:T(8,128)S(1)} copy-done((f32[1,1,4,128,128]{4,3,2,1,0:T(8,128)S(1)}, f32[1,1,4,128,128]{4,3,2,1,0:T(8,128)}, u32[]{:S(2)}) %copy-start.6) | copy-done | bytes 262168
  56.1 0.8 copy.30
  56.8 5.5 %all-to-all-start.2 = ((bf16[128,4,128]{2,1,0:T(4,128)(2,1)}), bf16[128,4,128]{2,1,0:T(4,128)(2,1)S(1)}, u32[]{:S(2)}, u32[]{:S(2)}) async-start(bf16[128,4,128]{2,1,0:T(4,128)(2,1)} %copy.30), calls=%async_computation.2 | async-start | bytes 262144 | tf_op jit(solution)/shard_map/all_to_all | solution.py:127
  62.5 11.3 %while.10 = (s32[]{:T(128)}, f32[8,128,128]{2,1,0:T(8,128)S(1)}, s32[]{:T(128)}) while((s32[]{:T(128)}, f32[8,128,128]{2,1,0:T(8,128)S(1)}, s32[]{:T(128)}) %tuple.29), condition=%wide.region_6.7_spmd, body=%wide.region_5.6_spmd.sunk | while | flops 201719808 | bytes 3670061 | solution.py:35
  62.5 0.7 fusion.64
  63.7 0.7 fusion.64
  64.8 0.7 fusion.64
  65.9 0.7 fusion.64
  67.0 0.7 fusion.64
  73.8 0.8 fusion.44
  75.2 1.1 %convolution_convert_fusion = bf16[4,256,128]{2,1,0:T(8,128)(2,1)} fusion(bf16[256,512]{1,0:T(8,128)(2,1)S(1)} %fusion.17, bf16[512,128]{1,0:T(8,128)(2,1)S(1)} %bitcast.91), kind=kOutput, calls=%fused_computation.2 | convolution fusion | flops 134348800 | bytes 655360 | tf_op jit(solution)/shard_map/gtp,pc->gtc/dot_general | solution.py:132
  76.3 3.4 %all-to-all-start.3 = ((bf16[4,256,128]{2,1,0:T(8,128)(2,1)}), bf16[4,256,128]{2,1,0:T(8,128)(2,1)S(1)}, u32[]{:S(2)}, u32[]{:S(2)}) async-start(bf16[4,256,128]{2,1,0:T(8,128)(2,1)} %convolution_convert_fusion), calls=%async_computation.3 | async-start | bytes 524288 | tf_op jit(solution)/shard_map/all_to_all | solution.py:134
  79.8 0.9 %fusion.23 = (f32[1,1,4,128,128]{4,3,2,1,0:T(8,128)}, f32[1,1,4,128,128]{4,3,2,1,0:T(8,128)}) fusion(f32[1,1,4,128,128]{4,3,2,1,0:T(8,128)S(1)} %copy-done.2, f32[4,128,128]{2,0,1:T(4,128)S(1)} %all-to-all-done.1, f32[4,128,128]{2,1,0:T(8,128)S(1)} %fusion.37, f32[1,1,4,128,128]{4,3,2,1,0:T(8,128)S(1)} %copy-done.9), kind=kLoop, calls=%fused_computation.37 | loop fusion | flops 458752 | bytes 1572864 | tf_op jit(solution)/shard_map/reshape | solution.py:136
  80.6 5.2 %all-to-all-done.3 = bf16[4,256,128]{2,1,0:T(8,128)(2,1)S(1)} async-done(((bf16[4,256,128]{2,1,0:T(8,128)(2,1)}), bf16[4,256,128]{2,1,0:T(8,128)(2,1)S(1)}, u32[]{:S(2)}, u32[]{:S(2)}) %all-to-all-start.3) | async-done | bytes 262176 | tf_op jit(solution)/shard_map/all_to_all | solution.py:134
  85.8 0.7 copy.58
  (69 shorter events, 14.1 us)
Async XLA Ops:
  0.6 4.9 %copy-start.10 = (s32[1024]{0:T(1024)S(1)}, s32[1024]{0:T(1024)}, u32[]{:S(2)}) copy-start(s32[1024]{0:T(1024)} %param.12) | copy-start | bytes 12292
  0.6 11.8 %all-to-all-start = ((f32[4,256,128]{2,1,0:T(8,128)}), f32[4,256,128]{2,1,0:T(8,128)S(1)}, u32[]{:S(2)}, u32[]{:S(2)}) async-start(f32[4,256,128]{2,1,0:T(8,128)} %bitcast.86), calls=%async_computation | async-start | bytes 1048576 | tf_op jit(solution)/shard_map/all_to_all | solution.py:96
  13.8 20.7 %copy-start.2 = (f32[1,1,4,128,128]{4,3,2,1,0:T(8,128)S(1)}, f32[1,1,4,128,128]{4,3,2,1,0:T(8,128)}, u32[]{:S(2)}) copy-start(f32[1,1,4,128,128]{4,3,2,1,0:T(8,128)} %param.14) | copy-start | bytes 786436
  13.8 35.8 %all-to-all-start.1 = ((f32[4,128,128]{2,0,1:T(4,128)}), f32[4,128,128]{2,0,1:T(4,128)S(1)}, u32[]{:S(2)}, u32[]{:S(2)}) async-start(f32[4,128,128]{2,0,1:T(4,128)} %copy.25), calls=%async_computation.1 | async-start | bytes 524288 | tf_op jit(solution)/shard_map/all_to_all | solution.py:101
  34.3 1.0 %copy-start = (f32[1,1,4,128,128]{4,3,2,1,0:T(8,128)S(1)}, f32[1,1,4,128,128]{4,3,2,1,0:T(8,128)}, u32[]{:S(2)}) copy-start(f32[1,1,4,128,128]{4,3,2,1,0:T(8,128)} %param.18) | copy-start | bytes 786436
  35.7 14.3 %copy-start.1 = (f32[1,1,4,128,128]{4,3,2,1,0:T(8,128)S(1)}, f32[1,1,4,128,128]{4,3,2,1,0:T(8,128)}, u32[]{:S(2)}) copy-start(f32[1,1,4,128,128]{4,3,2,1,0:T(8,128)} %param.19) | copy-start | bytes 786436
  50.0 1.0 %copy-start.9 = (f32[1,1,4,128,128]{4,3,2,1,0:T(8,128)S(1)}, f32[1,1,4,128,128]{4,3,2,1,0:T(8,128)}, u32[]{:S(2)}) copy-start(f32[1,1,4,128,128]{4,3,2,1,0:T(8,128)} %param.15) | copy-start | bytes 786436
  51.3 1.0 %copy-start.8 = (f32[1,1,4,128,128]{4,3,2,1,0:T(8,128)S(1)}, f32[1,1,4,128,128]{4,3,2,1,0:T(8,128)}, u32[]{:S(2)}) copy-start(f32[1,1,4,128,128]{4,3,2,1,0:T(8,128)} %param.13) | copy-start | bytes 786436
  52.6 1.5 %copy-start.5 = (f32[4,128,128]{2,1,0:T(8,128)}, f32[4,128,128]{2,1,0:T(8,128)S(1)}, u32[]{:S(2)}) copy-start(f32[4,128,128]{2,1,0:T(8,128)S(1)} %fusion.3) | copy-start | bytes 786436
  52.6 1.0 %copy-start.6 = (f32[1,1,4,128,128]{4,3,2,1,0:T(8,128)S(1)}, f32[1,1,4,128,128]{4,3,2,1,0:T(8,128)}, u32[]{:S(2)}) copy-start(f32[1,1,4,128,128]{4,3,2,1,0:T(8,128)} %param.16) | copy-start | bytes 786436
  53.7 0.9 %copy-start.7 = (f32[1,1,4,128,128]{4,3,2,1,0:T(8,128)S(1)}, f32[1,1,4,128,128]{4,3,2,1,0:T(8,128)}, u32[]{:S(2)}) copy-start(f32[1,1,4,128,128]{4,3,2,1,0:T(8,128)} %param.17) | copy-start | bytes 786436
  54.6 0.7 copy-start.3
  55.3 0.7 copy-start.4
  56.8 18.4 %all-to-all-start.2 = ((bf16[128,4,128]{2,1,0:T(4,128)(2,1)}), bf16[128,4,128]{2,1,0:T(4,128)(2,1)S(1)}, u32[]{:S(2)}, u32[]{:S(2)}) async-start(bf16[128,4,128]{2,1,0:T(4,128)(2,1)} %copy.30), calls=%async_computation.2 | async-start | bytes 262144 | tf_op jit(solution)/shard_map/all_to_all | solution.py:127
  76.3 9.5 %all-to-all-start.3 = ((bf16[4,256,128]{2,1,0:T(8,128)(2,1)}), bf16[4,256,128]{2,1,0:T(8,128)(2,1)S(1)}, u32[]{:S(2)}, u32[]{:S(2)}) async-start(bf16[4,256,128]{2,1,0:T(8,128)(2,1)} %convolution_convert_fusion), calls=%async_computation.3 | async-start | bytes 524288 | tf_op jit(solution)/shard_map/all_to_all | solution.py:134

commit v7 on v5

--- a/solution.py
+++ b/solution.py
@@ -50,20 +50,29 @@
     return master_new, first_new, second_new
 
 
-def soap_bases(gradient, lstat, rstat, lbasis, rbasis):
+def soap_bases(gradient, lstat, rstat, lbasis, rbasis, trips):
     count = gradient.shape[0]
-    lstat_new = stat_decay * lstat + (1.0 - stat_decay) * product(
-        "nik,njk->nij", gradient, gradient
+
+    def refresh(carry):
+        lstat_new = stat_decay * lstat + (1.0 - stat_decay) * product(
+            "nik,njk->nij", gradient, gradient
+        )
+        rstat_new = stat_decay * rstat + (1.0 - stat_decay) * product(
+            "nki,nkj->nij", gradient, gradient
+        )
+        pending = product(
+            "nij,njk->nik",
+            jnp.concatenate([lstat_new, rstat_new], axis=0),
+            jnp.concatenate([lbasis, rbasis], axis=0),
+        )
+        return carry[0] + 1, lstat_new, rstat_new, orthogonal(pending)
+
+    empty = jnp.zeros_like(lstat)
+    _, lstat_new, rstat_new, bases = lax.while_loop(
+        lambda carry: carry[0] < trips,
+        refresh,
+        (jnp.int32(0), empty, empty, jnp.concatenate([empty, empty], axis=0)),
     )
-    rstat_new = stat_decay * rstat + (1.0 - stat_decay) * product(
-        "nki,nkj->nij", gradient, gradient
-    )
-    pending = product(
-        "nij,njk->nik",
-        jnp.concatenate([lstat_new, rstat_new], axis=0),
-        jnp.concatenate([lbasis, rbasis], axis=0),
-    )
-    bases = orthogonal(pending)
     return lstat_new, rstat_new, bases[:count], bases[count:]
 
 
@@ -124,6 +133,7 @@
         as_tiles(right_stat),
         as_tiles(left_basis),
         as_tiles(right_basis),
+        1 + jnp.minimum(my_group, 0),
     )
     results = (master_new, first_new, second_new, lstat_new, rstat_new, lbasis_new, rbasis_new)
     shaped = [item.reshape(1, 1, capacity, block_size, block_size) for item in results]

time: 85.7 us -> 88.5 us (1.033)
  local copies, waits for them, and re-layouts: 5.61 us -> 8.77 us
  waiting for transfers between devices: 25.8 us -> 23.8 us
    broadcast_in_dim x0 -> x2, local copies, waits for them, and re-layouts: none -> 1.44 us  [soap_bases(): empty = jnp.zeros_like(lstat)]
    all_to_all x1, waiting for transfers between devices: 1.42 us -> 0.01 us  [body(): lax.all_to_all(weights, 'shard', split_axis=0, concat_axis=0, tiled=True)]
    unnamed x27 -> x25, local copies, waits for them, and re-layouts: 3.42 us -> 3.51 us
  transfers between devices with their start and end apart: 4 -> 4, of which waited for: 4 -> 3; matrix products, arithmetic and copies ran while one was open for 16% -> 21% of each run, Pallas kernels for 0% -> 0%
where the time goes in v7:
time: 88.5 us; the launch traced here: 87.3 us
  starting transfers between devices  34.3 us (39%)
  waiting for transfers between devices  23.8 us (27%)
  matrix products  15.5 us (18%)
  local copies, waits for them, and re-layouts  8.77 us (10%)
  other arithmetic  3.57 us (4%)
  between operations  0.9 us (1%)
    all_to_all x1, starting transfers between devices, body(): lax.all_to_all(outgoing, 'shard', split_axis=1, concat_axis=1, tiled=True)  20.5 us
    all_to_all x1, waiting for transfers between devices, body(): lax.all_to_all(outgoing, 'shard', split_axis=1, concat_axis=1, tiled=True)  14 us
    dot_general x27, matrix products, product(): return jnp.einsum(form, left, right, precision=precision)  13.9 us
    all_to_all x1, starting transfers between devices, body(): lax.all_to_all(weights, 'shard', split_axis=0, concat_axis=0, tiled=True)  5.54 us
    all_to_all x1, waiting for transfers between devices, body(): summed = jnp.sum(lax.all_to_all(parts, 'dp', 0, 0, tiled=True), axis=0)  5.19 us
    all_to_all x1, starting transfers between devices, body(): summed = jnp.sum(lax.all_to_all(parts, 'dp', 0, 0, tiled=True), axis=0)  4.85 us
    all_to_all x1, waiting for transfers between devices, body(): lax.all_to_all(spread, 'dp', 0, 0, tiled=True)  4.61 us
    unnamed x25, local copies, waits for them, and re-layouts  3.51 us
  transfers between devices with their start and end apart: 4, of which 3 were waited for; matrix products, arithmetic and copies ran while one was open for 21% of the time, Pallas kernels for 0%

profile of v7, /device:TPU:1, one launch (start us, length us, event | category | flops | bytes accessed | tf_op | source)
XLA Modules:
  0.0 87.3 jit_solution(2564552631249643916)
XLA Ops:
  0.6 4.9 %all-to-all-start = ((f32[4,256,128]{2,1,0:T(8,128)}), f32[4,256,128]{2,1,0:T(8,128)S(1)}, u32[]{:S(2)}, u32[]{:S(2)}) async-start(f32[4,256,128]{2,1,0:T(8,128)} %bitcast.82), calls=%async_computation | async-start | bytes 1048576 | tf_op jit(solution)/shard_map/all_to_all | solution.py:102
  5.7 0.9 fusion.6
  7.2 5.2 %all-to-all-done = f32[4,256,128]{2,1,0:T(8,128)S(1)} async-done(((f32[4,256,128]{2,1,0:T(8,128)}), f32[4,256,128]{2,1,0:T(8,128)S(1)}, u32[]{:S(2)}, u32[]{:S(2)}) %all-to-all-start) | async-done | bytes 524320 | tf_op jit(solution)/shard_map/all_to_all | solution.py:102
  12.9 0.9 %copy.25 = f32[4,128,128]{2,0,1:T(4,128)} copy(f32[4,128,128]{2,1,0:T(8,128)S(1)} %convolution_bitcast_fusion) | data formatting | bytes 524288 | tf_op jit(solution)/shard_map/transpose | solution.py:106
  13.8 20.5 %all-to-all-start.1 = ((f32[4,128,128]{2,0,1:T(4,128)}), f32[4,128,128]{2,0,1:T(4,128)S(1)}, u32[]{:S(2)}, u32[]{:S(2)}) async-start(f32[4,128,128]{2,0,1:T(4,128)} %copy.25), calls=%async_computation.1 | async-start | bytes 524288 | tf_op jit(solution)/shard_map/all_to_all | solution.py:107
  34.5 0.8 copy-done.8
  35.5 14.0 %all-to-all-done.1 = f32[4,128,128]{2,0,1:T(4,128)S(1)} async-done(((f32[4,128,128]{2,0,1:T(4,128)}), f32[4,128,128]{2,0,1:T(4,128)S(1)}, u32[]{:S(2)}, u32[]{:S(2)}) %all-to-all-start.1) | async-done | bytes 262176 | tf_op jit(solution)/shard_map/all_to_all | solution.py:107
  52.7 0.8 copy.34
  53.5 5.5 %all-to-all-start.2 = ((bf16[128,4,128]{2,1,0:T(4,128)(2,1)}), bf16[128,4,128]{2,1,0:T(4,128)(2,1)S(1)}, u32[]{:S(2)}, u32[]{:S(2)}) async-start(bf16[128,4,128]{2,1,0:T(4,128)(2,1)} %copy.34), calls=%async_computation.2 | async-start | bytes 262144 | tf_op jit(solution)/shard_map/all_to_all | solution.py:123
  60.4 0.8 multiply_reduce_fusion
  61.1 0.8 concatenate.27
  62.0 0.7 broadcast_in_dim.5
  62.7 0.7 broadcast_in_dim.5.clone
  63.4 13.1 %while.36 = (s32[]{:T(128)}, f32[4,128,128]{2,1,0:T(8,128)}, f32[4,128,128]{2,1,0:T(8,128)}, f32[8,128,128]{2,1,0:T(8,128)}, s32[]{:T(128)}, /*index=5*/f32[4,12...) while((s32[]{:T(128)}, f32[4,128,128]{2,1,0:T(8,128)}, ...), condition=%wide.region_8.9_spmd, body=%wide.region_5.0_spmd.sunk | while | flops 202244112 | bytes 8388942 | solution.py:71
  63.4 0.9 multiply_add_fusion.6
  64.4 11.3 %while.37 = (s32[]{:T(128)}, f32[8,128,128]{2,1,0:T(8,128)S(1)}, s32[]{:T(128)}) while((s32[]{:T(128)}, f32[8,128,128]{2,1,0:T(8,128)S(1)}, s32[]{:T(128)}) %tuple.68), condition=%wide.region_7.7_spmd, body=%wide.region_6.6_spmd.sunk | while | flops 201719808 | bytes 3670061 | solution.py:35
  68.9 0.7 fusion.63
  73.5 0.7 fusion.63
  75.7 0.8 copy-done
  76.5 1.1 %convolution_convert_fusion = bf16[4,256,128]{2,1,0:T(8,128)(2,1)} fusion(bf16[512,128,1]{1,0,2:T(8,128)(2,1)S(1)} %bitcast.85, bf16[256,512]{1,0:T(8,128)(2,1)S(1)} %fusion.18), kind=kOutput, calls=%fused_computation.6 | convolution fusion | flops 134348800 | bytes 655360 | tf_op jit(solution)/shard_map/gtp,pc->gtc/dot_general | solution.py:127
  77.7 3.4 %all-to-all-start.3 = ((bf16[4,256,128]{2,1,0:T(8,128)(2,1)}), bf16[4,256,128]{2,1,0:T(8,128)(2,1)S(1)}, u32[]{:S(2)}, u32[]{:S(2)}) async-start(bf16[4,256,128]{2,1,0:T(8,128)(2,1)} %convolution_convert_fusion), calls=%async_computation.3 | async-start | bytes 524288 | tf_op jit(solution)/shard_map/all_to_all | solution.py:129
  81.1 0.9 %slice_bitcast_fusion = (f32[1,1,4,128,128]{4,3,2,1,0:T(8,128)}, f32[1,1,4,128,128]{4,3,2,1,0:T(8,128)}, f32[1,1,4,128,128]{4,3,2,1,0:T(8,128)}) fusion(f32[8,128,128]{2,1,0:T(8,128)S(1)} %copy-done.1, f32[8,128,128]{2,1,0:T(8,128)S(1)} %fusion.3, f32[1,1,4,128,128]{4,3,2,1,0:T(8,128)S(1)} %copy-done.7), kind=kLoop, calls=%fused_computation.44 | loop fusion | flops 262144 | bytes 1835008 | tf_op jit(solution)/shard_map/reshape | solution.py:139
  82.0 4.6 %all-to-all-done.3 = bf16[4,256,128]{2,1,0:T(8,128)(2,1)S(1)} async-done(((bf16[4,256,128]{2,1,0:T(8,128)(2,1)}), bf16[4,256,128]{2,1,0:T(8,128)(2,1)S(1)}, u32[]{:S(2)}, u32[]{:S(2)}) %all-to-all-start.3) | async-done | bytes 262176 | tf_op jit(solution)/shard_map/all_to_all | solution.py:129
  86.6 0.7 copy.82
  (76 shorter events, 15.7 us)
Async XLA Ops:
  0.6 4.9 %copy-start.11 = (s32[1024]{0:T(1024)S(1)}, s32[1024]{0:T(1024)}, u32[]{:S(2)}) copy-start(s32[1024]{0:T(1024)} %param.14) | copy-start | bytes 12292
  0.6 11.8 %all-to-all-start = ((f32[4,256,128]{2,1,0:T(8,128)}), f32[4,256,128]{2,1,0:T(8,128)S(1)}, u32[]{:S(2)}, u32[]{:S(2)}) async-start(f32[4,256,128]{2,1,0:T(8,128)} %bitcast.82), calls=%async_computation | async-start | bytes 1048576 | tf_op jit(solution)/shard_map/all_to_all | solution.py:102
  13.8 20.6 %copy-start.5 = (f32[1,1,4,128,128]{4,3,2,1,0:T(8,128)S(1)}, f32[1,1,4,128,128]{4,3,2,1,0:T(8,128)}, u32[]{:S(2)}) copy-start(f32[1,1,4,128,128]{4,3,2,1,0:T(8,128)} %param.21) | copy-start | bytes 786436
  13.8 35.8 %all-to-all-start.1 = ((f32[4,128,128]{2,0,1:T(4,128)}), f32[4,128,128]{2,0,1:T(4,128)S(1)}, u32[]{:S(2)}, u32[]{:S(2)}) async-start(f32[4,128,128]{2,0,1:T(4,128)} %copy.25), calls=%async_computation.1 | async-start | bytes 524288 | tf_op jit(solution)/shard_map/all_to_all | solution.py:107
  34.3 1.0 %copy-start.8 = (f32[1,1,4,128,128]{4,3,2,1,0:T(8,128)S(1)}, f32[1,1,4,128,128]{4,3,2,1,0:T(8,128)}, u32[]{:S(2)}) copy-start(f32[1,1,4,128,128]{4,3,2,1,0:T(8,128)} %param.20) | copy-start | bytes 786436
  35.4 14.2 %copy-start.9 = (f32[1,1,4,128,128]{4,3,2,1,0:T(8,128)S(1)}, f32[1,1,4,128,128]{4,3,2,1,0:T(8,128)}, u32[]{:S(2)}) copy-start(f32[1,1,4,128,128]{4,3,2,1,0:T(8,128)} %param.16) | copy-start | bytes 786436
  49.6 0.7 copy-start.4
  50.3 0.9 %copy-start.7 = (f32[1,1,4,128,128]{4,3,2,1,0:T(8,128)S(1)}, f32[1,1,4,128,128]{4,3,2,1,0:T(8,128)}, u32[]{:S(2)}) copy-start(f32[1,1,4,128,128]{4,3,2,1,0:T(8,128)} %param.17) | copy-start | bytes 786436
  51.3 0.9 %copy-start.10 = (f32[1,1,4,128,128]{4,3,2,1,0:T(8,128)S(1)}, f32[1,1,4,128,128]{4,3,2,1,0:T(8,128)}, u32[]{:S(2)}) copy-start(f32[1,1,4,128,128]{4,3,2,1,0:T(8,128)} %param.15) | copy-start | bytes 786436
  52.6 0.8 copy-start.6
  52.7 6.3 %copy-start.3 = (f32[1,1,4,128,128]{4,3,2,1,0:T(8,128)S(1)}, f32[1,1,4,128,128]{4,3,2,1,0:T(8,128)}, u32[]{:S(2)}) copy-start(f32[1,1,4,128,128]{4,3,2,1,0:T(8,128)} %param.19) | copy-start | bytes 786436
  53.5 23.1 %all-to-all-start.2 = ((bf16[128,4,128]{2,1,0:T(4,128)(2,1)}), bf16[128,4,128]{2,1,0:T(4,128)(2,1)S(1)}, u32[]{:S(2)}, u32[]{:S(2)}) async-start(bf16[128,4,128]{2,1,0:T(4,128)(2,1)} %copy.34), calls=%async_computation.2 | async-start | bytes 262144 | tf_op jit(solution)/shard_map/all_to_all | solution.py:123
  59.0 1.0 %copy-start.2 = (f32[1,1,4,128,128]{4,3,2,1,0:T(8,128)S(1)}, f32[1,1,4,128,128]{4,3,2,1,0:T(8,128)}, u32[]{:S(2)}) copy-start(f32[1,1,4,128,128]{4,3,2,1,0:T(8,128)} %param.18) | copy-start | bytes 786436
  75.7 0.8 copy-start
  76.5 4.6 %copy-start.1 = (f32[8,128,128]{2,1,0:T(8,128)S(1)}, f32[8,128,128]{2,1,0:T(8,128)}, u32[]{:S(2)}) copy-start(f32[8,128,128]{2,1,0:T(8,128)} %get-tuple-element.219) | copy-start | bytes 1572868
  77.7 8.9 %all-to-all-start.3 = ((bf16[4,256,128]{2,1,0:T(8,128)(2,1)}), bf16[4,256,128]{2,1,0:T(8,128)(2,1)S(1)}, u32[]{:S(2)}, u32[]{:S(2)}) async-start(bf16[4,256,128]{2,1,0:T(8,128)(2,1)} %convolution_convert_fusion), calls=%async_computation.3 | async-start | bytes 524288 | tf_op jit(solution)/shard_map/all_to_all | solution.py:129

commit v8 on v7

--- a/solution.py
+++ b/solution.py
@@ -50,10 +50,10 @@
     return master_new, first_new, second_new
 
 
-def soap_bases(gradient, lstat, rstat, lbasis, rbasis, trips):
+def soap_bases(gradient, lstat, rstat, lbasis, rbasis, taken):
     count = gradient.shape[0]
 
-    def refresh(carry):
+    def refresh(gradient, lstat, rstat, lbasis, rbasis):
         lstat_new = stat_decay * lstat + (1.0 - stat_decay) * product(
             "nik,njk->nij", gradient, gradient
         )
@@ -65,15 +65,13 @@
             jnp.concatenate([lstat_new, rstat_new], axis=0),
             jnp.concatenate([lbasis, rbasis], axis=0),
         )
-        return carry[0] + 1, lstat_new, rstat_new, orthogonal(pending)
+        bases = orthogonal(pending)
+        return lstat_new, rstat_new, bases[:count], bases[count:]
 
-    empty = jnp.zeros_like(lstat)
-    _, lstat_new, rstat_new, bases = lax.while_loop(
-        lambda carry: carry[0] < trips,
-        refresh,
-        (jnp.int32(0), empty, empty, jnp.concatenate([empty, empty], axis=0)),
-    )
-    return lstat_new, rstat_new, bases[:count], bases[count:]
+    def unused(gradient, lstat, rstat, lbasis, rbasis):
+        return lstat, rstat, lbasis, rbasis
+
+    return lax.cond(taken, refresh, unused, gradient, lstat, rstat, lbasis, rbasis)
 
 
 def body(
@@ -133,7 +131,7 @@
         as_tiles(right_stat),
         as_tiles(left_basis),
         as_tiles(right_basis),
-        1 + jnp.minimum(my_group, 0),
+        my_group >= 0,
     )
     results = (master_new, first_new, second_new, lstat_new, rstat_new, lbasis_new, rbasis_new)
     shaped = [item.reshape(1, 1, capacity, block_size, block_size) for item in results]

time: 88.5 us -> 85.3 us (0.964)
  local copies, waits for them, and re-layouts: 8.77 us -> 5.65 us
  waiting for transfers between devices: 23.8 us -> 25.1 us
  other arithmetic: 3.57 us -> 2.56 us
    broadcast_in_dim x2 -> x0, local copies, waits for them, and re-layouts: 1.44 us -> none  [soap_bases(): empty = jnp.zeros_like(lstat)]
    all_to_all x1, waiting for transfers between devices: 14 us -> 15.1 us  [body(): lax.all_to_all(outgoing, 'shard', split_axis=1, concat_axis=1, tiled=True)]
    unnamed x25 -> x29, local copies, waits for them, and re-layouts: 3.51 us -> 3.29 us
  transfers between devices with their start and end apart: 4 -> 4, of which waited for: 3 -> 3; matrix products, arithmetic and copies ran while one was open for 21% -> 18% of each run, Pallas kernels for 0% -> 0%
where the time goes in v8:
time: 85.3 us; the launch traced here: 84.1 us
  starting transfers between devices  34.6 us (41%)
  waiting for transfers between devices  25.1 us (29%)
  matrix products  14.9 us (17%)
  local copies, waits for them, and re-layouts  5.65 us (7%)
  other arithmetic  2.56 us (3%)
  between operations  0.89 us (1%)
    all_to_all x1, starting transfers between devices, body(): lax.all_to_all(outgoing, 'shard', split_axis=1, concat_axis=1, tiled=True)  20.5 us
    all_to_all x1, waiting for transfers between devices, body(): lax.all_to_all(outgoing, 'shard', split_axis=1, concat_axis=1, tiled=True)  15.1 us
    dot_general x27, matrix products, product(): return jnp.einsum(form, left, right, precision=precision)  13.4 us
    all_to_all x1, starting transfers between devices, body(): lax.all_to_all(weights, 'shard', split_axis=0, concat_axis=0, tiled=True)  5.67 us
    all_to_all x1, waiting for transfers between devices, body(): summed = jnp.sum(lax.all_to_all(parts, 'dp', 0, 0, tiled=True), axis=0)  5.19 us
    all_to_all x1, starting transfers between devices, body(): summed = jnp.sum(lax.all_to_all(parts, 'dp', 0, 0, tiled=True), axis=0)  4.97 us
    all_to_all x1, waiting for transfers between devices, body(): lax.all_to_all(spread, 'dp', 0, 0, tiled=True)  4.77 us
    all_to_all x1, starting transfers between devices, body(): lax.all_to_all(spread, 'dp', 0, 0, tiled=True)  3.41 us
  transfers between devices with their start and end apart: 4, of which 3 were waited for; matrix products, arithmetic and copies ran while one was open for 18% of the time, Pallas kernels for 0%

profile of v8, /device:TPU:1, one launch (start us, length us, event | category | flops | bytes accessed | tf_op | source)
XLA Modules:
  0.0 84.1 jit_solution(7377162483670757251)
XLA Ops:
  0.6 1.0 %copy.84 = f32[1,1,4,128,128]{4,3,2,1,0:T(8,128)S(1)} copy(f32[1,1,4,128,128]{4,3,2,1,0:T(8,128)} %param.21) | data formatting | bytes 524288
  1.6 5.0 %all-to-all-start = ((f32[4,256,128]{2,1,0:T(8,128)}), f32[4,256,128]{2,1,0:T(8,128)S(1)}, u32[]{:S(2)}, u32[]{:S(2)}) async-start(f32[4,256,128]{2,1,0:T(8,128)} %bitcast.15), calls=%async_computation | async-start | bytes 1048576 | tf_op jit(solution)/shard_map/all_to_all | solution.py:100
  6.7 0.9 %fusion.15 = s32[4,128,2,128]{1,2,3,0:T(2,128)S(1)} fusion(s32[4,2,128]{1,2,0:T(8,128)S(1)} %copy.31), kind=kOutput, calls=%fused_computation.27 | output fusion | flops 16908288 | bytes 528384 | tf_op jit(solution)/shard_map/reduce-window
  8.3 5.2 %all-to-all-done = f32[4,256,128]{2,1,0:T(8,128)S(1)} async-done(((f32[4,256,128]{2,1,0:T(8,128)}), f32[4,256,128]{2,1,0:T(8,128)S(1)}, u32[]{:S(2)}, u32[]{:S(2)}) %all-to-all-start) | async-done | bytes 524320 | tf_op jit(solution)/shard_map/all_to_all | solution.py:100
  13.9 0.9 %copy.34 = f32[4,128,128]{2,0,1:T(4,128)} copy(f32[4,128,128]{2,1,0:T(8,128)S(1)} %convolution_bitcast_fusion) | data formatting | bytes 524288 | tf_op jit(solution)/shard_map/transpose | solution.py:104
  14.8 20.5 %all-to-all-start.1 = ((f32[4,128,128]{2,0,1:T(4,128)}), f32[4,128,128]{2,0,1:T(4,128)S(1)}, u32[]{:S(2)}, u32[]{:S(2)}) async-start(f32[4,128,128]{2,0,1:T(4,128)} %copy.34), calls=%async_computation.1 | async-start | bytes 524288 | tf_op jit(solution)/shard_map/all_to_all | solution.py:105
  35.5 15.1 %all-to-all-done.1 = f32[4,128,128]{2,0,1:T(4,128)S(1)} async-done(((f32[4,128,128]{2,0,1:T(4,128)}), f32[4,128,128]{2,0,1:T(4,128)S(1)}, u32[]{:S(2)}, u32[]{:S(2)}) %all-to-all-start.1) | async-done | bytes 262176 | tf_op jit(solution)/shard_map/all_to_all | solution.py:105
  53.7 0.8 copy.40
  54.5 5.7 %all-to-all-start.2 = ((bf16[128,4,128]{2,1,0:T(4,128)(2,1)}), bf16[128,4,128]{2,1,0:T(4,128)(2,1)S(1)}, u32[]{:S(2)}, u32[]{:S(2)}) async-start(bf16[128,4,128]{2,1,0:T(4,128)(2,1)} %copy.40), calls=%async_computation.2 | async-start | bytes 262144 | tf_op jit(solution)/shard_map/all_to_all | solution.py:121
  60.3 12.9 %conditional.1 = (f32[1,1,4,128,128]{4,3,2,1,0:T(8,128)S(1)}, f32[1,1,4,128,128]{4,3,2,1,0:T(8,128)S(1)}, f32[1,1,4,128,128]{4,3,2,1,0:T(8,128)S(1)}, f32[1,1,4,128,128]{4,3,2,1,0:T(8,128)S(1)}) conditional(s32[]{:T(128)} %convert_element_type.26, (f32[4,128,128]{2,1,0:T(8,128)S(1)}, f32[4,128,128]{2,1,0:T(8,128)S(1)}, f32[4,128,128]{1,2,0:T(8,128)S(1)}, ...), branch_computations={%region_4.5_spmd, %region_5.9_spmd} | conditional | flops 404094976 | bytes 9437421 | solution.py:74
  61.9 11.3 %while.9 = (s32[]{:T(128)}, f32[8,128,128]{2,1,0:T(8,128)S(1)}, s32[]{:T(128)}) while((s32[]{:T(128)}, f32[8,128,128]{2,1,0:T(8,128)S(1)}, s32[]{:T(128)}) %tuple.67), condition=%wide.region_8.8_spmd, body=%wide.region_7.7_spmd.sunk | while | flops 201719808 | bytes 3670061 | solution.py:35
  62.0 0.7 fusion.70
  63.1 0.7 fusion.70
  64.2 0.7 fusion.70
  65.4 0.7 fusion.70
  66.5 0.7 fusion.70
  67.6 0.7 fusion.70
  68.8 0.7 fusion.70
  72.1 0.7 fusion.70
  73.3 1.1 %convolution_convert_fusion = bf16[4,256,128]{2,1,0:T(8,128)(2,1)} fusion(bf16[512,128,1]{1,0,2:T(8,128)(2,1)S(1)} %bitcast.93, bf16[256,512]{1,0:T(8,128)(2,1)S(1)} %fusion.30), kind=kOutput, calls=%fused_computation.21 | convolution fusion | flops 134348800 | bytes 655360 | tf_op jit(solution)/shard_map/gtp,pc->gtc/dot_general | solution.py:125
  74.5 3.4 %all-to-all-start.3 = ((bf16[4,256,128]{2,1,0:T(8,128)(2,1)}), bf16[4,256,128]{2,1,0:T(8,128)(2,1)S(1)}, u32[]{:S(2)}, u32[]{:S(2)}) async-start(bf16[4,256,128]{2,1,0:T(8,128)(2,1)} %convolution_convert_fusion), calls=%async_computation.3 | async-start | bytes 524288 | tf_op jit(solution)/shard_map/all_to_all | solution.py:127
  77.9 0.7 fusion.42
  78.6 4.8 %all-to-all-done.3 = bf16[4,256,128]{2,1,0:T(8,128)(2,1)S(1)} async-done(((bf16[4,256,128]{2,1,0:T(8,128)(2,1)}), bf16[4,256,128]{2,1,0:T(8,128)(2,1)S(1)}, u32[]{:S(2)}, u32[]{:S(2)}) %all-to-all-start.3) | async-done | bytes 262176 | tf_op jit(solution)/shard_map/all_to_all | solution.py:127
  83.4 0.7 copy.86
  (76 shorter events, 11.8 us)
Async XLA Ops:
  1.6 5.0 %copy-start.12 = (s32[1024]{0:T(1024)S(1)}, s32[1024]{0:T(1024)}, u32[]{:S(2)}) copy-start(s32[1024]{0:T(1024)} %param.14) | copy-start | bytes 12292
  1.6 11.9 %all-to-all-start = ((f32[4,256,128]{2,1,0:T(8,128)}), f32[4,256,128]{2,1,0:T(8,128)S(1)}, u32[]{:S(2)}, u32[]{:S(2)}) async-start(f32[4,256,128]{2,1,0:T(8,128)} %bitcast.15), calls=%async_computation | async-start | bytes 1048576 | tf_op jit(solution)/shard_map/all_to_all | solution.py:100
  14.8 20.6 %copy-start.8 = (f32[1,1,4,128,128]{4,3,2,1,0:T(8,128)S(1)}, f32[1,1,4,128,128]{4,3,2,1,0:T(8,128)}, u32[]{:S(2)}) copy-start(f32[1,1,4,128,128]{4,3,2,1,0:T(8,128)} %param.20) | copy-start | bytes 786436
  14.8 35.8 %all-to-all-start.1 = ((f32[4,128,128]{2,0,1:T(4,128)}), f32[4,128,128]{2,0,1:T(4,128)S(1)}, u32[]{:S(2)}, u32[]{:S(2)}) async-start(f32[4,128,128]{2,0,1:T(4,128)} %copy.34), calls=%async_computation.1 | async-start | bytes 524288 | tf_op jit(solution)/shard_map/all_to_all | solution.py:105
  35.4 15.3 %copy-start.10 = (f32[1,1,4,128,128]{4,3,2,1,0:T(8,128)S(1)}, f32[1,1,4,128,128]{4,3,2,1,0:T(8,128)}, u32[]{:S(2)}) copy-start(f32[1,1,4,128,128]{4,3,2,1,0:T(8,128)} %param.16) | copy-start | bytes 786436
  50.7 0.7 copy-start.5
  51.4 0.9 %copy-start.7 = (f32[1,1,4,128,128]{4,3,2,1,0:T(8,128)S(1)}, f32[1,1,4,128,128]{4,3,2,1,0:T(8,128)}, u32[]{:S(2)}) copy-start(f32[1,1,4,128,128]{4,3,2,1,0:T(8,128)} %param.17) | copy-start | bytes 786436
  52.3 0.9 %copy-start.11 = (f32[1,1,4,128,128]{4,3,2,1,0:T(8,128)S(1)}, f32[1,1,4,128,128]{4,3,2,1,0:T(8,128)}, u32[]{:S(2)}) copy-start(f32[1,1,4,128,128]{4,3,2,1,0:T(8,128)} %param.15) | copy-start | bytes 786436
  53.7 0.8 copy-start.6
  54.5 5.8 %copy-start.2 = (f32[1,1,4,128,128]{4,3,2,1,0:T(8,128)S(1)}, f32[1,1,4,128,128]{4,3,2,1,0:T(8,128)}, u32[]{:S(2)}) copy-start(f32[1,1,4,128,128]{4,3,2,1,0:T(8,128)} %param.18) | copy-start | bytes 786436
  54.5 5.8 %copy-start.4 = (f32[1,1,4,128,128]{4,3,2,1,0:T(8,128)S(1)}, f32[1,1,4,128,128]{4,3,2,1,0:T(8,128)}, u32[]{:S(2)}) copy-start(f32[1,1,4,128,128]{4,3,2,1,0:T(8,128)} %param.19) | copy-start | bytes 786436
  54.5 18.8 %all-to-all-start.2 = ((bf16[128,4,128]{2,1,0:T(4,128)(2,1)}), bf16[128,4,128]{2,1,0:T(4,128)(2,1)S(1)}, u32[]{:S(2)}, u32[]{:S(2)}) async-start(bf16[128,4,128]{2,1,0:T(4,128)(2,1)} %copy.40), calls=%async_computation.2 | async-start | bytes 262144 | tf_op jit(solution)/shard_map/all_to_all | solution.py:121
  73.3 1.2 %copy-start = (f32[1,1,4,128,128]{4,3,2,1,0:T(8,128)}, f32[1,1,4,128,128]{4,3,2,1,0:T(8,128)S(1)}, u32[]{:S(2)}) copy-start(f32[1,1,4,128,128]{4,3,2,1,0:T(8,128)S(1)} %get-tuple-element.166) | copy-start | bytes 786436
  73.3 1.2 %copy-start.1 = (f32[1,1,4,128,128]{4,3,2,1,0:T(8,128)}, f32[1,1,4,128,128]{4,3,2,1,0:T(8,128)S(1)}, u32[]{:S(2)}) copy-start(f32[1,1,4,128,128]{4,3,2,1,0:T(8,128)S(1)} %get-tuple-element.163) | copy-start | bytes 786436
  73.3 1.2 %copy-start.3 = (f32[1,1,4,128,128]{4,3,2,1,0:T(8,128)}, f32[1,1,4,128,128]{4,3,2,1,0:T(8,128)S(1)}, u32[]{:S(2)}) copy-start(f32[1,1,4,128,128]{4,3,2,1,0:T(8,128)S(1)} %get-tuple-element.164) | copy-start | bytes 786436
  73.3 5.3 %copy-start.9 = (f32[1,1,4,128,128]{4,3,2,1,0:T(8,128)}, f32[1,1,4,128,128]{4,3,2,1,0:T(8,128)S(1)}, u32[]{:S(2)}) copy-start(f32[1,1,4,128,128]{4,3,2,1,0:T(8,128)S(1)} %get-tuple-element.165) | copy-start | bytes 786436
  74.5 8.9 %all-to-all-start.3 = ((bf16[4,256,128]{2,1,0:T(8,128)(2,1)}), bf16[4,256,128]{2,1,0:T(8,128)(2,1)S(1)}, u32[]{:S(2)}, u32[]{:S(2)}) async-start(bf16[4,256,128]{2,1,0:T(8,128)(2,1)} %convolution_convert_fusion), calls=%async_computation.3 | async-start | bytes 524288 | tf_op jit(solution)/shard_map/all_to_all | solution.py:127

commit v9 on v8

--- a/solution.py
+++ b/solution.py
@@ -26,13 +26,13 @@
     return jnp.sum(matches * running, axis=-1) - 1
 
 
-def orthogonal(pending):
-    iterate = pending * lax.rsqrt(jnp.sum(pending * pending, axis=(1, 2), keepdims=True) + 1e-06)
-    def newton_schulz(step, iterate):
-        gram = product("nik,njk->nij", iterate, iterate, high)
-        return 1.5 * iterate - 0.5 * product("nij,njk->nik", gram, iterate, high)
+def normalized(pending):
+    return pending * lax.rsqrt(jnp.sum(pending * pending, axis=(1, 2), keepdims=True) + 1e-06)
 
-    return lax.fori_loop(0, NS_STEPS, newton_schulz, iterate)
+
+def newton_schulz(step, iterate):
+    gram = product("nik,njk->nij", iterate, iterate, high)
+    return 1.5 * iterate - 0.5 * product("nij,njk->nik", gram, iterate, high)
 
 
 def soap_weights(gradient, master, first, second, lbasis, rbasis):
@@ -50,9 +50,7 @@
     return master_new, first_new, second_new
 
 
-def soap_bases(gradient, lstat, rstat, lbasis, rbasis, taken):
-    count = gradient.shape[0]
-
+def soap_bases(gradient, lstat, rstat, lbasis, rbasis, taken, early_steps):
     def refresh(gradient, lstat, rstat, lbasis, rbasis):
         lstat_new = stat_decay * lstat + (1.0 - stat_decay) * product(
             "nik,njk->nij", gradient, gradient
@@ -65,13 +63,20 @@
             jnp.concatenate([lstat_new, rstat_new], axis=0),
             jnp.concatenate([lbasis, rbasis], axis=0),
         )
-        bases = orthogonal(pending)
-        return lstat_new, rstat_new, bases[:count], bases[count:]
+        iterate = lax.fori_loop(0, early_steps, newton_schulz, normalized(pending))
+        return lstat_new, rstat_new, iterate
 
     def unused(gradient, lstat, rstat, lbasis, rbasis):
-        return lstat, rstat, lbasis, rbasis
+        return lstat, rstat, jnp.concatenate([lbasis, rbasis], axis=0)
 
     return lax.cond(taken, refresh, unused, gradient, lstat, rstat, lbasis, rbasis)
+
+
+def finish_bases(iterate, taken, early_steps):
+    def rest(iterate):
+        return lax.fori_loop(early_steps, NS_STEPS, newton_schulz, iterate)
+
+    return lax.cond(taken, rest, lambda iterate: iterate, iterate)
 
 
 def body(
@@ -118,21 +123,27 @@
     )
     weights = master_new.astype(jnp.bfloat16)
     weights = weights.transpose(1, 0, 2)
+    taken = my_group >= 0
+    early_steps = NS_STEPS - 2
+    lstat_new, rstat_new, iterate = soap_bases(
+        gradient,
+        as_tiles(left_stat),
+        as_tiles(right_stat),
+        as_tiles(left_basis),
+        as_tiles(right_basis),
+        taken,
+        early_steps,
+    )
     returned = lax.all_to_all(weights, "shard", split_axis=0, concat_axis=0, tiled=True)
     returned = returned.reshape(shards * capacity, piece_len)
+    returned, iterate = lax.optimization_barrier((returned, iterate))
     picking = (own_place[:, None] == places[None, :]).astype(jnp.bfloat16)
     picking = jnp.broadcast_to(picking[None], (groups,) + picking.shape)
     spread = jnp.einsum("gtp,pc->gtc", picking, returned, preferred_element_type=jnp.float32)
     spread = spread.astype(jnp.bfloat16)
     new_params = lax.all_to_all(spread, "dp", 0, 0, tiled=True).reshape(tile_count, piece_len)
-    lstat_new, rstat_new, lbasis_new, rbasis_new = soap_bases(
-        gradient,
-        as_tiles(left_stat),
-        as_tiles(right_stat),
-        as_tiles(left_basis),
-        as_tiles(right_basis),
-        my_group >= 0,
-    )
+    bases = finish_bases(iterate, taken, early_steps)
+    lbasis_new, rbasis_new = bases[:capacity], bases[capacity:]
     results = (master_new, first_new, second_new, lstat_new, rstat_new, lbasis_new, rbasis_new)
     shaped = [item.reshape(1, 1, capacity, block_size, block_size) for item in results]
     return (new_params, *shaped)

time: 85.3 us -> 102 us (1.20)
  matrix products: 14.9 us -> 26.1 us
  local copies, waits for them, and re-layouts: 5.65 us -> 14.6 us
  waiting for transfers between devices: 25.1 us -> 20.3 us
  other arithmetic: 2.56 us -> 4.53 us
    dot_general x27, matrix products: 13.4 us -> 24.5 us  [product(): return jnp.einsum(form, left, right, precision=precision)]
    while x10, local copies, waits for them, and re-layouts: 0.36 us -> 9.92 us
    all_to_all x1, waiting for transfers between devices: 4.77 us -> 0.01 us  [body(): lax.all_to_all(spread, 'dp', 0, 0, tiled=True)]
    reshape x1, other arithmetic: 0.75 us -> 1.92 us  [body(): item.reshape(1, 1, capacity, block_size, block_size)]
    unnamed x29 -> x26, local copies, waits for them, and re-layouts: 3.29 us -> 2.68 us
  transfers between devices with their start and end apart: 4 -> 4, of which waited for: 3 -> 2; matrix products, arithmetic and copies ran while one was open for 18% -> 37% of each run, Pallas kernels for 0% -> 0%
where the time goes in v9:
time: 102 us; the launch traced here: 101 us
  starting transfers between devices  34.5 us (34%)
  matrix products  26.1 us (26%)
  waiting for transfers between devices  20.3 us (20%)
  local copies, waits for them, and re-layouts  14.6 us (14%)
  other arithmetic  4.53 us (4%)
    dot_general x27, matrix products, product(): return jnp.einsum(form, left, right, precision=precision)  24.5 us
    all_to_all x1, starting transfers between devices, body(): lax.all_to_all(outgoing, 'shard', split_axis=1, concat_axis=1, tiled=True)  20.5 us
    all_to_all x1, waiting for transfers between devices, body(): lax.all_to_all(outgoing, 'shard', split_axis=1, concat_axis=1, tiled=True)  15.1 us
    while x10, local copies, waits for them, and re-layouts  9.92 us
    all_to_all x1, starting transfers between devices, body(): lax.all_to_all(weights, 'shard', split_axis=0, concat_axis=0, tiled=True)  5.67 us
    all_to_all x1, waiting for transfers between devices, body(): summed = jnp.sum(lax.all_to_all(parts, 'dp', 0, 0, tiled=True), axis=0)  5.19 us
    all_to_all x1, starting transfers between devices, body(): summed = jnp.sum(lax.all_to_all(parts, 'dp', 0, 0, tiled=True), axis=0)  4.85 us
    all_to_all x1, starting transfers between devices, body(): lax.all_to_all(spread, 'dp', 0, 0, tiled=True)  3.41 us
  transfers between devices with their start and end apart: 4, of which 2 were waited for; matrix products, arithmetic and copies ran while one was open for 37% of the time, Pallas kernels for 0%

profile of v9, /device:TPU:1, one launch (start us, length us, event | category | flops | bytes accessed | tf_op | source)
XLA Modules:
  0.0 100.9 jit_solution(11760260650787861655)
XLA Ops:
  0.6 4.9 %all-to-all-start = ((f32[4,256,128]{2,1,0:T(8,128)}), f32[4,256,128]{2,1,0:T(8,128)S(1)}, u32[]{:S(2)}, u32[]{:S(2)}) async-start(f32[4,256,128]{2,1,0:T(8,128)} %bitcast.7), calls=%async_computation | async-start | bytes 1048576 | tf_op jit(solution)/shard_map/all_to_all | solution.py:105
  7.2 5.2 %all-to-all-done = f32[4,256,128]{2,1,0:T(8,128)S(1)} async-done(((f32[4,256,128]{2,1,0:T(8,128)}), f32[4,256,128]{2,1,0:T(8,128)S(1)}, u32[]{:S(2)}, u32[]{:S(2)}) %all-to-all-start) | async-done | bytes 524320 | tf_op jit(solution)/shard_map/all_to_all | solution.py:105
  13.8 20.5 %all-to-all-start.1 = ((f32[4,128,128]{2,0,1:T(4,128)}), f32[4,128,128]{2,0,1:T(4,128)S(1)}, u32[]{:S(2)}, u32[]{:S(2)}) async-start(f32[4,128,128]{2,0,1:T(4,128)} %copy.34), calls=%async_computation.1 | async-start | bytes 524288 | tf_op jit(solution)/shard_map/all_to_all | solution.py:110
  34.5 15.1 %all-to-all-done.1 = f32[4,128,128]{2,0,1:T(4,128)S(1)} async-done(((f32[4,128,128]{2,0,1:T(4,128)}), f32[4,128,128]{2,0,1:T(4,128)S(1)}, u32[]{:S(2)}, u32[]{:S(2)}) %all-to-all-start.1) | async-done | bytes 262176 | tf_op jit(solution)/shard_map/all_to_all | solution.py:110
  53.8 5.7 %all-to-all-start.2 = ((bf16[128,4,128]{2,1,0:T(4,128)(2,1)}), bf16[128,4,128]{2,1,0:T(4,128)(2,1)S(1)}, u32[]{:S(2)}, u32[]{:S(2)}) async-start(bf16[128,4,128]{2,1,0:T(4,128)(2,1)} %copy.40), calls=%async_computation.2 | async-start | bytes 262144 | tf_op jit(solution)/shard_map/all_to_all | solution.py:137
  59.6 25.6 %conditional.2 = (f32[4,128,128]{2,1,0:T(8,128)S(1)}, f32[4,128,128]{2,1,0:T(8,128)S(1)}, f32[8,128,128]{2,1,0:T(8,128)}) conditional(s32[]{:T(128)} %convert_element_type.26, (f32[4,128,128]{1,2,0:T(8,128)S(1)}, f32[4,128,128]{2,1,0:T(8,128)S(1)}, f32[4,128,128]{2,1,0:T(8,128)S(1)}, f32[4,128,128]{2,1,0:T(8,128)S(1)}) %tuple.95, ...), branch_computations={%region_4.5_spmd, %region_5.9_spmd} | conditional | flops 404094976 | bytes 8388837 | solution.py:72
  62.0 23.2 %while.24 = (s32[]{:T(128)}, f32[8,128,128]{2,1,0:T(8,128)}, s32[]{:T(128)}) while((s32[]{:T(128)}, f32[8,128,128]{2,1,0:T(8,128)}, s32[]{:T(128)}) %tuple.80), condition=%wide.region_8.8_spmd, body=%wide.region_7.7_spmd.sunk | while | flops 201719808 | bytes 3670061 | solution.py:66
  63.7 1.2 %fusion.89 = f32[8,128,128]{2,1,0:T(8,128)} fusion(f32[8,128,128]{2,1,0:T(8,128)S(1)} %fusion.88, f32[8,128,128]{2,1,0:T(8,128)S(1)} %copy.88), kind=kOutput, calls=%fused_computation.2.clone.1 | convolution fusion | flops 101056512 | bytes 1572864 | tf_op jit(solution)/shard_map/cond/branch_1_fun/while/body/eval_jaxpr/nij,njk->nik/dot_general | solution.py:20
  66.6 1.2 %fusion.89 = f32[8,128,128]{2,1,0:T(8,128)} fusion(f32[8,128,128]{2,1,0:T(8,128)S(1)} %fusion.88, f32[8,128,128]{2,1,0:T(8,128)S(1)} %copy.88), kind=kOutput, calls=%fused_computation.2.clone.1 | convolution fusion | flops 101056512 | bytes 1572864 | tf_op jit(solution)/shard_map/cond/branch_1_fun/while/body/eval_jaxpr/nij,njk->nik/dot_general | solution.py:20
  69.5 1.2 %fusion.89 = f32[8,128,128]{2,1,0:T(8,128)} fusion(f32[8,128,128]{2,1,0:T(8,128)S(1)} %fusion.88, f32[8,128,128]{2,1,0:T(8,128)S(1)} %copy.88), kind=kOutput, calls=%fused_computation.2.clone.1 | convolution fusion | flops 101056512 | bytes 1572864 | tf_op jit(solution)/shard_map/cond/branch_1_fun/while/body/eval_jaxpr/nij,njk->nik/dot_general | solution.py:20
  72.4 1.2 %fusion.89 = f32[8,128,128]{2,1,0:T(8,128)} fusion(f32[8,128,128]{2,1,0:T(8,128)S(1)} %fusion.88, f32[8,128,128]{2,1,0:T(8,128)S(1)} %copy.88), kind=kOutput, calls=%fused_computation.2.clone.1 | convolution fusion | flops 101056512 | bytes 1572864 | tf_op jit(solution)/shard_map/cond/branch_1_fun/while/body/eval_jaxpr/nij,njk->nik/dot_general | solution.py:20
  75.3 1.2 %fusion.89 = f32[8,128,128]{2,1,0:T(8,128)} fusion(f32[8,128,128]{2,1,0:T(8,128)S(1)} %fusion.88, f32[8,128,128]{2,1,0:T(8,128)S(1)} %copy.88), kind=kOutput, calls=%fused_computation.2.clone.1 | convolution fusion | flops 101056512 | bytes 1572864 | tf_op jit(solution)/shard_map/cond/branch_1_fun/while/body/eval_jaxpr/nij,njk->nik/dot_general | solution.py:20
  78.2 1.2 %fusion.89 = f32[8,128,128]{2,1,0:T(8,128)} fusion(f32[8,128,128]{2,1,0:T(8,128)S(1)} %fusion.88, f32[8,128,128]{2,1,0:T(8,128)S(1)} %copy.88), kind=kOutput, calls=%fused_computation.2.clone.1 | convolution fusion | flops 101056512 | bytes 1572864 | tf_op jit(solution)/shard_map/cond/branch_1_fun/while/body/eval_jaxpr/nij,njk->nik/dot_general | solution.py:20
  81.1 1.2 %fusion.89 = f32[8,128,128]{2,1,0:T(8,128)} fusion(f32[8,128,128]{2,1,0:T(8,128)S(1)} %fusion.88, f32[8,128,128]{2,1,0:T(8,128)S(1)} %copy.88), kind=kOutput, calls=%fused_computation.2.clone.1 | convolution fusion | flops 101056512 | bytes 1572864 | tf_op jit(solution)/shard_map/cond/branch_1_fun/while/body/eval_jaxpr/nij,njk->nik/dot_general | solution.py:20
  84.0 1.2 %fusion.89 = f32[8,128,128]{2,1,0:T(8,128)} fusion(f32[8,128,128]{2,1,0:T(8,128)S(1)} %fusion.88, f32[8,128,128]{2,1,0:T(8,128)S(1)} %copy.88), kind=kOutput, calls=%fused_computation.2.clone.1 | convolution fusion | flops 101056512 | bytes 1572864 | tf_op jit(solution)/shard_map/cond/branch_1_fun/while/body/eval_jaxpr/nij,njk->nik/dot_general | solution.py:20
  85.2 1.1 %convolution_convert_fusion = bf16[4,256,128]{2,1,0:T(8,128)(2,1)} fusion(bf16[256,512]{1,0:T(8,128)(2,1)S(1)} %fusion.31, bf16[512,128]{1,0:T(8,128)(2,1)S(1)} %bitcast.97), kind=kOutput, calls=%fused_computation.22 | convolution fusion | flops 134348800 | bytes 655360 | tf_op jit(solution)/shard_map/gtp,pc->gtc/dot_general | solution.py:142
  86.3 3.4 %all-to-all-start.3 = ((bf16[4,256,128]{2,1,0:T(8,128)(2,1)}), bf16[4,256,128]{2,1,0:T(8,128)(2,1)S(1)}, u32[]{:S(2)}, u32[]{:S(2)}) async-start(bf16[4,256,128]{2,1,0:T(8,128)(2,1)} %convolution_convert_fusion), calls=%async_computation.3 | async-start | bytes 524288 | tf_op jit(solution)/shard_map/all_to_all | solution.py:144
  89.8 8.6 %conditional.3 = (f32[8,128,128]{2,1,0:T(8,128)}) conditional(s32[]{:T(128)} %convert_element_type.26, f32[8,128,128]{2,1,0:T(8,128)} %get-tuple-element.97, f32[8,128,128]{2,1,0:T(8,128)} %get-tuple-element.97), branch_computations={%region_9.10_spmd, %region_10.0_spmd} | conditional | flops 201719808 | bytes 3670101 | solution.py:79
  89.8 8.5 %while.25 = (s32[]{:T(128)}, f32[8,128,128]{2,1,0:T(8,128)}, s32[]{:T(128)}) while((s32[]{:T(128)}, f32[8,128,128]{2,1,0:T(8,128)}, s32[]{:T(128)}) %tuple.77), condition=%wide.region_12.12_spmd, body=%wide.region_11.11_spmd.sunk | while | flops 201719808 | bytes 3670061 | solution.py:77
  89.8 1.9 %fusion.82 = f32[8,128,128]{2,1,0:T(8,128)S(1)} fusion(f32[8,128,128]{2,1,0:T(8,128)} %get-tuple-element.162), kind=kOutput, calls=%fused_computation.81.clone.1 | convolution fusion | flops 100663296 | bytes 1048576 | tf_op jit(solution)/shard_map/cond/branch_1_fun/while/body/eval_jaxpr/nik,njk->nij/dot_general | solution.py:20
  91.6 1.6 %fusion.83 = f32[8,128,128]{2,1,0:T(8,128)S(1)} fusion(f32[8,128,128]{2,1,0:T(8,128)S(1)} %fusion.82, f32[8,128,128]{2,1,0:T(8,128)} %get-tuple-element.162), kind=kOutput, calls=%fused_computation.21.clone.1 | convolution fusion | flops 101056512 | bytes 1572864 | tf_op jit(solution)/shard_map/cond/branch_1_fun/while/body/eval_jaxpr/nij,njk->nik/dot_general | solution.py:20
  94.0 1.9 %fusion.82 = f32[8,128,128]{2,1,0:T(8,128)S(1)} fusion(f32[8,128,128]{2,1,0:T(8,128)} %get-tuple-element.162), kind=kOutput, calls=%fused_computation.81.clone.1 | convolution fusion | flops 100663296 | bytes 1048576 | tf_op jit(solution)/shard_map/cond/branch_1_fun/while/body/eval_jaxpr/nik,njk->nij/dot_general | solution.py:20
  95.9 1.6 %fusion.83 = f32[8,128,128]{2,1,0:T(8,128)S(1)} fusion(f32[8,128,128]{2,1,0:T(8,128)S(1)} %fusion.82, f32[8,128,128]{2,1,0:T(8,128)} %get-tuple-element.162), kind=kOutput, calls=%fused_computation.21.clone.1 | convolution fusion | flops 101056512 | bytes 1572864 | tf_op jit(solution)/shard_map/cond/branch_1_fun/while/body/eval_jaxpr/nij,njk->nik/dot_general | solution.py:20
  98.3 1.9 %slice_bitcast_fusion = (f32[1,1,4,128,128]{4,3,2,1,0:T(8,128)}, f32[1,1,4,128,128]{4,3,2,1,0:T(8,128)}, f32[1,1,4,128,128]{4,3,2,1,0:T(8,128)}) fusion(f32[8,128,128]{2,1,0:T(8,128)} %get-tuple-element.198, f32[8,128,128]{2,1,0:T(8,128)S(1)} %fusion.24, f32[1,1,4,128,128]{4,3,2,1,0:T(8,128)S(1)} %copy-done.7), kind=kLoop, calls=%fused_computation.50 | loop fusion | flops 262144 | bytes 1835008 | tf_op jit(solution)/shard_map/reshape | solution.py:148
  (74 shorter events, 25.7 us)
Async XLA Ops:
  0.6 4.9 %copy-start.11 = (s32[1024]{0:T(1024)S(1)}, s32[1024]{0:T(1024)}, u32[]{:S(2)}) copy-start(s32[1024]{0:T(1024)} %param.18) | copy-start | bytes 12292
  0.6 11.8 %all-to-all-start = ((f32[4,256,128]{2,1,0:T(8,128)}), f32[4,256,128]{2,1,0:T(8,128)S(1)}, u32[]{:S(2)}, u32[]{:S(2)}) async-start(f32[4,256,128]{2,1,0:T(8,128)} %bitcast.7), calls=%async_computation | async-start | bytes 1048576 | tf_op jit(solution)/shard_map/all_to_all | solution.py:105
  13.8 20.6 %copy-start.8 = (f32[1,1,4,128,128]{4,3,2,1,0:T(8,128)S(1)}, f32[1,1,4,128,128]{4,3,2,1,0:T(8,128)}, u32[]{:S(2)}) copy-start(f32[1,1,4,128,128]{4,3,2,1,0:T(8,128)} %param.24) | copy-start | bytes 786436
  13.8 35.8 %all-to-all-start.1 = ((f32[4,128,128]{2,0,1:T(4,128)}), f32[4,128,128]{2,0,1:T(4,128)S(1)}, u32[]{:S(2)}, u32[]{:S(2)}) async-start(f32[4,128,128]{2,0,1:T(4,128)} %copy.34), calls=%async_computation.1 | async-start | bytes 524288 | tf_op jit(solution)/shard_map/all_to_all | solution.py:110
  34.3 15.3 %copy-start.9 = (f32[1,1,4,128,128]{4,3,2,1,0:T(8,128)S(1)}, f32[1,1,4,128,128]{4,3,2,1,0:T(8,128)}, u32[]{:S(2)}) copy-start(f32[1,1,4,128,128]{4,3,2,1,0:T(8,128)} %param.20) | copy-start | bytes 786436
  49.6 0.7 copy-start.5
  49.6 1.0 %copy-start = (f32[1,1,4,128,128]{4,3,2,1,0:T(8,128)S(1)}, f32[1,1,4,128,128]{4,3,2,1,0:T(8,128)}, u32[]{:S(2)}) copy-start(f32[1,1,4,128,128]{4,3,2,1,0:T(8,128)} %param.25) | copy-start | bytes 786436
  50.7 0.9 copy-start.7
  51.6 0.9 copy-start.10
  53.0 0.8 copy-start.6
  53.8 5.8 %copy-start.2 = (f32[1,1,4,128,128]{4,3,2,1,0:T(8,128)S(1)}, f32[1,1,4,128,128]{4,3,2,1,0:T(8,128)}, u32[]{:S(2)}) copy-start(f32[1,1,4,128,128]{4,3,2,1,0:T(8,128)} %param.22) | copy-start | bytes 786436
  53.8 5.8 %copy-start.4 = (f32[1,1,4,128,128]{4,3,2,1,0:T(8,128)S(1)}, f32[1,1,4,128,128]{4,3,2,1,0:T(8,128)}, u32[]{:S(2)}) copy-start(f32[1,1,4,128,128]{4,3,2,1,0:T(8,128)} %param.23) | copy-start | bytes 786436
  53.8 31.4 %all-to-all-start.2 = ((bf16[128,4,128]{2,1,0:T(4,128)(2,1)}), bf16[128,4,128]{2,1,0:T(4,128)(2,1)S(1)}, u32[]{:S(2)}, u32[]{:S(2)}) async-start(bf16[128,4,128]{2,1,0:T(4,128)(2,1)} %copy.40), calls=%async_computation.2 | async-start | bytes 262144 | tf_op jit(solution)/shard_map/all_to_all | solution.py:137
  85.2 1.2 %copy-start.1 = (f32[4,128,128]{2,1,0:T(8,128)}, f32[4,128,128]{2,1,0:T(8,128)S(1)}, u32[]{:S(2)}) copy-start(f32[4,128,128]{2,1,0:T(8,128)S(1)} %get-tuple-element.95) | copy-start | bytes 786436
  85.2 1.2 %copy-start.3 = (f32[4,128,128]{2,1,0:T(8,128)}, f32[4,128,128]{2,1,0:T(8,128)S(1)}, u32[]{:S(2)}) copy-start(f32[4,128,128]{2,1,0:T(8,128)S(1)} %get-tuple-element.96) | copy-start | bytes 786436
  86.3 13.9 %all-to-all-start.3 = ((bf16[4,256,128]{2,1,0:T(8,128)(2,1)}), bf16[4,256,128]{2,1,0:T(8,128)(2,1)S(1)}, u32[]{:S(2)}, u32[]{:S(2)}) async-start(bf16[4,256,128]{2,1,0:T(8,128)(2,1)} %convolution_convert_fusion), calls=%async_computation.3 | async-start | bytes 524288 | tf_op jit(solution)/shard_map/all_to_all | solution.py:144

commit v10 on v8

--- a/solution.py
+++ b/solution.py
@@ -32,7 +32,9 @@
         gram = product("nik,njk->nij", iterate, iterate, high)
         return 1.5 * iterate - 0.5 * product("nij,njk->nik", gram, iterate, high)
 
-    return lax.fori_loop(0, NS_STEPS, newton_schulz, iterate)
+    for step in range(NS_STEPS):
+        iterate = newton_schulz(step, iterate)
+    return iterate
 
 
 def soap_weights(gradient, master, first, second, lbasis, rbasis):

time: 85.3 us -> 84.7 us (level)
  transfers between devices with their start and end apart: 4 -> 4, of which waited for: 3 -> 4; matrix products, arithmetic and copies ran while one was open for 18% -> 18% of each run, Pallas kernels for 0% -> 0%
where the time goes in v10:
time: 84.7 us; the launch traced here: 83.8 us
  starting transfers between devices  34.6 us (41%)
  waiting for transfers between devices  25.3 us (30%)
  matrix products  15.1 us (18%)
  local copies, waits for them, and re-layouts  5.29 us (6%)
  other arithmetic  2.45 us (3%)
  between operations  0.89 us (1%)
    all_to_all x1, starting transfers between devices, body(): lax.all_to_all(outgoing, 'shard', split_axis=1, concat_axis=1, tiled=True)  20.5 us
    all_to_all x1, waiting for transfers between devices, body(): lax.all_to_all(outgoing, 'shard', split_axis=1, concat_axis=1, tiled=True)  15.1 us
    dot_general x27, matrix products, product(): return jnp.einsum(form, left, right, precision=precision)  13.5 us
    all_to_all x1, starting transfers between devices, body(): lax.all_to_all(weights, 'shard', split_axis=0, concat_axis=0, tiled=True)  5.68 us
    all_to_all x1, waiting for transfers between devices, body(): summed = jnp.sum(lax.all_to_all(parts, 'dp', 0, 0, tiled=True), axis=0)  5.19 us
    all_to_all x1, starting transfers between devices, body(): summed = jnp.sum(lax.all_to_all(parts, 'dp', 0, 0, tiled=True), axis=0)  4.97 us
    all_to_all x1, waiting for transfers between devices, body(): lax.all_to_all(spread, 'dp', 0, 0, tiled=True)  4.77 us
    all_to_all x1, starting transfers between devices, body(): lax.all_to_all(spread, 'dp', 0, 0, tiled=True)  3.41 us
  transfers between devices with their start and end apart: 4, of which 4 were waited for; matrix products, arithmetic and copies ran while one was open for 18% of the time, Pallas kernels for 0%

profile of v10, /device:TPU:1, one launch (start us, length us, event | category | flops | bytes accessed | tf_op | source)
XLA Modules:
  0.0 83.8 jit_solution(3781751236698223690)
XLA Ops:
  0.6 1.0 %copy.75 = f32[1,1,4,128,128]{4,3,2,1,0:T(8,128)S(1)} copy(f32[1,1,4,128,128]{4,3,2,1,0:T(8,128)} %param.19) | data formatting | bytes 524288
  1.6 5.0 %all-to-all-start = ((f32[4,256,128]{2,1,0:T(8,128)}), f32[4,256,128]{2,1,0:T(8,128)S(1)}, u32[]{:S(2)}, u32[]{:S(2)}) async-start(f32[4,256,128]{2,1,0:T(8,128)} %bitcast.15), calls=%async_computation | async-start | bytes 1048576 | tf_op jit(solution)/shard_map/all_to_all | solution.py:102
  6.7 0.9 %fusion.29 = s32[4,128,2,128]{1,2,3,0:T(2,128)S(1)} fusion(s32[4,2,128]{1,2,0:T(8,128)S(1)} %copy.31), kind=kOutput, calls=%fused_computation.49 | output fusion | flops 16908288 | bytes 528384 | tf_op jit(solution)/shard_map/reduce-window
  8.3 5.2 %all-to-all-done = f32[4,256,128]{2,1,0:T(8,128)S(1)} async-done(((f32[4,256,128]{2,1,0:T(8,128)}), f32[4,256,128]{2,1,0:T(8,128)S(1)}, u32[]{:S(2)}, u32[]{:S(2)}) %all-to-all-start) | async-done | bytes 524320 | tf_op jit(solution)/shard_map/all_to_all | solution.py:102
  13.9 0.9 %copy.34 = f32[4,128,128]{2,0,1:T(4,128)} copy(f32[4,128,128]{2,1,0:T(8,128)S(1)} %convolution_bitcast_fusion) | data formatting | bytes 524288 | tf_op jit(solution)/shard_map/transpose | solution.py:106
  14.8 20.5 %all-to-all-start.1 = ((f32[4,128,128]{2,0,1:T(4,128)}), f32[4,128,128]{2,0,1:T(4,128)S(1)}, u32[]{:S(2)}, u32[]{:S(2)}) async-start(f32[4,128,128]{2,0,1:T(4,128)} %copy.34), calls=%async_computation.1 | async-start | bytes 524288 | tf_op jit(solution)/shard_map/all_to_all | solution.py:107
  35.5 15.1 %all-to-all-done.1 = f32[4,128,128]{2,0,1:T(4,128)S(1)} async-done(((f32[4,128,128]{2,0,1:T(4,128)}), f32[4,128,128]{2,0,1:T(4,128)S(1)}, u32[]{:S(2)}, u32[]{:S(2)}) %all-to-all-start.1) | async-done | bytes 262176 | tf_op jit(solution)/shard_map/all_to_all | solution.py:107
  53.7 0.8 copy.40
  54.5 5.7 %all-to-all-start.2 = ((bf16[128,4,128]{2,1,0:T(4,128)(2,1)}), bf16[128,4,128]{2,1,0:T(4,128)(2,1)S(1)}, u32[]{:S(2)}, u32[]{:S(2)}) async-start(bf16[128,4,128]{2,1,0:T(4,128)(2,1)} %copy.40), calls=%async_computation.2 | async-start | bytes 262144 | tf_op jit(solution)/shard_map/all_to_all | solution.py:123
  60.3 12.4 %conditional.1 = (f32[1,1,4,128,128]{4,3,2,1,0:T(8,128)S(1)}, f32[1,1,4,128,128]{4,3,2,1,0:T(8,128)S(1)}, f32[1,1,4,128,128]{4,3,2,1,0:T(8,128)S(1)}, f32[1,1,4,128,128]{4,3,2,1,0:T(8,128)S(1)}) conditional(s32[]{:T(128)} %convert_element_type.26, (f32[4,128,128]{2,1,0:T(8,128)S(1)}, f32[4,128,128]{2,1,0:T(8,128)S(1)}, f32[4,128,128]{1,2,0:T(8,128)S(1)}, ...), branch_computations={%region_4.5_spmd, %region_5.7_spmd} | conditional | flops 2219835392 | bytes 30933184 | solution.py:76
  61.8 0.8 fusion.19
  63.0 0.7 fusion.66
  65.2 0.7 fusion.68
  66.2 0.7 fusion.69
  67.3 0.7 fusion.70
  68.4 0.7 fusion.71
  69.5 0.7 fusion.72
  70.5 0.7 fusion.73
  71.6 0.7 fusion.74
  73.0 1.1 %convolution_convert_fusion = bf16[4,256,128]{2,1,0:T(8,128)(2,1)} fusion(bf16[512,128,1]{1,0,2:T(8,128)(2,1)S(1)} %bitcast.118, bf16[256,512]{1,0:T(8,128)(2,1)S(1)} %fusion.44), kind=kOutput, calls=%fused_computation.43 | convolution fusion | flops 134348800 | bytes 655360 | tf_op jit(solution)/shard_map/gtp,pc->gtc/dot_general | solution.py:127
  74.2 3.4 %all-to-all-start.3 = ((bf16[4,256,128]{2,1,0:T(8,128)(2,1)}), bf16[4,256,128]{2,1,0:T(8,128)(2,1)S(1)}, u32[]{:S(2)}, u32[]{:S(2)}) async-start(bf16[4,256,128]{2,1,0:T(8,128)(2,1)} %convolution_convert_fusion), calls=%async_computation.3 | async-start | bytes 524288 | tf_op jit(solution)/shard_map/all_to_all | solution.py:129
  77.6 0.7 fusion.56
  78.4 4.8 %all-to-all-done.3 = bf16[4,256,128]{2,1,0:T(8,128)(2,1)S(1)} async-done(((bf16[4,256,128]{2,1,0:T(8,128)(2,1)}), bf16[4,256,128]{2,1,0:T(8,128)(2,1)S(1)}, u32[]{:S(2)}, u32[]{:S(2)}) %all-to-all-start.3) | async-done | bytes 262176 | tf_op jit(solution)/shard_map/all_to_all | solution.py:129
  83.1 0.7 copy.76
  (64 shorter events, 11.0 us)
Async XLA Ops:
  1.6 5.0 %copy-start.12 = (s32[1024]{0:T(1024)S(1)}, s32[1024]{0:T(1024)}, u32[]{:S(2)}) copy-start(s32[1024]{0:T(1024)} %param.12) | copy-start | bytes 12292
  1.6 11.9 %all-to-all-start = ((f32[4,256,128]{2,1,0:T(8,128)}), f32[4,256,128]{2,1,0:T(8,128)S(1)}, u32[]{:S(2)}, u32[]{:S(2)}) async-start(f32[4,256,128]{2,1,0:T(8,128)} %bitcast.15), calls=%async_computation | async-start | bytes 1048576 | tf_op jit(solution)/shard_map/all_to_all | solution.py:102
  14.8 20.6 %copy-start.8 = (f32[1,1,4,128,128]{4,3,2,1,0:T(8,128)S(1)}, f32[1,1,4,128,128]{4,3,2,1,0:T(8,128)}, u32[]{:S(2)}) copy-start(f32[1,1,4,128,128]{4,3,2,1,0:T(8,128)} %param.18) | copy-start | bytes 786436
  14.8 35.8 %all-to-all-start.1 = ((f32[4,128,128]{2,0,1:T(4,128)}), f32[4,128,128]{2,0,1:T(4,128)S(1)}, u32[]{:S(2)}, u32[]{:S(2)}) async-start(f32[4,128,128]{2,0,1:T(4,128)} %copy.34), calls=%async_computation.1 | async-start | bytes 524288 | tf_op jit(solution)/shard_map/all_to_all | solution.py:107
  35.4 15.3 %copy-start.10 = (f32[1,1,4,128,128]{4,3,2,1,0:T(8,128)S(1)}, f32[1,1,4,128,128]{4,3,2,1,0:T(8,128)}, u32[]{:S(2)}) copy-start(f32[1,1,4,128,128]{4,3,2,1,0:T(8,128)} %param.14) | copy-start | bytes 786436
  50.7 0.7 copy-start.5
  51.4 0.9 %copy-start.7 = (f32[1,1,4,128,128]{4,3,2,1,0:T(8,128)S(1)}, f32[1,1,4,128,128]{4,3,2,1,0:T(8,128)}, u32[]{:S(2)}) copy-start(f32[1,1,4,128,128]{4,3,2,1,0:T(8,128)} %param.15) | copy-start | bytes 786436
  52.3 0.9 %copy-start.11 = (f32[1,1,4,128,128]{4,3,2,1,0:T(8,128)S(1)}, f32[1,1,4,128,128]{4,3,2,1,0:T(8,128)}, u32[]{:S(2)}) copy-start(f32[1,1,4,128,128]{4,3,2,1,0:T(8,128)} %param.13) | copy-start | bytes 786436
  53.7 0.8 copy-start.6
  54.5 5.8 %copy-start.2 = (f32[1,1,4,128,128]{4,3,2,1,0:T(8,128)S(1)}, f32[1,1,4,128,128]{4,3,2,1,0:T(8,128)}, u32[]{:S(2)}) copy-start(f32[1,1,4,128,128]{4,3,2,1,0:T(8,128)} %param.16) | copy-start | bytes 786436
  54.5 5.8 %copy-start.4 = (f32[1,1,4,128,128]{4,3,2,1,0:T(8,128)S(1)}, f32[1,1,4,128,128]{4,3,2,1,0:T(8,128)}, u32[]{:S(2)}) copy-start(f32[1,1,4,128,128]{4,3,2,1,0:T(8,128)} %param.17) | copy-start | bytes 786436
  54.5 18.5 %all-to-all-start.2 = ((bf16[128,4,128]{2,1,0:T(4,128)(2,1)}), bf16[128,4,128]{2,1,0:T(4,128)(2,1)S(1)}, u32[]{:S(2)}, u32[]{:S(2)}) async-start(bf16[128,4,128]{2,1,0:T(4,128)(2,1)} %copy.40), calls=%async_computation.2 | async-start | bytes 262144 | tf_op jit(solution)/shard_map/all_to_all | solution.py:123
  72.7 1.5 %copy-start = (f32[1,1,4,128,128]{4,3,2,1,0:T(8,128)}, f32[1,1,4,128,128]{4,3,2,1,0:T(8,128)S(1)}, u32[]{:S(2)}) copy-start(f32[1,1,4,128,128]{4,3,2,1,0:T(8,128)S(1)} %get-tuple-element.128) | copy-start | bytes 786436
  72.7 1.4 %copy-start.1 = (f32[1,1,4,128,128]{4,3,2,1,0:T(8,128)}, f32[1,1,4,128,128]{4,3,2,1,0:T(8,128)S(1)}, u32[]{:S(2)}) copy-start(f32[1,1,4,128,128]{4,3,2,1,0:T(8,128)S(1)} %get-tuple-element.125) | copy-start | bytes 786436
  72.7 1.4 %copy-start.3 = (f32[1,1,4,128,128]{4,3,2,1,0:T(8,128)}, f32[1,1,4,128,128]{4,3,2,1,0:T(8,128)S(1)}, u32[]{:S(2)}) copy-start(f32[1,1,4,128,128]{4,3,2,1,0:T(8,128)S(1)} %get-tuple-element.126) | copy-start | bytes 786436
  72.8 5.6 %copy-start.9 = (f32[1,1,4,128,128]{4,3,2,1,0:T(8,128)}, f32[1,1,4,128,128]{4,3,2,1,0:T(8,128)S(1)}, u32[]{:S(2)}) copy-start(f32[1,1,4,128,128]{4,3,2,1,0:T(8,128)S(1)} %get-tuple-element.127) | copy-start | bytes 786436
  74.2 8.9 %all-to-all-start.3 = ((bf16[4,256,128]{2,1,0:T(8,128)(2,1)}), bf16[4,256,128]{2,1,0:T(8,128)(2,1)S(1)}, u32[]{:S(2)}, u32[]{:S(2)}) async-start(bf16[4,256,128]{2,1,0:T(8,128)(2,1)} %convolution_convert_fusion), calls=%async_computation.3 | async-start | bytes 524288 | tf_op jit(solution)/shard_map/all_to_all | solution.py:129

commit v11 on v10

--- a/solution.py
+++ b/solution.py
@@ -29,8 +29,8 @@
 def orthogonal(pending):
     iterate = pending * lax.rsqrt(jnp.sum(pending * pending, axis=(1, 2), keepdims=True) + 1e-06)
     def newton_schulz(step, iterate):
-        gram = product("nik,njk->nij", iterate, iterate, high)
-        return 1.5 * iterate - 0.5 * product("nij,njk->nik", gram, iterate, high)
+        gram = product("nki,nkj->nij", iterate, iterate, high)
+        return 1.5 * iterate - 0.5 * product("nij,njk->nik", iterate, gram, high)
 
     for step in range(NS_STEPS):
         iterate = newton_schulz(step, iterate)

time: 84.7 us -> 84.8 us (level)
  waiting for transfers between devices: 25.3 us -> 26.7 us
  transfers between devices with their start and end apart: 4 -> 4, of which waited for: 4 -> 4; matrix products, arithmetic and copies ran while one was open for 18% -> 17% of each run, Pallas kernels for 0% -> 0%
where the time goes in v11:
time: 84.8 us; the launch traced here: 84.4 us
  starting transfers between devices  34.6 us (41%)
  waiting for transfers between devices  26.7 us (31%)
  matrix products  14.3 us (17%)
  local copies, waits for them, and re-layouts  5.29 us (6%)
  other arithmetic  2.45 us (3%)
  between operations  0.89 us (1%)
    all_to_all x1, starting transfers between devices, body(): lax.all_to_all(outgoing, 'shard', split_axis=1, concat_axis=1, tiled=True)  20.5 us
    all_to_all x1, waiting for transfers between devices, body(): lax.all_to_all(outgoing, 'shard', split_axis=1, concat_axis=1, tiled=True)  15.1 us
    dot_general x27, matrix products, product(): return jnp.einsum(form, left, right, precision=precision)  12.8 us
    all_to_all x1, starting transfers between devices, body(): lax.all_to_all(weights, 'shard', split_axis=0, concat_axis=0, tiled=True)  5.68 us
    all_to_all x1, waiting for transfers between devices, body(): lax.all_to_all(spread, 'dp', 0, 0, tiled=True)  5.31 us
    all_to_all x1, waiting for transfers between devices, body(): summed = jnp.sum(lax.all_to_all(parts, 'dp', 0, 0, tiled=True), axis=0)  5.19 us
    all_to_all x1, starting transfers between devices, body(): summed = jnp.sum(lax.all_to_all(parts, 'dp', 0, 0, tiled=True), axis=0)  4.97 us
    all_to_all x1, starting transfers between devices, body(): lax.all_to_all(spread, 'dp', 0, 0, tiled=True)  3.41 us
  transfers between devices with their start and end apart: 4, of which 4 were waited for; matrix products, arithmetic and copies ran while one was open for 17% of the time, Pallas kernels for 0%

profile of v11, /device:TPU:1, one launch (start us, length us, event | category | flops | bytes accessed | tf_op | source)
XLA Modules:
  0.0 84.4 jit_solution(5794456724286055945)
XLA Ops:
  0.6 1.0 %copy.95 = f32[1,1,4,128,128]{4,3,2,1,0:T(8,128)S(1)} copy(f32[1,1,4,128,128]{4,3,2,1,0:T(8,128)} %param.19) | data formatting | bytes 524288
  1.6 5.0 %all-to-all-start = ((f32[4,256,128]{2,1,0:T(8,128)}), f32[4,256,128]{2,1,0:T(8,128)S(1)}, u32[]{:S(2)}, u32[]{:S(2)}) async-start(f32[4,256,128]{2,1,0:T(8,128)} %bitcast.15), calls=%async_computation | async-start | bytes 1048576 | tf_op jit(solution)/shard_map/all_to_all | solution.py:102
  6.7 0.9 %fusion.29 = s32[4,128,2,128]{1,2,3,0:T(2,128)S(1)} fusion(s32[4,2,128]{1,2,0:T(8,128)S(1)} %copy.41), kind=kOutput, calls=%fused_computation.49 | output fusion | flops 16908288 | bytes 528384 | tf_op jit(solution)/shard_map/reduce-window
  8.3 5.2 %all-to-all-done = f32[4,256,128]{2,1,0:T(8,128)S(1)} async-done(((f32[4,256,128]{2,1,0:T(8,128)}), f32[4,256,128]{2,1,0:T(8,128)S(1)}, u32[]{:S(2)}, u32[]{:S(2)}) %all-to-all-start) | async-done | bytes 524320 | tf_op jit(solution)/shard_map/all_to_all | solution.py:102
  13.9 0.9 %copy.44 = f32[4,128,128]{2,0,1:T(4,128)} copy(f32[4,128,128]{2,1,0:T(8,128)S(1)} %convolution_bitcast_fusion) | data formatting | bytes 524288 | tf_op jit(solution)/shard_map/transpose | solution.py:106
  14.8 20.5 %all-to-all-start.1 = ((f32[4,128,128]{2,0,1:T(4,128)}), f32[4,128,128]{2,0,1:T(4,128)S(1)}, u32[]{:S(2)}, u32[]{:S(2)}) async-start(f32[4,128,128]{2,0,1:T(4,128)} %copy.44), calls=%async_computation.1 | async-start | bytes 524288 | tf_op jit(solution)/shard_map/all_to_all | solution.py:107
  35.5 15.1 %all-to-all-done.1 = f32[4,128,128]{2,0,1:T(4,128)S(1)} async-done(((f32[4,128,128]{2,0,1:T(4,128)}), f32[4,128,128]{2,0,1:T(4,128)S(1)}, u32[]{:S(2)}, u32[]{:S(2)}) %all-to-all-start.1) | async-done | bytes 262176 | tf_op jit(solution)/shard_map/all_to_all | solution.py:107
  53.7 0.8 copy.50
  54.5 5.7 %all-to-all-start.2 = ((bf16[128,4,128]{2,1,0:T(4,128)(2,1)}), bf16[128,4,128]{2,1,0:T(4,128)(2,1)S(1)}, u32[]{:S(2)}, u32[]{:S(2)}) async-start(bf16[128,4,128]{2,1,0:T(4,128)(2,1)} %copy.50), calls=%async_computation.2 | async-start | bytes 262144 | tf_op jit(solution)/shard_map/all_to_all | solution.py:123
  60.3 11.6 %conditional.1 = (f32[1,1,4,128,128]{4,3,2,1,0:T(8,128)S(1)}, f32[1,1,4,128,128]{4,3,2,1,0:T(8,128)S(1)}, f32[1,1,4,128,128]{4,3,2,1,0:T(8,128)S(1)}, f32[1,1,4,128,128]{4,3,2,1,0:T(8,128)S(1)}) conditional(s32[]{:T(128)} %convert_element_type.26, (f32[4,128,128]{2,1,0:T(8,128)S(1)}, f32[4,128,128]{2,1,0:T(8,128)S(1)}, f32[4,128,128]{1,2,0:T(8,128)S(1)}, ...), branch_computations={%region_4.5_spmd, %region_5.7_spmd} | conditional | flops 2219835392 | bytes 30933184 | solution.py:76
  61.8 0.7 fusion.19
  62.9 0.6 fusion.66
  63.9 0.6 fusion.67
  64.9 0.6 fusion.68
  65.9 0.6 fusion.69
  66.9 0.6 fusion.70
  67.9 0.6 fusion.71
  68.9 0.6 fusion.72
  72.0 1.1 %all-to-all-done.2 = bf16[128,4,128]{2,1,0:T(4,128)(2,1)S(1)} async-done(((bf16[128,4,128]{2,1,0:T(4,128)(2,1)}), bf16[128,4,128]{2,1,0:T(4,128)(2,1)S(1)}, u32[]{:S(2)}, u32[]{:S(2)}) %all-to-all-start.2) | async-done | bytes 131104 | tf_op jit(solution)/shard_map/all_to_all | solution.py:123
  73.0 1.1 %convolution_convert_fusion = bf16[4,256,128]{2,1,0:T(8,128)(2,1)} fusion(bf16[512,128,1]{1,0,2:T(8,128)(2,1)S(1)} %bitcast.118, bf16[256,512]{1,0:T(8,128)(2,1)S(1)} %fusion.44), kind=kOutput, calls=%fused_computation.43 | convolution fusion | flops 134348800 | bytes 655360 | tf_op jit(solution)/shard_map/gtp,pc->gtc/dot_general | solution.py:127
  74.2 3.4 %all-to-all-start.3 = ((bf16[4,256,128]{2,1,0:T(8,128)(2,1)}), bf16[4,256,128]{2,1,0:T(8,128)(2,1)S(1)}, u32[]{:S(2)}, u32[]{:S(2)}) async-start(bf16[4,256,128]{2,1,0:T(8,128)(2,1)} %convolution_convert_fusion), calls=%async_computation.3 | async-start | bytes 524288 | tf_op jit(solution)/shard_map/all_to_all | solution.py:129
  77.6 0.7 fusion.56
  78.4 5.3 %all-to-all-done.3 = bf16[4,256,128]{2,1,0:T(8,128)(2,1)S(1)} async-done(((bf16[4,256,128]{2,1,0:T(8,128)(2,1)}), bf16[4,256,128]{2,1,0:T(8,128)(2,1)S(1)}, u32[]{:S(2)}, u32[]{:S(2)}) %all-to-all-start.3) | async-done | bytes 262176 | tf_op jit(solution)/shard_map/all_to_all | solution.py:129
  83.7 0.7 copy.96
  (64 shorter events, 11.2 us)
Async XLA Ops:
  1.6 5.0 %copy-start.12 = (s32[1024]{0:T(1024)S(1)}, s32[1024]{0:T(1024)}, u32[]{:S(2)}) copy-start(s32[1024]{0:T(1024)} %param.12) | copy-start | bytes 12292
  1.6 11.9 %all-to-all-start = ((f32[4,256,128]{2,1,0:T(8,128)}), f32[4,256,128]{2,1,0:T(8,128)S(1)}, u32[]{:S(2)}, u32[]{:S(2)}) async-start(f32[4,256,128]{2,1,0:T(8,128)} %bitcast.15), calls=%async_computation | async-start | bytes 1048576 | tf_op jit(solution)/shard_map/all_to_all | solution.py:102
  14.8 20.6 %copy-start.8 = (f32[1,1,4,128,128]{4,3,2,1,0:T(8,128)S(1)}, f32[1,1,4,128,128]{4,3,2,1,0:T(8,128)}, u32[]{:S(2)}) copy-start(f32[1,1,4,128,128]{4,3,2,1,0:T(8,128)} %param.18) | copy-start | bytes 786436
  14.8 35.8 %all-to-all-start.1 = ((f32[4,128,128]{2,0,1:T(4,128)}), f32[4,128,128]{2,0,1:T(4,128)S(1)}, u32[]{:S(2)}, u32[]{:S(2)}) async-start(f32[4,128,128]{2,0,1:T(4,128)} %copy.44), calls=%async_computation.1 | async-start | bytes 524288 | tf_op jit(solution)/shard_map/all_to_all | solution.py:107
  35.4 15.3 %copy-start.10 = (f32[1,1,4,128,128]{4,3,2,1,0:T(8,128)S(1)}, f32[1,1,4,128,128]{4,3,2,1,0:T(8,128)}, u32[]{:S(2)}) copy-start(f32[1,1,4,128,128]{4,3,2,1,0:T(8,128)} %param.14) | copy-start | bytes 786436
  50.7 0.7 copy-start.5
  51.4 0.9 %copy-start.7 = (f32[1,1,4,128,128]{4,3,2,1,0:T(8,128)S(1)}, f32[1,1,4,128,128]{4,3,2,1,0:T(8,128)}, u32[]{:S(2)}) copy-start(f32[1,1,4,128,128]{4,3,2,1,0:T(8,128)} %param.15) | copy-start | bytes 786436
  52.3 0.9 %copy-start.11 = (f32[1,1,4,128,128]{4,3,2,1,0:T(8,128)S(1)}, f32[1,1,4,128,128]{4,3,2,1,0:T(8,128)}, u32[]{:S(2)}) copy-start(f32[1,1,4,128,128]{4,3,2,1,0:T(8,128)} %param.13) | copy-start | bytes 786436
  53.7 0.8 copy-start.6
  54.5 5.8 %copy-start.2 = (f32[1,1,4,128,128]{4,3,2,1,0:T(8,128)S(1)}, f32[1,1,4,128,128]{4,3,2,1,0:T(8,128)}, u32[]{:S(2)}) copy-start(f32[1,1,4,128,128]{4,3,2,1,0:T(8,128)} %param.16) | copy-start | bytes 786436
  54.5 5.8 %copy-start.4 = (f32[1,1,4,128,128]{4,3,2,1,0:T(8,128)S(1)}, f32[1,1,4,128,128]{4,3,2,1,0:T(8,128)}, u32[]{:S(2)}) copy-start(f32[1,1,4,128,128]{4,3,2,1,0:T(8,128)} %param.17) | copy-start | bytes 786436
  54.5 18.5 %all-to-all-start.2 = ((bf16[128,4,128]{2,1,0:T(4,128)(2,1)}), bf16[128,4,128]{2,1,0:T(4,128)(2,1)S(1)}, u32[]{:S(2)}, u32[]{:S(2)}) async-start(bf16[128,4,128]{2,1,0:T(4,128)(2,1)} %copy.50), calls=%async_computation.2 | async-start | bytes 262144 | tf_op jit(solution)/shard_map/all_to_all | solution.py:123
  71.9 2.3 %copy-start = (f32[1,1,4,128,128]{4,3,2,1,0:T(8,128)}, f32[1,1,4,128,128]{4,3,2,1,0:T(8,128)S(1)}, u32[]{:S(2)}) copy-start(f32[1,1,4,128,128]{4,3,2,1,0:T(8,128)S(1)} %get-tuple-element.128) | copy-start | bytes 786436
  71.9 2.2 %copy-start.1 = (f32[1,1,4,128,128]{4,3,2,1,0:T(8,128)}, f32[1,1,4,128,128]{4,3,2,1,0:T(8,128)S(1)}, u32[]{:S(2)}) copy-start(f32[1,1,4,128,128]{4,3,2,1,0:T(8,128)S(1)} %get-tuple-element.125) | copy-start | bytes 786436
  71.9 2.2 %copy-start.3 = (f32[1,1,4,128,128]{4,3,2,1,0:T(8,128)}, f32[1,1,4,128,128]{4,3,2,1,0:T(8,128)S(1)}, u32[]{:S(2)}) copy-start(f32[1,1,4,128,128]{4,3,2,1,0:T(8,128)S(1)} %get-tuple-element.126) | copy-start | bytes 786436
  72.0 6.4 %copy-start.9 = (f32[1,1,4,128,128]{4,3,2,1,0:T(8,128)}, f32[1,1,4,128,128]{4,3,2,1,0:T(8,128)S(1)}, u32[]{:S(2)}) copy-start(f32[1,1,4,128,128]{4,3,2,1,0:T(8,128)S(1)} %get-tuple-element.127) | copy-start | bytes 786436
  74.2 9.5 %all-to-all-start.3 = ((bf16[4,256,128]{2,1,0:T(8,128)(2,1)}), bf16[4,256,128]{2,1,0:T(8,128)(2,1)S(1)}, u32[]{:S(2)}, u32[]{:S(2)}) async-start(bf16[4,256,128]{2,1,0:T(8,128)(2,1)} %convolution_convert_fusion), calls=%async_computation.3 | async-start | bytes 524288 | tf_op jit(solution)/shard_map/all_to_all | solution.py:129

commit v12 on v11

--- a/solution.py
+++ b/solution.py
@@ -123,9 +123,9 @@
     returned = lax.all_to_all(weights, "shard", split_axis=0, concat_axis=0, tiled=True)
     returned = returned.reshape(shards * capacity, piece_len)
     picking = (own_place[:, None] == places[None, :]).astype(jnp.bfloat16)
-    picking = jnp.broadcast_to(picking[None], (groups,) + picking.shape)
-    spread = jnp.einsum("gtp,pc->gtc", picking, returned, preferred_element_type=jnp.float32)
-    spread = spread.astype(jnp.bfloat16)
+    picking = jnp.tile(picking, (groups, 1))
+    spread = jnp.dot(picking, returned, preferred_element_type=jnp.float32)
+    spread = spread.astype(jnp.bfloat16).reshape(groups, per_group, piece_len)
     new_params = lax.all_to_all(spread, "dp", 0, 0, tiled=True).reshape(tile_count, piece_len)
     lstat_new, rstat_new, lbasis_new, rbasis_new = soap_bases(
         gradient,

time: 84.8 us -> 84.8 us (level)
  no operation moved by 1% of the time
where the time goes in v12:
time: 84.8 us; the launch traced here: 83.9 us
  starting transfers between devices  34.6 us (41%)
  waiting for transfers between devices  26.1 us (31%)
  matrix products  14.3 us (17%)
  local copies, waits for them, and re-layouts  5.36 us (6%)
  other arithmetic  2.45 us (3%)
  between operations  0.92 us (1%)
    all_to_all x1, starting transfers between devices, body(): lax.all_to_all(outgoing, 'shard', split_axis=1, concat_axis=1, tiled=True)  20.5 us
    all_to_all x1, waiting for transfers between devices, body(): lax.all_to_all(outgoing, 'shard', split_axis=1, concat_axis=1, tiled=True)  15.1 us
    dot_general x27, matrix products, product(): return jnp.einsum(form, left, right, precision=precision)  12.8 us
    all_to_all x1, starting transfers between devices, body(): lax.all_to_all(weights, 'shard', split_axis=0, concat_axis=0, tiled=True)  5.68 us
    all_to_all x1, waiting for transfers between devices, body(): summed = jnp.sum(lax.all_to_all(parts, 'dp', 0, 0, tiled=True), axis=0)  5.19 us
    all_to_all x1, starting transfers between devices, body(): summed = jnp.sum(lax.all_to_all(parts, 'dp', 0, 0, tiled=True), axis=0)  4.97 us
    all_to_all x1, waiting for transfers between devices, body(): lax.all_to_all(spread, 'dp', 0, 0, tiled=True)  4.78 us
    all_to_all x1, starting transfers between devices, body(): lax.all_to_all(spread, 'dp', 0, 0, tiled=True)  3.41 us
  transfers between devices with their start and end apart: 4, of which 4 were waited for; matrix products, arithmetic and copies ran while one was open for 17% of the time, Pallas kernels for 0%

profile of v12, /device:TPU:1, one launch (start us, length us, event | category | flops | bytes accessed | tf_op | source)
XLA Modules:
  0.0 83.9 jit_solution(17222566004664289555)
XLA Ops:
  0.6 1.0 %copy.95 = f32[1,1,4,128,128]{4,3,2,1,0:T(8,128)S(1)} copy(f32[1,1,4,128,128]{4,3,2,1,0:T(8,128)} %param.19) | data formatting | bytes 524288
  1.6 5.0 %all-to-all-start = ((f32[4,256,128]{2,1,0:T(8,128)}), f32[4,256,128]{2,1,0:T(8,128)S(1)}, u32[]{:S(2)}, u32[]{:S(2)}) async-start(f32[4,256,128]{2,1,0:T(8,128)} %bitcast.16), calls=%async_computation | async-start | bytes 1048576 | tf_op jit(solution)/shard_map/all_to_all | solution.py:102
  6.7 0.9 %fusion.29 = s32[4,128,2,128]{1,2,3,0:T(2,128)S(1)} fusion(s32[4,2,128]{1,2,0:T(8,128)S(1)} %copy.41), kind=kOutput, calls=%fused_computation.49 | output fusion | flops 16908288 | bytes 528384 | tf_op jit(solution)/shard_map/reduce-window
  8.3 5.2 %all-to-all-done = f32[4,256,128]{2,1,0:T(8,128)S(1)} async-done(((f32[4,256,128]{2,1,0:T(8,128)}), f32[4,256,128]{2,1,0:T(8,128)S(1)}, u32[]{:S(2)}, u32[]{:S(2)}) %all-to-all-start) | async-done | bytes 524320 | tf_op jit(solution)/shard_map/all_to_all | solution.py:102
  13.9 0.9 %copy.44 = f32[4,128,128]{2,0,1:T(4,128)} copy(f32[4,128,128]{2,1,0:T(8,128)S(1)} %convolution_bitcast_fusion) | data formatting | bytes 524288 | tf_op jit(solution)/shard_map/transpose | solution.py:106
  14.8 20.5 %all-to-all-start.1 = ((f32[4,128,128]{2,0,1:T(4,128)}), f32[4,128,128]{2,0,1:T(4,128)S(1)}, u32[]{:S(2)}, u32[]{:S(2)}) async-start(f32[4,128,128]{2,0,1:T(4,128)} %copy.44), calls=%async_computation.1 | async-start | bytes 524288 | tf_op jit(solution)/shard_map/all_to_all | solution.py:107
  35.5 15.1 %all-to-all-done.1 = f32[4,128,128]{2,0,1:T(4,128)S(1)} async-done(((f32[4,128,128]{2,0,1:T(4,128)}), f32[4,128,128]{2,0,1:T(4,128)S(1)}, u32[]{:S(2)}, u32[]{:S(2)}) %all-to-all-start.1) | async-done | bytes 262176 | tf_op jit(solution)/shard_map/all_to_all | solution.py:107
  53.7 0.8 copy.50
  54.5 5.7 %all-to-all-start.2 = ((bf16[128,4,128]{2,1,0:T(4,128)(2,1)}), bf16[128,4,128]{2,1,0:T(4,128)(2,1)S(1)}, u32[]{:S(2)}, u32[]{:S(2)}) async-start(bf16[128,4,128]{2,1,0:T(4,128)(2,1)} %copy.50), calls=%async_computation.2 | async-start | bytes 262144 | tf_op jit(solution)/shard_map/all_to_all | solution.py:123
  60.3 11.6 %conditional.1 = (f32[1,1,4,128,128]{4,3,2,1,0:T(8,128)S(1)}, f32[1,1,4,128,128]{4,3,2,1,0:T(8,128)S(1)}, f32[1,1,4,128,128]{4,3,2,1,0:T(8,128)S(1)}, f32[1,1,4,128,128]{4,3,2,1,0:T(8,128)S(1)}) conditional(s32[]{:T(128)} %convert_element_type.26, (f32[4,128,128]{2,1,0:T(8,128)S(1)}, f32[4,128,128]{2,1,0:T(8,128)S(1)}, f32[4,128,128]{1,2,0:T(8,128)S(1)}, ...), branch_computations={%region_4.5_spmd, %region_5.7_spmd} | conditional | flops 2219835392 | bytes 30933184 | solution.py:76
  61.8 0.7 fusion.19
  62.9 0.6 fusion.65
  63.9 0.6 fusion.66
  64.9 0.6 fusion.67
  65.9 0.6 fusion.68
  66.9 0.6 fusion.69
  67.9 0.6 fusion.70
  68.9 0.6 fusion.71
  72.0 1.1 %all-to-all-done.2 = bf16[128,4,128]{2,1,0:T(4,128)(2,1)S(1)} async-done(((bf16[128,4,128]{2,1,0:T(4,128)(2,1)}), bf16[128,4,128]{2,1,0:T(4,128)(2,1)S(1)}, u32[]{:S(2)}, u32[]{:S(2)}) %all-to-all-start.2) | async-done | bytes 131104 | tf_op jit(solution)/shard_map/all_to_all | solution.py:123
  73.2 1.1 %convolution_convert_fusion = bf16[1024,128]{1,0:T(8,128)(2,1)} fusion(bf16[1024,512]{1,0:T(8,128)(2,1)S(1)} %bitcast.100, bf16[512,128]{1,0:T(8,128)(2,1)S(1)} %bitcast.119), kind=kOutput, calls=%fused_computation.43 | convolution fusion | flops 134348800 | bytes 1441792 | tf_op jit(solution)/shard_map/dot_general | solution.py:127
  74.3 3.4 %all-to-all-start.3 = ((bf16[4,256,128]{2,1,0:T(8,128)(2,1)}), bf16[4,256,128]{2,1,0:T(8,128)(2,1)S(1)}, u32[]{:S(2)}, u32[]{:S(2)}) async-start(bf16[4,256,128]{2,1,0:T(8,128)(2,1)} %bitcast.25), calls=%async_computation.3 | async-start | bytes 524288 | tf_op jit(solution)/shard_map/all_to_all | solution.py:129
  77.7 0.7 fusion.55
  78.5 4.8 %all-to-all-done.3 = bf16[4,256,128]{2,1,0:T(8,128)(2,1)S(1)} async-done(((bf16[4,256,128]{2,1,0:T(8,128)(2,1)}), bf16[4,256,128]{2,1,0:T(8,128)(2,1)S(1)}, u32[]{:S(2)}, u32[]{:S(2)}) %all-to-all-start.3) | async-done | bytes 262176 | tf_op jit(solution)/shard_map/all_to_all | solution.py:129
  83.2 0.7 copy.96
  (65 shorter events, 11.3 us)
Async XLA Ops:
  1.6 5.0 %copy-start.12 = (s32[1024]{0:T(1024)S(1)}, s32[1024]{0:T(1024)}, u32[]{:S(2)}) copy-start(s32[1024]{0:T(1024)} %param.12) | copy-start | bytes 12292
  1.6 11.9 %all-to-all-start = ((f32[4,256,128]{2,1,0:T(8,128)}), f32[4,256,128]{2,1,0:T(8,128)S(1)}, u32[]{:S(2)}, u32[]{:S(2)}) async-start(f32[4,256,128]{2,1,0:T(8,128)} %bitcast.16), calls=%async_computation | async-start | bytes 1048576 | tf_op jit(solution)/shard_map/all_to_all | solution.py:102
  14.8 20.6 %copy-start.8 = (f32[1,1,4,128,128]{4,3,2,1,0:T(8,128)S(1)}, f32[1,1,4,128,128]{4,3,2,1,0:T(8,128)}, u32[]{:S(2)}) copy-start(f32[1,1,4,128,128]{4,3,2,1,0:T(8,128)} %param.18) | copy-start | bytes 786436
  14.8 35.8 %all-to-all-start.1 = ((f32[4,128,128]{2,0,1:T(4,128)}), f32[4,128,128]{2,0,1:T(4,128)S(1)}, u32[]{:S(2)}, u32[]{:S(2)}) async-start(f32[4,128,128]{2,0,1:T(4,128)} %copy.44), calls=%async_computation.1 | async-start | bytes 524288 | tf_op jit(solution)/shard_map/all_to_all | solution.py:107
  35.4 15.3 %copy-start.10 = (f32[1,1,4,128,128]{4,3,2,1,0:T(8,128)S(1)}, f32[1,1,4,128,128]{4,3,2,1,0:T(8,128)}, u32[]{:S(2)}) copy-start(f32[1,1,4,128,128]{4,3,2,1,0:T(8,128)} %param.14) | copy-start | bytes 786436
  50.7 0.7 copy-start.5
  51.4 0.9 %copy-start.7 = (f32[1,1,4,128,128]{4,3,2,1,0:T(8,128)S(1)}, f32[1,1,4,128,128]{4,3,2,1,0:T(8,128)}, u32[]{:S(2)}) copy-start(f32[1,1,4,128,128]{4,3,2,1,0:T(8,128)} %param.15) | copy-start | bytes 786436
  52.3 0.9 %copy-start.11 = (f32[1,1,4,128,128]{4,3,2,1,0:T(8,128)S(1)}, f32[1,1,4,128,128]{4,3,2,1,0:T(8,128)}, u32[]{:S(2)}) copy-start(f32[1,1,4,128,128]{4,3,2,1,0:T(8,128)} %param.13) | copy-start | bytes 786436
  53.7 0.8 copy-start.6
  54.5 5.8 %copy-start.2 = (f32[1,1,4,128,128]{4,3,2,1,0:T(8,128)S(1)}, f32[1,1,4,128,128]{4,3,2,1,0:T(8,128)}, u32[]{:S(2)}) copy-start(f32[1,1,4,128,128]{4,3,2,1,0:T(8,128)} %param.16) | copy-start | bytes 786436
  54.5 5.8 %copy-start.4 = (f32[1,1,4,128,128]{4,3,2,1,0:T(8,128)S(1)}, f32[1,1,4,128,128]{4,3,2,1,0:T(8,128)}, u32[]{:S(2)}) copy-start(f32[1,1,4,128,128]{4,3,2,1,0:T(8,128)} %param.17) | copy-start | bytes 786436
  54.5 18.5 %all-to-all-start.2 = ((bf16[128,4,128]{2,1,0:T(4,128)(2,1)}), bf16[128,4,128]{2,1,0:T(4,128)(2,1)S(1)}, u32[]{:S(2)}, u32[]{:S(2)}) async-start(bf16[128,4,128]{2,1,0:T(4,128)(2,1)} %copy.50), calls=%async_computation.2 | async-start | bytes 262144 | tf_op jit(solution)/shard_map/all_to_all | solution.py:123
  71.9 1.2 %copy-start = (f32[1,1,4,128,128]{4,3,2,1,0:T(8,128)}, f32[1,1,4,128,128]{4,3,2,1,0:T(8,128)S(1)}, u32[]{:S(2)}) copy-start(f32[1,1,4,128,128]{4,3,2,1,0:T(8,128)S(1)} %get-tuple-element.128) | copy-start | bytes 786436
  71.9 1.2 %copy-start.1 = (f32[1,1,4,128,128]{4,3,2,1,0:T(8,128)}, f32[1,1,4,128,128]{4,3,2,1,0:T(8,128)S(1)}, u32[]{:S(2)}) copy-start(f32[1,1,4,128,128]{4,3,2,1,0:T(8,128)S(1)} %get-tuple-element.125) | copy-start | bytes 786436
  71.9 1.2 %copy-start.3 = (f32[1,1,4,128,128]{4,3,2,1,0:T(8,128)}, f32[1,1,4,128,128]{4,3,2,1,0:T(8,128)S(1)}, u32[]{:S(2)}) copy-start(f32[1,1,4,128,128]{4,3,2,1,0:T(8,128)S(1)} %get-tuple-element.126) | copy-start | bytes 786436
  72.0 1.2 %copy-start.9 = (f32[1,1,4,128,128]{4,3,2,1,0:T(8,128)}, f32[1,1,4,128,128]{4,3,2,1,0:T(8,128)S(1)}, u32[]{:S(2)}) copy-start(f32[1,1,4,128,128]{4,3,2,1,0:T(8,128)S(1)} %get-tuple-element.127) | copy-start | bytes 786436
  74.3 8.9 %all-to-all-start.3 = ((bf16[4,256,128]{2,1,0:T(8,128)(2,1)}), bf16[4,256,128]{2,1,0:T(8,128)(2,1)S(1)}, u32[]{:S(2)}, u32[]{:S(2)}) async-start(bf16[4,256,128]{2,1,0:T(8,128)(2,1)} %bitcast.25), calls=%async_computation.3 | async-start | bytes 524288 | tf_op jit(solution)/shard_map/all_to_all | solution.py:129

commit v13 on v11

--- a/solution.py
+++ b/solution.py
@@ -47,7 +47,7 @@
     grad_rot, first_rot = rotated[:count], rotated[count:]
     second_new = beta_two * second + (1.0 - beta_two) * grad_rot * grad_rot
     normed = first_rot / (jnp.sqrt(second_new) + adam_eps)
-    update = product("nik,nlk->nil", product("nij,njk->nik", lbasis, normed), rbasis)
+    update = product("nij,njl->nil", lbasis, product("njk,nlk->njl", normed, rbasis))
     master_new = master - learn_rate * (update + weight_decay * master)
     return master_new, first_new, second_new
 

time: 84.8 us -> 84.8 us (level)
  no operation moved by 1% of the time
where the time goes in v13:
time: 84.8 us; the launch traced here: 84.4 us
  starting transfers between devices  34.6 us (41%)
  waiting for transfers between devices  26.7 us (31%)
  matrix products  14.4 us (17%)
  local copies, waits for them, and re-layouts  5.21 us (6%)
  other arithmetic  2.45 us (3%)
  between operations  0.88 us (1%)
    all_to_all x1, starting transfers between devices, body(): lax.all_to_all(outgoing, 'shard', split_axis=1, concat_axis=1, tiled=True)  20.5 us
    all_to_all x1, waiting for transfers between devices, body(): lax.all_to_all(outgoing, 'shard', split_axis=1, concat_axis=1, tiled=True)  15.1 us
    dot_general x27, matrix products, product(): return jnp.einsum(form, left, right, precision=precision)  12.9 us
    all_to_all x1, starting transfers between devices, body(): lax.all_to_all(weights, 'shard', split_axis=0, concat_axis=0, tiled=True)  5.68 us
    all_to_all x1, waiting for transfers between devices, body(): lax.all_to_all(spread, 'dp', 0, 0, tiled=True)  5.31 us
    all_to_all x1, waiting for transfers between devices, body(): summed = jnp.sum(lax.all_to_all(parts, 'dp', 0, 0, tiled=True), axis=0)  5.19 us
    all_to_all x1, starting transfers between devices, body(): summed = jnp.sum(lax.all_to_all(parts, 'dp', 0, 0, tiled=True), axis=0)  4.97 us
    all_to_all x1, starting transfers between devices, body(): lax.all_to_all(spread, 'dp', 0, 0, tiled=True)  3.41 us
  transfers between devices with their start and end apart: 4, of which 4 were waited for; matrix products, arithmetic and copies ran while one was open for 17% of the time, Pallas kernels for 0%

profile of v13, /device:TPU:1, one launch (start us, length us, event | category | flops | bytes accessed | tf_op | source)
XLA Modules:
  0.0 84.4 jit_solution(16131571023583148554)
XLA Ops:
  0.6 1.0 %copy.97 = f32[1,1,4,128,128]{4,3,2,1,0:T(8,128)S(1)} copy(f32[1,1,4,128,128]{4,3,2,1,0:T(8,128)} %param.19) | data formatting | bytes 524288
  1.6 5.0 %all-to-all-start = ((f32[4,256,128]{2,1,0:T(8,128)}), f32[4,256,128]{2,1,0:T(8,128)S(1)}, u32[]{:S(2)}, u32[]{:S(2)}) async-start(f32[4,256,128]{2,1,0:T(8,128)} %bitcast.15), calls=%async_computation | async-start | bytes 1048576 | tf_op jit(solution)/shard_map/all_to_all | solution.py:102
  6.7 0.9 %fusion.30 = s32[4,128,2,128]{1,2,3,0:T(2,128)S(1)} fusion(s32[4,2,128]{1,2,0:T(8,128)S(1)} %copy.43), kind=kOutput, calls=%fused_computation.50 | output fusion | flops 16908288 | bytes 528384 | tf_op jit(solution)/shard_map/reduce-window
  8.3 5.2 %all-to-all-done = f32[4,256,128]{2,1,0:T(8,128)S(1)} async-done(((f32[4,256,128]{2,1,0:T(8,128)}), f32[4,256,128]{2,1,0:T(8,128)S(1)}, u32[]{:S(2)}, u32[]{:S(2)}) %all-to-all-start) | async-done | bytes 524320 | tf_op jit(solution)/shard_map/all_to_all | solution.py:102
  13.9 0.9 %copy.46 = f32[4,128,128]{2,0,1:T(4,128)} copy(f32[4,128,128]{2,1,0:T(8,128)S(1)} %convolution_bitcast_fusion.1) | data formatting | bytes 524288 | tf_op jit(solution)/shard_map/transpose | solution.py:106
  14.8 20.5 %all-to-all-start.1 = ((f32[4,128,128]{2,0,1:T(4,128)}), f32[4,128,128]{2,0,1:T(4,128)S(1)}, u32[]{:S(2)}, u32[]{:S(2)}) async-start(f32[4,128,128]{2,0,1:T(4,128)} %copy.46), calls=%async_computation.1 | async-start | bytes 524288 | tf_op jit(solution)/shard_map/all_to_all | solution.py:107
  35.5 15.1 %all-to-all-done.1 = f32[4,128,128]{2,0,1:T(4,128)S(1)} async-done(((f32[4,128,128]{2,0,1:T(4,128)}), f32[4,128,128]{2,0,1:T(4,128)S(1)}, u32[]{:S(2)}, u32[]{:S(2)}) %all-to-all-start.1) | async-done | bytes 262176 | tf_op jit(solution)/shard_map/all_to_all | solution.py:107
  53.7 0.8 copy.52
  54.5 5.7 %all-to-all-start.2 = ((bf16[128,4,128]{2,1,0:T(4,128)(2,1)}), bf16[128,4,128]{2,1,0:T(4,128)(2,1)S(1)}, u32[]{:S(2)}, u32[]{:S(2)}) async-start(bf16[128,4,128]{2,1,0:T(4,128)(2,1)} %copy.52), calls=%async_computation.2 | async-start | bytes 262144 | tf_op jit(solution)/shard_map/all_to_all | solution.py:123
  60.3 11.6 %conditional.1 = (f32[1,1,4,128,128]{4,3,2,1,0:T(8,128)S(1)}, f32[1,1,4,128,128]{4,3,2,1,0:T(8,128)S(1)}, f32[1,1,4,128,128]{4,3,2,1,0:T(8,128)S(1)}, f32[1,1,4,128,128]{4,3,2,1,0:T(8,128)S(1)}) conditional(s32[]{:T(128)} %convert_element_type.26, (f32[4,128,128]{2,1,0:T(8,128)S(1)}, f32[4,128,128]{2,1,0:T(8,128)S(1)}, f32[4,128,128]{1,2,0:T(8,128)S(1)}, ...), branch_computations={%region_4.5_spmd, %region_5.7_spmd} | conditional | flops 2219835392 | bytes 30933184 | solution.py:76
  61.8 0.7 fusion.19
  62.9 0.6 fusion.67
  63.9 0.6 fusion.68
  64.9 0.6 fusion.69
  65.9 0.6 fusion.70
  66.9 0.6 fusion.71
  67.9 0.6 fusion.72
  68.9 0.6 fusion.73
  72.0 1.1 %all-to-all-done.2 = bf16[128,4,128]{2,1,0:T(4,128)(2,1)S(1)} async-done(((bf16[128,4,128]{2,1,0:T(4,128)(2,1)}), bf16[128,4,128]{2,1,0:T(4,128)(2,1)S(1)}, u32[]{:S(2)}, u32[]{:S(2)}) %all-to-all-start.2) | async-done | bytes 131104 | tf_op jit(solution)/shard_map/all_to_all | solution.py:123
  73.0 1.1 %convolution_convert_fusion = bf16[4,256,128]{2,1,0:T(8,128)(2,1)} fusion(bf16[512,128,1]{1,0,2:T(8,128)(2,1)S(1)} %bitcast.126, bf16[256,512]{1,0:T(8,128)(2,1)S(1)} %fusion.45), kind=kOutput, calls=%fused_computation.43 | convolution fusion | flops 134348800 | bytes 655360 | tf_op jit(solution)/shard_map/gtp,pc->gtc/dot_general | solution.py:127
  74.2 3.4 %all-to-all-start.3 = ((bf16[4,256,128]{2,1,0:T(8,128)(2,1)}), bf16[4,256,128]{2,1,0:T(8,128)(2,1)S(1)}, u32[]{:S(2)}, u32[]{:S(2)}) async-start(bf16[4,256,128]{2,1,0:T(8,128)(2,1)} %convolution_convert_fusion), calls=%async_computation.3 | async-start | bytes 524288 | tf_op jit(solution)/shard_map/all_to_all | solution.py:129
  77.6 0.7 fusion.57
  78.4 5.3 %all-to-all-done.3 = bf16[4,256,128]{2,1,0:T(8,128)(2,1)S(1)} async-done(((bf16[4,256,128]{2,1,0:T(8,128)(2,1)}), bf16[4,256,128]{2,1,0:T(8,128)(2,1)S(1)}, u32[]{:S(2)}, u32[]{:S(2)}) %all-to-all-start.3) | async-done | bytes 262176 | tf_op jit(solution)/shard_map/all_to_all | solution.py:129
  83.7 0.7 copy.98
  (64 shorter events, 11.2 us)
Async XLA Ops:
  1.6 5.0 %copy-start.12 = (s32[1024]{0:T(1024)S(1)}, s32[1024]{0:T(1024)}, u32[]{:S(2)}) copy-start(s32[1024]{0:T(1024)} %param.12) | copy-start | bytes 12292
  1.6 11.9 %all-to-all-start = ((f32[4,256,128]{2,1,0:T(8,128)}), f32[4,256,128]{2,1,0:T(8,128)S(1)}, u32[]{:S(2)}, u32[]{:S(2)}) async-start(f32[4,256,128]{2,1,0:T(8,128)} %bitcast.15), calls=%async_computation | async-start | bytes 1048576 | tf_op jit(solution)/shard_map/all_to_all | solution.py:102
  14.8 20.6 %copy-start.6 = (f32[1,1,4,128,128]{4,3,2,1,0:T(8,128)S(1)}, f32[1,1,4,128,128]{4,3,2,1,0:T(8,128)}, u32[]{:S(2)}) copy-start(f32[1,1,4,128,128]{4,3,2,1,0:T(8,128)} %param.18) | copy-start | bytes 786436
  14.8 35.8 %all-to-all-start.1 = ((f32[4,128,128]{2,0,1:T(4,128)}), f32[4,128,128]{2,0,1:T(4,128)S(1)}, u32[]{:S(2)}, u32[]{:S(2)}) async-start(f32[4,128,128]{2,0,1:T(4,128)} %copy.46), calls=%async_computation.1 | async-start | bytes 524288 | tf_op jit(solution)/shard_map/all_to_all | solution.py:107
  35.4 15.3 %copy-start.10 = (f32[1,1,4,128,128]{4,3,2,1,0:T(8,128)S(1)}, f32[1,1,4,128,128]{4,3,2,1,0:T(8,128)}, u32[]{:S(2)}) copy-start(f32[1,1,4,128,128]{4,3,2,1,0:T(8,128)} %param.14) | copy-start | bytes 786436
  50.7 0.7 copy-start.5
  51.4 0.9 %copy-start.8 = (f32[1,1,4,128,128]{4,3,2,1,0:T(8,128)S(1)}, f32[1,1,4,128,128]{4,3,2,1,0:T(8,128)}, u32[]{:S(2)}) copy-start(f32[1,1,4,128,128]{4,3,2,1,0:T(8,128)} %param.15) | copy-start | bytes 786436
  52.3 0.9 %copy-start.11 = (f32[1,1,4,128,128]{4,3,2,1,0:T(8,128)S(1)}, f32[1,1,4,128,128]{4,3,2,1,0:T(8,128)}, u32[]{:S(2)}) copy-start(f32[1,1,4,128,128]{4,3,2,1,0:T(8,128)} %param.13) | copy-start | bytes 786436
  53.7 0.8 copy-start.7
  54.5 5.8 %copy-start.2 = (f32[1,1,4,128,128]{4,3,2,1,0:T(8,128)S(1)}, f32[1,1,4,128,128]{4,3,2,1,0:T(8,128)}, u32[]{:S(2)}) copy-start(f32[1,1,4,128,128]{4,3,2,1,0:T(8,128)} %param.16) | copy-start | bytes 786436
  54.5 5.8 %copy-start.4 = (f32[1,1,4,128,128]{4,3,2,1,0:T(8,128)S(1)}, f32[1,1,4,128,128]{4,3,2,1,0:T(8,128)}, u32[]{:S(2)}) copy-start(f32[1,1,4,128,128]{4,3,2,1,0:T(8,128)} %param.17) | copy-start | bytes 786436
  54.5 18.5 %all-to-all-start.2 = ((bf16[128,4,128]{2,1,0:T(4,128)(2,1)}), bf16[128,4,128]{2,1,0:T(4,128)(2,1)S(1)}, u32[]{:S(2)}, u32[]{:S(2)}) async-start(bf16[128,4,128]{2,1,0:T(4,128)(2,1)} %copy.52), calls=%async_computation.2 | async-start | bytes 262144 | tf_op jit(solution)/shard_map/all_to_all | solution.py:123
  71.9 2.2 %copy-start = (f32[1,1,4,128,128]{4,3,2,1,0:T(8,128)}, f32[1,1,4,128,128]{4,3,2,1,0:T(8,128)S(1)}, u32[]{:S(2)}) copy-start(f32[1,1,4,128,128]{4,3,2,1,0:T(8,128)S(1)} %get-tuple-element.128) | copy-start | bytes 786436
  71.9 2.2 %copy-start.1 = (f32[1,1,4,128,128]{4,3,2,1,0:T(8,128)}, f32[1,1,4,128,128]{4,3,2,1,0:T(8,128)S(1)}, u32[]{:S(2)}) copy-start(f32[1,1,4,128,128]{4,3,2,1,0:T(8,128)S(1)} %get-tuple-element.125) | copy-start | bytes 786436
  71.9 2.2 %copy-start.3 = (f32[1,1,4,128,128]{4,3,2,1,0:T(8,128)}, f32[1,1,4,128,128]{4,3,2,1,0:T(8,128)S(1)}, u32[]{:S(2)}) copy-start(f32[1,1,4,128,128]{4,3,2,1,0:T(8,128)S(1)} %get-tuple-element.126) | copy-start | bytes 786436
  72.0 6.4 %copy-start.9 = (f32[1,1,4,128,128]{4,3,2,1,0:T(8,128)}, f32[1,1,4,128,128]{4,3,2,1,0:T(8,128)S(1)}, u32[]{:S(2)}) copy-start(f32[1,1,4,128,128]{4,3,2,1,0:T(8,128)S(1)} %get-tuple-element.127) | copy-start | bytes 786436
  74.2 9.5 %all-to-all-start.3 = ((bf16[4,256,128]{2,1,0:T(8,128)(2,1)}), bf16[4,256,128]{2,1,0:T(8,128)(2,1)S(1)}, u32[]{:S(2)}, u32[]{:S(2)}) async-start(bf16[4,256,128]{2,1,0:T(8,128)(2,1)} %convolution_convert_fusion), calls=%async_computation.3 | async-start | bytes 524288 | tf_op jit(solution)/shard_map/all_to_all | solution.py:129
